TPU v7x, 32 devices: a whole 2x2x4 slice. The times are simulated.
32 devices in a mesh: parts: 2 (over x), chan: 8 (over z, y), samp: 2 (over core).
Axes of the slice: x: 2, y: 2, z: 4, core: 2. Of those that a mesh axis runs over, the one named last changes fastest.
Arguments:
- images: bfloat16 [512, 256, 784], P(('parts', 'samp'), 'chan'), parts along dimension 0, may hold values from -6 to 6
- out_grads: bfloat16 [512, 256, 196], P(('parts', 'samp'), 'chan'), parts along dimension 0, may hold values from -6 to 6
- in_signs: int32 [256, 288], P('chan'), may hold values from 0 to 1
- out_signs: int32 [256, 32], P('chan'), may hold values from 0 to 1
Outputs:
- sketch_rows: float32 [2, 256, 1024], P('samp', ('parts', 'chan')), parts along dimension 1
- r_factor: float32 [2048, 1024], P(('parts', 'chan')), parts along dimension 0
There are 2 independent parts, one for each index of `parts`. A program takes and returns all parts, laid end to end along the dimension named above; an argument that names none is the same for every part. Nothing has to cross between parts.
All inputs are finite; a program needn't handle non-finite values.
Results may differ from a plain program's by a relative error of at most 0.0003.
Values sent between devices are 32-bit elements; how exact they have to be, the bound alone decides.
No kernel may reach another device: no remote copies, remote signals or barrier semaphores. Data moves between devices by JAX's collectives and lax.ppermute only.
A program may use at most 128 MiB of HBM per device.

v0:
```python
import math

import jax
import jax.numpy as jnp
from jax import lax
from jax.sharding import PartitionSpec as P

C = 256


def project(images, out_grads, in_signs, out_signs):
    samples, channels, cells = images.shape
    side_in = math.isqrt(cells)
    side_out = side_in // 2
    picture = images.reshape(samples, channels, side_in, side_in)
    padded = jnp.pad(picture, ((0, 0), (0, 0), (1, 1), (1, 1)))
    tap_list = []
    for row_tap in range(3):
        for col_tap in range(3):
            tap_list.append(
                padded[
                    :,
                    :,
                    row_tap : row_tap + 2 * side_out - 1 : 2,
                    col_tap : col_tap + 2 * side_out - 1 : 2,
                ]
            )
    patches = jnp.stack(tap_list, axis=2).reshape(samples, channels, 9, side_out * side_out)
    width_in = in_signs.shape[1] // 9
    in_matrix = (2 * in_signs - 1).astype(jnp.bfloat16).reshape(channels, 9, width_in)
    out_matrix = (2 * out_signs - 1).astype(jnp.bfloat16)
    in_part = jnp.einsum("nctp,ctj->njp", patches, in_matrix, preferred_element_type=jnp.float32)
    out_part = jnp.einsum("ncp,cl->nlp", out_grads, out_matrix, preferred_element_type=jnp.float32)
    return (in_part, out_part)


def sketch(in_sum, out_sum, total_channels):
    in_feat = in_sum / math.sqrt(9 * total_channels)
    out_feat = out_sum / math.sqrt(total_channels)
    cells = in_sum.shape[2]
    outer = jnp.einsum(
        "nlp,njp->nlj", out_feat, in_feat, precision=lax.Precision.HIGHEST
    ) / math.sqrt(cells)
    return outer.reshape(outer.shape[0], -1)


def local(images, out_grads, in_signs, out_signs):
    samples = images.shape[0]
    in_part, out_part = project(images, out_grads, in_signs, out_signs)
    chan_count = lax.axis_size("chan")
    local_rows = samples // chan_count
    in_sum, out_sum = lax.psum((in_part, out_part), "chan")
    every = sketch(in_sum, out_sum, C)
    own = lax.dynamic_slice_in_dim(every, lax.axis_index("chan") * local_rows, local_rows, 0)
    batch_total = samples * lax.axis_size("samp")
    width = every.shape[1]
    identity_mat = jnp.eye(width, dtype=jnp.float32)
    gram_part = jnp.einsum("nk,nm->km", every, every, precision=lax.Precision.HIGHEST) / batch_total
    factor = jnp.linalg.cholesky(lax.psum(gram_part, "samp") + identity_mat).T
    rows_here = width // chan_count
    r_rows = lax.dynamic_slice_in_dim(factor, lax.axis_index("chan") * rows_here, rows_here, 0)
    return (own[None], r_rows)


def solution(mesh):
    in_specs = (
        P(("parts", "samp"), "chan", None),
        P(("parts", "samp"), "chan", None),
        P("chan", None),
        P("chan", None),
    )
    out_specs = (P("samp", ("parts", "chan"), None), P(("parts", "chan"), None))
    return jax.shard_map(local, mesh=mesh, in_specs=in_specs, out_specs=out_specs, check_vma=False)
```

profile of v0, /device:TPU:0, one launch (start us, length us, event | category | flops | bytes accessed | tf_op | source)
XLA Modules:
  0.0 631.2 jit_solution(10612608494008498298)
XLA Ops:
  7.2 4.5 copy.36
  11.7 5.5 pad_slice_fusion
  17.2 3.6 copy.37
  22.3 4.8 copy.38
  27.1 3.4 copy.39
  30.4 4.8 copy.40
  35.3 3.3 copy.41
  38.6 3.4 copy.42
  42.0 4.8 copy.43
  46.9 3.4 copy.44
  50.2 3.4 copy.45
  53.7 3.6 copy.34
  57.4 3.4 constant_dynamic-update-slice_fusion.7
  68.4 1.6 constant_dynamic-update-slice_fusion.1
  70.0 1.6 constant_dynamic-update-slice_fusion
  71.6 12.2 %convolution_bitcast_fusion = f32[128,32,196]{2,1,0:T(8,128)} fusion(bf16[32,9,32,1]{0,2,1,3:T(8,128)(2,1)S(1)} %bitcast.86, bf16[128,32,9,196]{3,1,2,0:T(8,128)(2,1)} %constant_dynamic-update-slice_fusion), kind=kOutput, calls=%fused_computation.16 | convolution fusion | flops 462422016 | bytes 17680384 | tf_op jit(solution)/shard_map/nctp,ctj->njp/dot_general | solution.py:32
  83.8 2.7 convolution_bitcast_fusion.1
  86.8 273.7 %all-reduce.8.cloned.1.call-done = (f32[128,32,196]{2,1,0:T(8,128)}, f32[128,32,196]{2,1,0:T(8,128)}) async-done(((f32[128,32,196]{2,1,0:T(8,128)}, f32[128,32,196]{2,1,0:T(8,128)}), (f32[128,32,196]{2,1,0:T(8,128)}, f32[128,32,196]{2,1,0:T(8,128)})) %all-reduce.8.cloned.1.call-update) | async-done | bytes 6422544 | tf_op jit(solution)/shard_map/psum | solution.py:52
  360.5 7.8 %fusion.6 = f32[128,32,32]{2,1,0:T(8,128)S(1)} fusion(f32[128,32,196]{2,1,0:T(8,128)} %get-tuple-element.10, f32[128,32,196]{2,1,0:T(8,128)} %get-tuple-element.11), kind=kOutput, calls=%fused_computation.21 | convolution fusion | flops 310018048 | bytes 6946816 | tf_op jit(solution)/shard_map/nlp,njp->nlj/dot_general | solution.py:41
  369.5 5.0 convolution_multiply_fusion
  375.6 26.6 %all-reduce.6.cloned.1.call-done = f32[1024,1024]{0,1:T(8,128)} async-done(((f32[1024,1024]{0,1:T(8,128)}), f32[1024,1024]{0,1:T(8,128)}) %all-reduce.6.cloned.1.call-update) | async-done | bytes 4194320 | tf_op jit(solution)/shard_map/psum | solution.py:59
  402.1 4.8 convert_add_fusion
  407.0 5.5 copy.49
  412.5 4.5 fusion
  417.0 1.9 copy-done
  418.9 11.7 %cholesky.223 = f32[128,128]{1,0:T(8,128)S(1)} custom-call(f32[128,128]{1,0:T(8,128)S(1)} %cholesky.580), custom_call_target="Cholesky" | custom-call | tf_op jit(solution)/shard_map/jit(cholesky)/cholesky | solution.py:59
  430.6 2.5 cholesky.255
  433.1 9.8 %custom-call.59 = f32[1,128,128]{1,2,0:T(8,128)S(1)} custom-call(f32[1,128,128]{2,1,0:T(8,128)S(1)} %get-tuple-element.42), custom_call_target="InvertDiagBlocksLowerTriangular" | custom-call | tf_op jit(solution)/shard_map/jit(cholesky)/cholesky | solution.py:59
  443.0 2.4 constant_dynamic-update-slice_fusion.16
  446.9 12.1 %cholesky.244 = f32[128,128]{1,0:T(8,128)S(1)} custom-call(f32[128,128]{1,0:T(8,128)S(1)} %cholesky.584), custom_call_target="Cholesky" | custom-call | tf_op jit(solution)/shard_map/jit(cholesky)/cholesky | solution.py:59
  459.6 9.8 %custom-call.60 = f32[1,128,128]{1,2,0:T(8,128)S(1)} custom-call(f32[1,128,128]{2,1,0:T(8,128)S(1)} %get-tuple-element.39), custom_call_target="InvertDiagBlocksLowerTriangular" | custom-call | tf_op jit(solution)/shard_map/jit(cholesky)/cholesky | solution.py:59
  470.7 2.1 convolution_subtract_fusion.1
  472.8 11.7 %cholesky.468 = f32[128,128]{1,0:T(8,128)S(1)} custom-call(f32[128,128]{1,0:T(8,128)S(1)} %cholesky.589), custom_call_target="Cholesky" | custom-call | tf_op jit(solution)/shard_map/jit(cholesky)/cholesky | solution.py:59
  485.8 9.8 %custom-call.61 = f32[1,128,128]{1,2,0:T(8,128)S(1)} custom-call(f32[1,128,128]{2,1,0:T(8,128)S(1)} %get-tuple-element.36), custom_call_target="InvertDiagBlocksLowerTriangular" | custom-call | tf_op jit(solution)/shard_map/jit(cholesky)/cholesky | solution.py:59
  496.7 2.3 convolution_subtract_fusion.2
  499.1 11.9 %cholesky.487 = f32[128,128]{1,0:T(8,128)S(1)} custom-call(f32[128,128]{1,0:T(8,128)S(1)} %cholesky.594), custom_call_target="Cholesky" | custom-call | tf_op jit(solution)/shard_map/jit(cholesky)/cholesky | solution.py:59
  512.3 9.8 %custom-call.62 = f32[1,128,128]{1,2,0:T(8,128)S(1)} custom-call(f32[1,128,128]{2,1,0:T(8,128)S(1)} %get-tuple-element.33), custom_call_target="InvertDiagBlocksLowerTriangular" | custom-call | tf_op jit(solution)/shard_map/jit(cholesky)/cholesky | solution.py:59
  523.2 2.3 convolution_subtract_fusion.3
  525.5 11.7 %cholesky.506 = f32[128,128]{1,0:T(8,128)S(1)} custom-call(f32[128,128]{1,0:T(8,128)S(1)} %cholesky.599), custom_call_target="Cholesky" | custom-call | tf_op jit(solution)/shard_map/jit(cholesky)/cholesky | solution.py:59
  538.5 10.0 %custom-call.63 = f32[1,128,128]{1,2,0:T(8,128)S(1)} custom-call(f32[1,128,128]{2,1,0:T(8,128)S(1)} %get-tuple-element.30), custom_call_target="InvertDiagBlocksLowerTriangular" | custom-call | tf_op jit(solution)/shard_map/jit(cholesky)/cholesky | solution.py:59
  549.6 2.3 convolution_subtract_fusion.4
  551.8 11.7 %cholesky.526 = f32[128,128]{1,0:T(8,128)S(1)} custom-call(f32[128,128]{1,0:T(8,128)S(1)} %cholesky.604), custom_call_target="Cholesky" | custom-call | tf_op jit(solution)/shard_map/jit(cholesky)/cholesky | solution.py:59
  564.8 9.8 %custom-call.64 = f32[1,128,128]{1,2,0:T(8,128)S(1)} custom-call(f32[1,128,128]{2,1,0:T(8,128)S(1)} %get-tuple-element.27), custom_call_target="InvertDiagBlocksLowerTriangular" | custom-call | tf_op jit(solution)/shard_map/jit(cholesky)/cholesky | solution.py:59
  575.6 2.0 convolution_subtract_fusion.5
  577.6 11.9 %cholesky.546 = f32[128,128]{1,0:T(8,128)S(1)} custom-call(f32[128,128]{1,0:T(8,128)S(1)} %cholesky.609), custom_call_target="Cholesky" | custom-call | tf_op jit(solution)/shard_map/jit(cholesky)/cholesky | solution.py:59
  590.8 9.8 %custom-call.65 = f32[1,128,128]{1,2,0:T(8,128)S(1)} custom-call(f32[1,128,128]{2,1,0:T(8,128)S(1)} %get-tuple-element.24), custom_call_target="InvertDiagBlocksLowerTriangular" | custom-call | tf_op jit(solution)/shard_map/jit(cholesky)/cholesky | solution.py:59
  601.5 1.8 convolution_subtract_fusion.6
  603.3 11.7 %cholesky.564 = f32[128,128]{1,0:T(8,128)S(1)} custom-call(f32[128,128]{1,0:T(8,128)S(1)} %convolution_subtract_fusion.6), custom_call_target="Cholesky" | custom-call | tf_op jit(solution)/shard_map/jit(cholesky)/cholesky | solution.py:59
  (75 shorter events, 31.0 us)
Async XLA Ops:
  7.2 353.3 %all-reduce.8.cloned.1.call-start = ((), (), s32[]{:S(2)}) async-start(), calls=%async_computation.1 | async-start | bytes 16777216 | tf_op jit(solution)/shard_map/psum | solution.py:52
  22.3 4.8 copy-start.12
  27.1 8.2 %copy-start.11 = (bf16[128,32,14,14]{0,1,3,2:T(8,128)(2,1)S(1)}, bf16[128,32,14,14]{0,1,3,2:T(8,128)(2,1)}, u32[]{:S(2)}) copy-start(bf16[128,32,14,14]{0,1,3,2:T(8,128)(2,1)} %get-tuple-element.16) | copy-start | bytes 4816900
  30.4 8.2 %copy-start.10 = (bf16[128,32,14,14]{0,1,3,2:T(8,128)(2,1)S(1)}, bf16[128,32,14,14]{0,1,3,2:T(8,128)(2,1)}, u32[]{:S(2)}) copy-start(bf16[128,32,14,14]{0,1,3,2:T(8,128)(2,1)} %get-tuple-element.17) | copy-start | bytes 4816900
  38.6 8.2 %copy-start.9 = (bf16[128,32,14,14]{0,1,3,2:T(8,128)(2,1)S(1)}, bf16[128,32,14,14]{0,1,3,2:T(8,128)(2,1)}, u32[]{:S(2)}) copy-start(bf16[128,32,14,14]{0,1,3,2:T(8,128)(2,1)} %get-tuple-element.19) | copy-start | bytes 4816900
  42.0 8.2 %copy-start.8 = (bf16[128,32,14,14]{0,1,3,2:T(8,128)(2,1)S(1)}, bf16[128,32,14,14]{0,1,3,2:T(8,128)(2,1)}, u32[]{:S(2)}) copy-start(bf16[128,32,14,14]{0,1,3,2:T(8,128)(2,1)} %get-tuple-element.12) | copy-start | bytes 4816900
  46.9 6.7 %copy-start.13 = (s32[32,288]{1,0:T(8,128)S(1)}, s32[32,288]{1,0:T(8,128)}, u32[]{:S(2)}) copy-start(s32[32,288]{1,0:T(8,128)} %param.6) | copy-start | bytes 110596
  57.3 3.4 copy-start.7
  57.4 4.9 copy-start.6
  60.8 3.1 copy-start.5
  62.3 3.1 copy-start.4
  63.8 3.1 copy-start.3
  65.4 3.1 copy-start.1
  66.9 3.1 copy-start.2
  71.6 12.2 %copy-start.14 = (s32[32,32]{1,0:T(8,128)S(1)}, s32[32,32]{1,0:T(8,128)}, u32[]{:S(2)}) copy-start(s32[32,32]{1,0:T(8,128)} %param.7) | copy-start | bytes 12292
  86.5 315.6 %all-reduce.6.cloned.1.call-start = ((), (), s32[]{:S(2)}) async-start(), calls=%async_computation | async-start | bytes 8388608 | tf_op jit(solution)/shard_map/psum | solution.py:59
  417.0 1.9 copy-start
Sparse Core Ops, SparseCore 0:
  86.6 273.7 all-reduce.7
  374.7 27.4 all-reduce.5
where the time goes:
time: 641 us; the launch traced here: 631 us
  waiting for transfers between devices  300 us (47%)
  other arithmetic  183 us (29%)
  local copies, waits for them, and re-layouts  77.6 us (12%)
  matrix products  50.7 us (8%)
  between operations  19.6 us (3%)
    psum x1, waiting for transfers between devices, local(): in_sum, out_sum = lax.psum((in_part, out_part), 'chan')  274 us
    another operation x30, other arithmetic, local(): factor = jnp.linalg.cholesky(lax.psum(gram_part, 'samp') + identity_mat).T  172 us
    another operation x10, local copies, waits for them, and re-layouts, project(): jnp.stack(tap_list, axis=2)  36.4 us
    psum x1, waiting for transfers between devices, local(): factor = jnp.linalg.cholesky(lax.psum(gram_part, 'samp') + identity_mat).T  26.6 us
    unnamed x41, local copies, waits for them, and re-layouts  25.2 us
    another operation x14, matrix products, local(): factor = jnp.linalg.cholesky(lax.psum(gram_part, 'samp') + identity_mat).T  23.1 us
  transfers between devices with their start and end apart: 2, of which 2 were waited for; matrix products, arithmetic and copies ran while one was open for 0% of the time, Pallas kernels for 0%

commit v1 on v0

v1 whole, which is shorter than its diff:
```python
import math

import jax
import jax.numpy as jnp
from jax import lax
from jax.sharding import PartitionSpec as P

C = 256


def project(images, out_grads, in_signs, out_signs):
    samples, channels, cells = images.shape
    side_in = math.isqrt(cells)
    picture = images.reshape(samples, channels, side_in, side_in)
    width_in = in_signs.shape[1] // 9
    in_matrix = (2 * in_signs - 1).astype(jnp.bfloat16).reshape(channels, 3, 3, width_in)
    kernel = jnp.transpose(in_matrix, (3, 0, 1, 2))
    in_part = lax.conv_general_dilated(
        picture,
        kernel,
        window_strides=(2, 2),
        padding=((1, 1), (1, 1)),
        dimension_numbers=("NCHW", "OIHW", "NCHW"),
        preferred_element_type=jnp.float32,
    )
    in_part = in_part.reshape(samples, width_in, -1)
    out_matrix = (2 * out_signs - 1).astype(jnp.bfloat16)
    out_part = jnp.einsum("ncp,cl->nlp", out_grads, out_matrix, preferred_element_type=jnp.float32)
    return (in_part, out_part)


def sketch(in_sum, out_sum, total_channels):
    in_feat = in_sum / math.sqrt(9 * total_channels)
    out_feat = out_sum / math.sqrt(total_channels)
    cells = in_sum.shape[2]
    outer = jnp.einsum(
        "nlp,njp->nlj", out_feat, in_feat, precision=lax.Precision.HIGHEST
    ) / math.sqrt(cells)
    return outer.reshape(outer.shape[0], -1)


def local(images, out_grads, in_signs, out_signs):
    samples = images.shape[0]
    in_part, out_part = project(images, out_grads, in_signs, out_signs)
    width_in = in_part.shape[1]
    both = jnp.concatenate([in_part, out_part], axis=1).reshape(samples, -1)
    both = lax.psum_scatter(both, "chan", scatter_dimension=0, tiled=True)
    both = both.reshape(both.shape[0], -1, in_part.shape[2])
    in_sum = both[:, :width_in]
    out_sum = both[:, width_in:]
    own = sketch(in_sum, out_sum, C)
    every = lax.all_gather(own, ("samp", "chan"), axis=0, tiled=True)
    batch_total = samples * lax.axis_size("samp")
    width = every.shape[1]
    identity_mat = jnp.eye(width, dtype=jnp.float32)
    gram = jnp.einsum("nk,nm->km", every, every, precision=lax.Precision.HIGHEST) / batch_total
    factor = jnp.linalg.cholesky(gram + identity_mat).T
    chan_count = lax.axis_size("chan")
    rows_here = width // chan_count
    r_rows = lax.dynamic_slice_in_dim(factor, lax.axis_index("chan") * rows_here, rows_here, 0)
    return (own[None], r_rows)


def solution(mesh):
    in_specs = (
        P(("parts", "samp"), "chan", None),
        P(("parts", "samp"), "chan", None),
        P("chan", None),
        P("chan", None),
    )
    out_specs = (P("samp", ("parts", "chan"), None), P(("parts", "chan"), None))
    return jax.shard_map(local, mesh=mesh, in_specs=in_specs, out_specs=out_specs, check_vma=False)
```

time: 641 us -> 444 us (0.69)
  waiting for transfers between devices: 300 us -> 159 us
  local copies, waits for them, and re-layouts: 77.6 us -> 40.9 us
  matrix products: 50.7 us -> 37.9 us
    psum x2 -> x0, waiting for transfers between devices: 300 us -> none  [the longest x1 274 us: local(): in_sum, out_sum = lax.psum((in_part, out_part), 'chan')]
    reduce_scatter x0 -> x1, waiting for transfers between devices: none -> 122 us  [local(): both = lax.psum_scatter(both, 'chan', scatter_dimension=0, tiled=True)]
    all_gather x0 -> x1, waiting for transfers between devices: none -> 36.5 us  [local(): every = lax.all_gather(own, ('samp', 'chan'), axis=0, tiled=True)]
    another operation x18 -> x9, local copies, waits for them, and re-layouts: 39 us -> 3.31 us  [the longest x8 2.54 us: local(): factor = jnp.linalg.cholesky(gram + identity_mat).T]
    dot_general x1 -> x0, matrix products: 12.2 us -> none  [project(): jnp.einsum('nctp,ctj->njp', patches, in_matrix, preferred_element_type=jn...]
    dot_general x1, matrix products: 7.8 us -> 0.65 us  [sketch(): jnp.einsum('nlp,njp->nlj', out_feat, in_feat, precision=lax.Precision.HIG...]
    unnamed x41 -> x14, local copies, waits for them, and re-layouts: 25.2 us -> 28.2 us
where the time goes in v1:
time: 444 us; the launch traced here: 439 us
  other arithmetic  181 us (41%)
  waiting for transfers between devices  159 us (36%)
  local copies, waits for them, and re-layouts  40.9 us (9%)
  matrix products  37.9 us (9%)
  between operations  19.3 us (4%)
    another operation x30, other arithmetic, local(): factor = jnp.linalg.cholesky(gram + identity_mat).T  172 us
    reduce_scatter x1, waiting for transfers between devices, local(): both = lax.psum_scatter(both, 'chan', scatter_dimension=0, tiled=True)  122 us
    all_gather x1, waiting for transfers between devices, local(): every = lax.all_gather(own, ('samp', 'chan'), axis=0, tiled=True)  36.5 us
    unnamed x14, local copies, waits for them, and re-layouts  28.2 us
    another operation x14, matrix products, local(): factor = jnp.linalg.cholesky(gram + identity_mat).T  23.2 us
  transfers between devices with their start and end apart: 2, of which 2 were waited for; matrix products, arithmetic and copies ran while one was open for 0% of the time, Pallas kernels for 0%

profile of v1, /device:TPU:0, one launch (start us, length us, event | category | flops | bytes accessed | tf_op | source)
XLA Modules:
  0.0 438.7 jit_solution(2141450663651336238)
XLA Ops:
  7.2 7.3 %copy.20 = bf16[128,32,784]{0,1,2:T(8,128)(2,1)} copy(bf16[128,32,784]{0,2,1:T(8,128)(2,1)} %param.4) | data formatting | bytes 12845056 | tf_op args[0]
  14.7 4.8 %fusion.41 = f32[128,32,14,14]{0,1,3,2:T(8,128)S(1)} fusion(bf16[128,32,28,28]{0,1,3,2:T(8,128)(2,1)} %bitcast.60, bf16[32,3,3,32]{0,3,2,1:T(8,128)(2,1)S(1)} %bitcast.62), kind=kOutput, calls=%fused_computation.99 | convolution fusion | flops 440664064 | bytes 9652224 | tf_op jit(solution)/shard_map/conv_general_dilated | solution.py:18
  20.1 3.4 pad_maximum_fusion
  23.6 9.1 %copy.34 = f32[128,64,196]{2,1,0:T(8,128)} copy(f32[128,64,196]{0,1,2:T(8,128)} %pad_maximum_fusion) | data formatting | bytes 12845056
  32.6 8.9 %reshape.84 = f32[128,12544]{1,0:T(8,128)} reshape(f32[128,64,196]{2,1,0:T(8,128)} %copy.34) | data formatting | bytes 12845056
  41.9 122.4 %reduce-scatter.4.cloned.1.call-done = f32[16,12544]{1,0:T(8,128)} async-done(((f32[128,12544]{1,0:T(8,128)}), f32[16,12544]{1,0:T(8,128)}) %reduce-scatter.4.cloned.1.call-update) | async-done | bytes 802832 | tf_op jit(solution)/shard_map/reduce_scatter | solution.py:47
  164.3 2.6 reshape.77
  166.9 0.7 convolution_multiply_fusion
  167.6 0.8 reshape.78
  168.4 0.8 broadcast_in_dim_reshape.3
  169.2 36.5 %all-gather.2.cloned.1.call-done = f32[256,1024]{1,0:T(8,128)} async-done(((f32[16,1024]{1,0:T(8,128)}), f32[256,1024]{1,0:T(8,128)}) %all-gather.2.cloned.1.call-update) | async-done | bytes 1048592 | tf_op jit(solution)/shard_map/all_gather | solution.py:52
  205.7 8.7 %convert_add_fusion = (f32[1024,1024]{0,1:T(8,128)}, f32[1024,1024]{0,1:T(8,128)}) fusion(f32[256,1024]{1,0:T(8,128)} %all-gather.2.cloned.1.call-done), kind=kOutput, calls=%fused_computation.5 | convolution fusion | flops 3225419776 | bytes 9437184 | tf_op jit(solution)/shard_map/nk,nm->km/dot_general | solution.py:56
  214.3 5.8 %copy.26 = f32[1024,1024]{1,0:T(8,128)} copy(f32[1024,1024]{0,1:T(8,128)} %get-tuple-element.30) | data formatting | bytes 8388608 | tf_op jit(solution)/shard_map/add | solution.py:57
  220.2 4.5 %fusion.1 = f32[1024,1024]{1,0:T(8,128)S(1)} fusion(f32[1024,1024]{1,0:T(8,128)} %copy.26, f32[1024,1024]{0,1:T(8,128)} %get-tuple-element.31), kind=kLoop, calls=%fused_computation.3 | loop fusion | flops 6291456 | bytes 12582912 | tf_op jit(solution)/shard_map/jit(cholesky)/div | solution.py:57
  224.6 1.9 copy-done.2
  226.6 11.7 %cholesky.223 = f32[128,128]{1,0:T(8,128)S(1)} custom-call(f32[128,128]{1,0:T(8,128)S(1)} %cholesky.580), custom_call_target="Cholesky" | custom-call | tf_op jit(solution)/shard_map/jit(cholesky)/cholesky | solution.py:57
  238.3 9.8 %custom-call.59 = f32[1,128,128]{1,2,0:T(8,128)S(1)} custom-call(f32[1,128,128]{2,1,0:T(8,128)S(1)} %get-tuple-element.29), custom_call_target="InvertDiagBlocksLowerTriangular" | custom-call | tf_op jit(solution)/shard_map/jit(cholesky)/cholesky | solution.py:57
  248.1 2.5 cholesky.255
  250.6 2.4 constant_dynamic-update-slice_fusion.7
  253.0 1.5 convolution_subtract_fusion
  254.6 11.8 %cholesky.244 = f32[128,128]{1,0:T(8,128)S(1)} custom-call(f32[128,128]{1,0:T(8,128)S(1)} %cholesky.584), custom_call_target="Cholesky" | custom-call | tf_op jit(solution)/shard_map/jit(cholesky)/cholesky | solution.py:57
  267.1 9.8 %custom-call.60 = f32[1,128,128]{1,2,0:T(8,128)S(1)} custom-call(f32[1,128,128]{2,1,0:T(8,128)S(1)} %get-tuple-element.26), custom_call_target="InvertDiagBlocksLowerTriangular" | custom-call | tf_op jit(solution)/shard_map/jit(cholesky)/cholesky | solution.py:57
  276.9 1.2 convolution_dynamic-update-slice_fusion
  278.1 2.1 convolution_subtract_fusion.1
  280.2 11.7 %cholesky.468 = f32[128,128]{1,0:T(8,128)S(1)} custom-call(f32[128,128]{1,0:T(8,128)S(1)} %cholesky.589), custom_call_target="Cholesky" | custom-call | tf_op jit(solution)/shard_map/jit(cholesky)/cholesky | solution.py:57
  293.2 9.8 %custom-call.61 = f32[1,128,128]{1,2,0:T(8,128)S(1)} custom-call(f32[1,128,128]{2,1,0:T(8,128)S(1)} %get-tuple-element.23), custom_call_target="InvertDiagBlocksLowerTriangular" | custom-call | tf_op jit(solution)/shard_map/jit(cholesky)/cholesky | solution.py:57
  303.0 1.2 convolution_dynamic-update-slice_fusion.1
  304.2 2.3 convolution_subtract_fusion.2
  306.5 11.9 %cholesky.487 = f32[128,128]{1,0:T(8,128)S(1)} custom-call(f32[128,128]{1,0:T(8,128)S(1)} %cholesky.594), custom_call_target="Cholesky" | custom-call | tf_op jit(solution)/shard_map/jit(cholesky)/cholesky | solution.py:57
  319.7 9.8 %custom-call.62 = f32[1,128,128]{1,2,0:T(8,128)S(1)} custom-call(f32[1,128,128]{2,1,0:T(8,128)S(1)} %get-tuple-element.20), custom_call_target="InvertDiagBlocksLowerTriangular" | custom-call | tf_op jit(solution)/shard_map/jit(cholesky)/cholesky | solution.py:57
  329.5 1.1 convolution_dynamic-update-slice_fusion.2
  330.6 2.4 convolution_subtract_fusion.3
  333.1 11.7 %cholesky.506 = f32[128,128]{1,0:T(8,128)S(1)} custom-call(f32[128,128]{1,0:T(8,128)S(1)} %cholesky.599), custom_call_target="Cholesky" | custom-call | tf_op jit(solution)/shard_map/jit(cholesky)/cholesky | solution.py:57
  346.1 10.2 %custom-call.63 = f32[1,128,128]{1,2,0:T(8,128)S(1)} custom-call(f32[1,128,128]{2,1,0:T(8,128)S(1)} %get-tuple-element.17), custom_call_target="InvertDiagBlocksLowerTriangular" | custom-call | tf_op jit(solution)/shard_map/jit(cholesky)/cholesky | solution.py:57
  356.3 1.0 convolution_dynamic-update-slice_fusion.3
  357.4 2.3 convolution_subtract_fusion.4
  359.6 11.7 %cholesky.526 = f32[128,128]{1,0:T(8,128)S(1)} custom-call(f32[128,128]{1,0:T(8,128)S(1)} %cholesky.604), custom_call_target="Cholesky" | custom-call | tf_op jit(solution)/shard_map/jit(cholesky)/cholesky | solution.py:57
  372.6 9.8 %custom-call.64 = f32[1,128,128]{1,2,0:T(8,128)S(1)} custom-call(f32[1,128,128]{2,1,0:T(8,128)S(1)} %get-tuple-element.14), custom_call_target="InvertDiagBlocksLowerTriangular" | custom-call | tf_op jit(solution)/shard_map/jit(cholesky)/cholesky | solution.py:57
  382.4 0.9 convolution_dynamic-update-slice_fusion.4
  383.4 2.0 convolution_subtract_fusion.5
  385.4 11.9 %cholesky.546 = f32[128,128]{1,0:T(8,128)S(1)} custom-call(f32[128,128]{1,0:T(8,128)S(1)} %cholesky.609), custom_call_target="Cholesky" | custom-call | tf_op jit(solution)/shard_map/jit(cholesky)/cholesky | solution.py:57
  398.5 9.8 %custom-call.65 = f32[1,128,128]{1,2,0:T(8,128)S(1)} custom-call(f32[1,128,128]{2,1,0:T(8,128)S(1)} %get-tuple-element.11), custom_call_target="InvertDiagBlocksLowerTriangular" | custom-call | tf_op jit(solution)/shard_map/jit(cholesky)/cholesky | solution.py:57
  408.4 0.8 convolution_dynamic-update-slice_fusion.5
  409.2 1.8 convolution_subtract_fusion.6
  411.0 11.7 %cholesky.564 = f32[128,128]{1,0:T(8,128)S(1)} custom-call(f32[128,128]{1,0:T(8,128)S(1)} %convolution_subtract_fusion.6), custom_call_target="Cholesky" | custom-call | tf_op jit(solution)/shard_map/jit(cholesky)/cholesky | solution.py:57
  423.3 0.7 compare_reduce_fusion
  429.5 1.1 fusion.8
  430.6 1.0 copy.27
  (37 shorter events, 9.5 us)
Async XLA Ops:
  7.2 12.3 %copy-start = (bf16[128,32,196]{0,1,2:T(8,128)(2,1)S(1)}, bf16[128,32,196]{0,1,2:T(8,128)(2,1)}, u32[]{:S(2)}) copy-start(bf16[128,32,196]{0,1,2:T(8,128)(2,1)} %param.5) | copy-start | bytes 4816900
  7.2 7.3 %copy-start.3 = (s32[32,288]{1,0:T(8,128)S(1)}, s32[32,288]{1,0:T(8,128)}, u32[]{:S(2)}) copy-start(s32[32,288]{1,0:T(8,128)} %param.6) | copy-start | bytes 110596
  7.2 157.1 %reduce-scatter.4.cloned.1.call-start = ((), (), s32[]{:S(2)}) async-start(), calls=%async_computation.2 | async-start | bytes 7225344 | tf_op jit(solution)/shard_map/reduce_scatter | solution.py:47
  14.7 4.8 %copy-start.4 = (s32[32,32]{1,0:T(8,128)S(1)}, s32[32,32]{1,0:T(8,128)}, u32[]{:S(2)}) copy-start(s32[32,32]{1,0:T(8,128)} %param.7) | copy-start | bytes 12292
  41.6 164.1 %all-gather.2.cloned.1.call-start = ((), (), s32[]{:S(2)}) async-start(), calls=%async_computation.1 | async-start | bytes 1114112 | tf_op jit(solution)/shard_map/all_gather | solution.py:52
  224.6 1.9 copy-start.2
  330.6 101.0 %copy-start.1 = (bf16[128,32,196]{0,1,2:T(8,128)(2,1)S(1)}, bf16[128,32,196]{0,1,2:T(8,128)(2,1)}, u32[]{:S(2)}) copy-start(bf16[128,32,196]{0,1,2:T(8,128)(2,1)} %param.5) | copy-start | bytes 4816900
Sparse Core Ops, SparseCore 0:
  41.7 122.5 reduce-scatter.3
  168.5 37.0 all-gather.1

commit v2 on v1

--- a/solution.py
+++ b/solution.py
@@ -3,9 +3,73 @@
 import jax
 import jax.numpy as jnp
 from jax import lax
+from jax.experimental import pallas as pl
+from jax.experimental.pallas import tpu as pltpu
 from jax.sharding import PartitionSpec as P
+import functools
 
 C = 256
+HI = lax.Precision.HIGHEST
+
+
+def _factor_block(d, b):
+    rows = lax.broadcasted_iota(jnp.int32, (b, 2 * b), 0)
+    lanes = lax.broadcasted_iota(jnp.int32, (1, 2 * b), 1)
+    x = jnp.concatenate([d, jnp.eye(b, dtype=jnp.float32)], axis=1)
+    for j in range(b):
+        row = x[j:j + 1, :]
+        s = lax.rsqrt(row[:, j:j + 1])
+        r = jnp.where(lanes >= j, row * s, 0.0)
+        c = jnp.where(rows[:, :1] > j, x[:, j:j + 1] * s, 0.0)
+        x = jnp.where(rows == j, r, x - c * r)
+    return x[:, :b], x[:, b:]
+
+
+def _chol_kernel(a_ref, r_ref, w_ref, *, nb, b):
+    n = nb * b
+    w_ref[...] = a_ref[...]
+
+    def step(k, carry):
+        wk = w_ref[k]
+        d = jnp.zeros((b, b), jnp.float32)
+        for j in range(nb):
+            d = jnp.where(k == j, wk[:, j * b:(j + 1) * b], d)
+        rkk, linv = _factor_block(d, b)
+        pfull = jnp.dot(linv, wk, precision=HI, preferred_element_type=jnp.float32)
+        blocks = []
+        pblocks = []
+        for j in range(nb):
+            pj = pfull[:, j * b:(j + 1) * b]
+            blocks.append(jnp.where(j > k, pj, jnp.where(j == k, rkk, 0.0)))
+            pblocks.append(jnp.where(j > k, pj, 0.0))
+        r_ref[k] = jnp.concatenate(blocks, axis=1)
+        p = jnp.concatenate(pblocks, axis=1)
+        for i in range(nb):
+            @pl.when(i > k)
+            def _():
+                ti = pblocks[i]
+                upd = lax.dot_general(ti, p, (((0,), (0,)), ((), ())), precision=HI,
+                                      preferred_element_type=jnp.float32)
+                w_ref[i] = w_ref[i] - upd
+        return carry
+
+    lax.fori_loop(0, nb, step, 0)
+
+
+def cholesky_upper(a, b=128, interpret=False):
+    n = a.shape[0]
+    nb = n // b
+    a3 = a.reshape(nb, b, n)
+    out = pl.pallas_call(
+        functools.partial(_chol_kernel, nb=nb, b=b),
+        out_shape=jax.ShapeDtypeStruct((nb, b, n), jnp.float32),
+        in_specs=[pl.BlockSpec(memory_space=pltpu.VMEM)],
+        out_specs=pl.BlockSpec(memory_space=pltpu.VMEM),
+        scratch_shapes=[pltpu.VMEM((nb, b, n), jnp.float32)],
+        compiler_params=pltpu.CompilerParams(vmem_limit_bytes=48 * 1024 * 1024),
+        interpret=interpret,
+    )(a3)
+    return out.reshape(n, n)
 
 
 def project(images, out_grads, in_signs, out_signs):
@@ -54,7 +118,7 @@
     width = every.shape[1]
     identity_mat = jnp.eye(width, dtype=jnp.float32)
     gram = jnp.einsum("nk,nm->km", every, every, precision=lax.Precision.HIGHEST) / batch_total
-    factor = jnp.linalg.cholesky(gram + identity_mat).T
+    factor = cholesky_upper(gram + identity_mat)
     chan_count = lax.axis_size("chan")
     rows_here = width // chan_count
     r_rows = lax.dynamic_slice_in_dim(factor, lax.axis_index("chan") * rows_here, rows_here, 0)

time: 444 us -> 333 us (0.75); the launches traced: 439 us -> 333 us
  other arithmetic: 181 us -> 3.45 us
  Pallas kernels: 0 us -> 113 us
  matrix products: 37.9 us -> 13.2 us
  local copies, waits for them, and re-layouts: 40.9 us -> 30.4 us
  between operations: 19.3 us -> 14.1 us
    another operation x30 -> x0, other arithmetic: 172 us -> none  [local(): factor = jnp.linalg.cholesky(gram + identity_mat).T]
    pallas_call x0 -> x1, Pallas kernels: none -> 113 us  [cholesky_upper(): pl.pallas_call(functools.partial(_chol_kernel, nb=nb, b=b), out_shape=jax...]
    another operation x14 -> x0, matrix products: 23.2 us -> none  [local(): factor = jnp.linalg.cholesky(gram + identity_mat).T]
    add x1 -> x0, local copies, waits for them, and re-layouts: 5.84 us -> none  [local(): factor = jnp.linalg.cholesky(gram + identity_mat).T]
    div x1 -> x0, other arithmetic: 4.46 us -> none  [local(): factor = jnp.linalg.cholesky(gram + identity_mat).T]
    unnamed x14 -> x9, local copies, waits for them, and re-layouts: 28.2 us -> 25.3 us
where the time goes in v2:
time: 333 us
  waiting for transfers between devices  159 us (48%)
  Pallas kernels  113 us (34%)
  local copies, waits for them, and re-layouts  30.4 us (9%)
  between operations  14.1 us (4%)
  matrix products  13.2 us (4%)
  other arithmetic  3.45 us (1%)
    reduce_scatter x1, waiting for transfers between devices, local(): both = lax.psum_scatter(both, 'chan', scatter_dimension=0, tiled=True)  123 us
    pallas_call x1, Pallas kernels, cholesky_upper(): pl.pallas_call(functools.partial(_chol_kernel, nb=nb, b=b), out_shape=jax...  113 us
    all_gather x1, waiting for transfers between devices, local(): every = lax.all_gather(own, ('samp', 'chan'), axis=0, tiled=True)  36.5 us
    unnamed x9, local copies, waits for them, and re-layouts  25.3 us
    dot_general x1, matrix products, local(): jnp.einsum('nk,nm->km', every, every, precision=lax.Precision.HIGHEST)  7.1 us
  transfers between devices with their start and end apart: 2, of which 2 were waited for; matrix products, arithmetic and copies ran while one was open for 0% of the time, Pallas kernels for 0%

profile of v2, /device:TPU:0, one launch (start us, length us, event | category | flops | bytes accessed | tf_op | source)
XLA Modules:
  0.0 333.0 jit_solution(10285640926389403024)
XLA Ops:
  7.2 0.0 copy-start
  7.2 0.0 copy-start.1
  7.2 0.0 copy-start.2
  7.2 0.0 reduce-scatter.4.cloned.1.call-start
  7.2 7.3 %copy.14 = bf16[128,32,784]{0,1,2:T(8,128)(2,1)} copy(bf16[128,32,784]{0,2,1:T(8,128)(2,1)} %param.4) | data formatting | bytes 12845056 | tf_op args[0]
  14.5 0.0 copy-done.1
  14.5 0.1 copy.20
  14.6 0.0 copy-done
  14.7 0.0 copy-done.2
  14.7 0.6 convolution_bitcast_fusion
  15.3 4.8 %fusion.10 = f32[128,32,14,14]{0,1,3,2:T(8,128)S(1)} fusion(bf16[128,32,28,28]{0,1,3,2:T(8,128)(2,1)} %bitcast.18, bf16[32,3,3,32]{0,3,2,1:T(8,128)(2,1)S(1)} %bitcast.20), kind=kOutput, calls=%fused_computation.19 | convolution fusion | flops 440664064 | bytes 9652224 | tf_op jit(solution)/shard_map/conv_general_dilated | solution.py:82
  20.1 3.4 %pad_maximum_fusion = f32[128,64,196]{0,1,2:T(8,128)} fusion(f32[128,32,196]{0,1,2:T(8,128)S(1)} %convolution_bitcast_fusion, f32[128,32,196]{0,1,2:T(8,128)S(1)} %bitcast.19), kind=kLoop, calls=%fused_computation | loop fusion | flops 1605632 | bytes 12845056 | tf_op jit(solution)/shard_map/concatenate | solution.py:110
  23.5 9.1 %copy.24 = f32[128,64,196]{2,1,0:T(8,128)} copy(f32[128,64,196]{0,1,2:T(8,128)} %pad_maximum_fusion) | data formatting | bytes 12845056
  32.6 8.9 %reshape.37 = f32[128,12544]{1,0:T(8,128)} reshape(f32[128,64,196]{2,1,0:T(8,128)} %copy.24) | data formatting | bytes 12845056
  41.5 0.0 reduce-scatter.4.cloned.1.call-update
  41.6 0.0 all-gather.2.cloned.1.call-start
  41.6 122.7 %reduce-scatter.4.cloned.1.call-done = f32[16,12544]{1,0:T(8,128)} async-done(((f32[128,12544]{1,0:T(8,128)}), f32[16,12544]{1,0:T(8,128)}) %reduce-scatter.4.cloned.1.call-update) | async-done | bytes 802832 | tf_op jit(solution)/shard_map/reduce_scatter | solution.py:111
  164.3 2.6 reshape.32
  167.0 0.7 convolution_multiply_fusion
  167.6 0.8 reshape.33
  168.4 0.0 all-gather.2.cloned.1.call-update
  168.4 0.8 broadcast_in_dim_reshape.3
  169.2 36.5 %all-gather.2.cloned.1.call-done = f32[256,1024]{1,0:T(8,128)} async-done(((f32[16,1024]{1,0:T(8,128)}), f32[256,1024]{1,0:T(8,128)}) %all-gather.2.cloned.1.call-update) | async-done | bytes 1048592 | tf_op jit(solution)/shard_map/all_gather | solution.py:116
  205.7 7.1 %convert_add_fusion = f32[1024,1024]{1,0:T(8,128)} fusion(f32[256,1024]{1,0:T(8,128)} %all-gather.2.cloned.1.call-done), kind=kOutput, calls=%fused_computation.1 | convolution fusion | flops 3225419776 | bytes 5242880 | tf_op jit(solution)/shard_map/nk,nm->km/dot_general | solution.py:120
  212.8 112.5 %shard_map.59 = f32[8,128,1024]{2,1,0:T(8,128)S(1)} custom-call(f32[8,128,1024]{2,1,0:T(8,128)} %bitcast.17), custom_call_target="tpu_custom_call" | custom-call | tf_op jit(solution)/shard_map/pallas_call | solution.py:63
  325.3 0.8 constant_dynamic-slice_fusion
  (1 shorter events, 0.0 us)
Async XLA Ops:
  7.2 7.5 %copy-start = (bf16[128,32,196]{0,1,2:T(8,128)(2,1)S(1)}, bf16[128,32,196]{0,1,2:T(8,128)(2,1)}, u32[]{:S(2)}) copy-start(bf16[128,32,196]{0,1,2:T(8,128)(2,1)} %param.5) | copy-start | bytes 4816900
  7.2 7.3 %copy-start.1 = (s32[32,288]{1,0:T(8,128)S(1)}, s32[32,288]{1,0:T(8,128)}, u32[]{:S(2)}) copy-start(s32[32,288]{1,0:T(8,128)} %param.6) | copy-start | bytes 110596
  7.2 7.5 %copy-start.2 = (s32[32,32]{1,0:T(8,128)S(1)}, s32[32,32]{1,0:T(8,128)}, u32[]{:S(2)}) copy-start(s32[32,32]{1,0:T(8,128)} %param.7) | copy-start | bytes 12292
  7.2 157.1 %reduce-scatter.4.cloned.1.call-start = ((), (), s32[]{:S(2)}) async-start(), calls=%async_computation.2 | async-start | bytes 7225344 | tf_op jit(solution)/shard_map/reduce_scatter | solution.py:111
  41.6 164.1 %all-gather.2.cloned.1.call-start = ((), (), s32[]{:S(2)}) async-start(), calls=%async_computation.1 | async-start | bytes 1114112 | tf_op jit(solution)/shard_map/all_gather | solution.py:116
Sparse Core Ops, SparseCore 0:
  41.7 122.6 reduce-scatter.3
  168.6 37.0 all-gather.1

commit v3 on v2

--- a/solution.py
+++ b/solution.py
@@ -44,13 +44,13 @@
             pblocks.append(jnp.where(j > k, pj, 0.0))
         r_ref[k] = jnp.concatenate(blocks, axis=1)
         p = jnp.concatenate(pblocks, axis=1)
-        for i in range(nb):
+        for i in range(1, nb):
             @pl.when(i > k)
             def _():
                 ti = pblocks[i]
-                upd = lax.dot_general(ti, p, (((0,), (0,)), ((), ())), precision=HI,
+                upd = lax.dot_general(ti, p[:, i * b:], (((0,), (0,)), ((), ())), precision=HI,
                                       preferred_element_type=jnp.float32)
-                w_ref[i] = w_ref[i] - upd
+                w_ref[i, :, i * b:] = w_ref[i, :, i * b:] - upd
         return carry
 
     lax.fori_loop(0, nb, step, 0)

time: 333 us -> 326 us (0.979)
  Pallas kernels: 113 us -> 105 us
    pallas_call x1, Pallas kernels: 113 us -> 105 us  [cholesky_upper(): pl.pallas_call(functools.partial(_chol_kernel, nb=nb, b=b), out_shape=jax...]
where the time goes in v3:
time: 326 us
  waiting for transfers between devices  159 us (49%)
  Pallas kernels  105 us (32%)
  local copies, waits for them, and re-layouts  30.4 us (9%)
  between operations  14.1 us (4%)
  matrix products  13.2 us (4%)
  other arithmetic  3.45 us (1%)
    reduce_scatter x1, waiting for transfers between devices, local(): both = lax.psum_scatter(both, 'chan', scatter_dimension=0, tiled=True)  123 us
    pallas_call x1, Pallas kernels, cholesky_upper(): pl.pallas_call(functools.partial(_chol_kernel, nb=nb, b=b), out_shape=jax...  105 us
    all_gather x1, waiting for transfers between devices, local(): every = lax.all_gather(own, ('samp', 'chan'), axis=0, tiled=True)  36.5 us
    unnamed x9, local copies, waits for them, and re-layouts  25.3 us
    dot_general x1, matrix products, local(): jnp.einsum('nk,nm->km', every, every, precision=lax.Precision.HIGHEST)  7.1 us
  transfers between devices with their start and end apart: 2, of which 2 were waited for; matrix products, arithmetic and copies ran while one was open for 0% of the time, Pallas kernels for 0%

profile of v3, /device:TPU:0, one launch (start us, length us, event | category | flops | bytes accessed | tf_op | source)
XLA Modules:
  0.0 325.8 jit_solution(6441287064491514188)
XLA Ops:
  7.2 0.0 copy-start
  7.2 0.0 copy-start.1
  7.2 0.0 copy-start.2
  7.2 0.0 reduce-scatter.4.cloned.1.call-start
  7.2 7.3 %copy.14 = bf16[128,32,784]{0,1,2:T(8,128)(2,1)} copy(bf16[128,32,784]{0,2,1:T(8,128)(2,1)} %param.4) | data formatting | bytes 12845056 | tf_op args[0]
  14.5 0.0 copy-done.1
  14.5 0.1 copy.20
  14.6 0.0 copy-done
  14.7 0.0 copy-done.2
  14.7 0.6 convolution_bitcast_fusion
  15.3 4.8 %fusion.10 = f32[128,32,14,14]{0,1,3,2:T(8,128)S(1)} fusion(bf16[128,32,28,28]{0,1,3,2:T(8,128)(2,1)} %bitcast.18, bf16[32,3,3,32]{0,3,2,1:T(8,128)(2,1)S(1)} %bitcast.20), kind=kOutput, calls=%fused_computation.19 | convolution fusion | flops 440664064 | bytes 9652224 | tf_op jit(solution)/shard_map/conv_general_dilated | solution.py:82
  20.1 3.4 %pad_maximum_fusion = f32[128,64,196]{0,1,2:T(8,128)} fusion(f32[128,32,196]{0,1,2:T(8,128)S(1)} %convolution_bitcast_fusion, f32[128,32,196]{0,1,2:T(8,128)S(1)} %bitcast.19), kind=kLoop, calls=%fused_computation | loop fusion | flops 1605632 | bytes 12845056 | tf_op jit(solution)/shard_map/concatenate | solution.py:110
  23.5 9.1 %copy.24 = f32[128,64,196]{2,1,0:T(8,128)} copy(f32[128,64,196]{0,1,2:T(8,128)} %pad_maximum_fusion) | data formatting | bytes 12845056
  32.6 8.9 %reshape.37 = f32[128,12544]{1,0:T(8,128)} reshape(f32[128,64,196]{2,1,0:T(8,128)} %copy.24) | data formatting | bytes 12845056
  41.5 0.0 reduce-scatter.4.cloned.1.call-update
  41.6 0.0 all-gather.2.cloned.1.call-start
  41.6 122.7 %reduce-scatter.4.cloned.1.call-done = f32[16,12544]{1,0:T(8,128)} async-done(((f32[128,12544]{1,0:T(8,128)}), f32[16,12544]{1,0:T(8,128)}) %reduce-scatter.4.cloned.1.call-update) | async-done | bytes 802832 | tf_op jit(solution)/shard_map/reduce_scatter | solution.py:111
  164.3 2.6 reshape.32
  167.0 0.7 convolution_multiply_fusion
  167.6 0.8 reshape.33
  168.4 0.0 all-gather.2.cloned.1.call-update
  168.4 0.8 broadcast_in_dim_reshape.3
  169.2 36.5 %all-gather.2.cloned.1.call-done = f32[256,1024]{1,0:T(8,128)} async-done(((f32[16,1024]{1,0:T(8,128)}), f32[256,1024]{1,0:T(8,128)}) %all-gather.2.cloned.1.call-update) | async-done | bytes 1048592 | tf_op jit(solution)/shard_map/all_gather | solution.py:116
  205.7 7.1 %convert_add_fusion = f32[1024,1024]{1,0:T(8,128)} fusion(f32[256,1024]{1,0:T(8,128)} %all-gather.2.cloned.1.call-done), kind=kOutput, calls=%fused_computation.1 | convolution fusion | flops 3225419776 | bytes 5242880 | tf_op jit(solution)/shard_map/nk,nm->km/dot_general | solution.py:120
  212.8 105.3 %shard_map.59 = f32[8,128,1024]{2,1,0:T(8,128)S(1)} custom-call(f32[8,128,1024]{2,1,0:T(8,128)} %bitcast.17), custom_call_target="tpu_custom_call" | custom-call | tf_op jit(solution)/shard_map/pallas_call | solution.py:63
  318.1 0.8 constant_dynamic-slice_fusion
  (1 shorter events, 0.0 us)
Async XLA Ops:
  7.2 7.5 %copy-start = (bf16[128,32,196]{0,1,2:T(8,128)(2,1)S(1)}, bf16[128,32,196]{0,1,2:T(8,128)(2,1)}, u32[]{:S(2)}) copy-start(bf16[128,32,196]{0,1,2:T(8,128)(2,1)} %param.5) | copy-start | bytes 4816900
  7.2 7.3 %copy-start.1 = (s32[32,288]{1,0:T(8,128)S(1)}, s32[32,288]{1,0:T(8,128)}, u32[]{:S(2)}) copy-start(s32[32,288]{1,0:T(8,128)} %param.6) | copy-start | bytes 110596
  7.2 7.5 %copy-start.2 = (s32[32,32]{1,0:T(8,128)S(1)}, s32[32,32]{1,0:T(8,128)}, u32[]{:S(2)}) copy-start(s32[32,32]{1,0:T(8,128)} %param.7) | copy-start | bytes 12292
  7.2 157.1 %reduce-scatter.4.cloned.1.call-start = ((), (), s32[]{:S(2)}) async-start(), calls=%async_computation.2 | async-start | bytes 7225344 | tf_op jit(solution)/shard_map/reduce_scatter | solution.py:111
  41.6 164.1 %all-gather.2.cloned.1.call-start = ((), (), s32[]{:S(2)}) async-start(), calls=%async_computation.1 | async-start | bytes 1114112 | tf_op jit(solution)/shard_map/all_gather | solution.py:116
Sparse Core Ops, SparseCore 0:
  41.7 122.6 reduce-scatter.3
  168.6 37.0 all-gather.1

commit v4 on v3

--- a/solution.py
+++ b/solution.py
@@ -103,12 +103,40 @@
     return outer.reshape(outer.shape[0], -1)
 
 
+def _ring_order(n):
+    if n % 2:
+        return list(range(n))
+    return list(range(0, n, 2)) + list(range(n - 1, 0, -2))
+
+
+def ring_reduce_scatter(x, axis):
+    n = lax.axis_size(axis)
+    order = _ring_order(n)
+    pos = jnp.asarray([order.index(c) for c in range(n)], jnp.int32)[lax.axis_index(axis)]
+    owner = jnp.asarray(order, jnp.int32)
+    blocks = x.reshape(n, -1, x.shape[-1])
+    h = x.shape[-1] // 2
+    fwd = [(order[q], order[(q + 1) % n]) for q in range(n)]
+    bwd = [(order[(q + 1) % n], order[q]) for q in range(n)]
+
+    def take(q, lo, hi):
+        blk = lax.dynamic_index_in_dim(blocks, owner[q % n], 0, keepdims=False)
+        return blk[:, lo:hi]
+
+    fa = take(pos - 1 + n, 0, h)
+    ba = take(pos + 1, h, x.shape[-1])
+    for step in range(1, n):
+        fa = lax.ppermute(fa, axis, fwd) + take(pos - 1 - step + 2 * n, 0, h)
+        ba = lax.ppermute(ba, axis, bwd) + take(pos + 1 + step, h, x.shape[-1])
+    return jnp.concatenate([fa, ba], axis=-1)
+
+
 def local(images, out_grads, in_signs, out_signs):
     samples = images.shape[0]
     in_part, out_part = project(images, out_grads, in_signs, out_signs)
     width_in = in_part.shape[1]
     both = jnp.concatenate([in_part, out_part], axis=1).reshape(samples, -1)
-    both = lax.psum_scatter(both, "chan", scatter_dimension=0, tiled=True)
+    both = ring_reduce_scatter(both, "chan")
     both = both.reshape(both.shape[0], -1, in_part.shape[2])
     in_sum = both[:, :width_in]
     out_sum = both[:, width_in:]

time: 326 us -> 374 us (1.15)
  between operations: 14.1 us -> 50.3 us
  starting transfers between devices: 0.08 us -> 21.4 us
  waiting for transfers between devices: 159 us -> 145 us
  local copies, waits for them, and re-layouts: 30.4 us -> 34.9 us
    reduce_scatter x1 -> x0, waiting for transfers between devices: 123 us -> none  [local(): both = lax.psum_scatter(both, 'chan', scatter_dimension=0, tiled=True)]
    ppermute x0 -> x14, waiting for transfers between devices: none -> 107 us  [the longest x7 56.9 us: ring_reduce_scatter(): fa = lax.ppermute(fa, axis, fwd) + take(pos - 1 - step + 2 * n, 0, h)]
    ppermute x0 -> x14, starting transfers between devices: none -> 21.4 us  [the longest x7 11.5 us: ring_reduce_scatter(): fa = lax.ppermute(fa, axis, fwd) + take(pos - 1 - step + 2 * n, 0, h)]
    unnamed x9 -> x7, local copies, waits for them, and re-layouts: 25.3 us -> 4.5 us
    concatenate x0 -> x1, local copies, waits for them, and re-layouts: none -> 9.06 us  [local(): both = jnp.concatenate([in_part, out_part], axis=1).reshape(samples, -1)]
    another operation x0 -> x1, local copies, waits for them, and re-layouts: none -> 8.93 us  [ring_reduce_scatter(): blocks = x.reshape(n, -1, x.shape[-1])]
    squeeze x0 -> x1, local copies, waits for them, and re-layouts: none -> 5.07 us  [take(): blk = lax.dynamic_index_in_dim(blocks, owner[q % n], 0, keepdims=False)]
  transfers between devices with their start and end apart: 2 -> 15, of which waited for: 2 -> 14; matrix products, arithmetic and copies ran while one was open for 0% -> 0% of each run, Pallas kernels for 0% -> 0%
where the time goes in v4:
time: 374 us; the launch traced here: 373 us
  waiting for transfers between devices  145 us (39%)
  Pallas kernels  105 us (28%)
  between operations  50.3 us (13%)
  local copies, waits for them, and re-layouts  34.9 us (9%)
  starting transfers between devices  21.4 us (6%)
  matrix products  11 us (3%)
  other arithmetic  5.12 us (1%)
    pallas_call x1, Pallas kernels, cholesky_upper(): pl.pallas_call(functools.partial(_chol_kernel, nb=nb, b=b), out_shape=jax...  105 us
    ppermute x7, waiting for transfers between devices, ring_reduce_scatter(): fa = lax.ppermute(fa, axis, fwd) + take(pos - 1 - step + 2 * n, 0, h)  56.9 us
    ppermute x7, waiting for transfers between devices, ring_reduce_scatter(): ba = lax.ppermute(ba, axis, bwd) + take(pos + 1 + step, h, x.shape[-1])  50.2 us
    all_gather x1, waiting for transfers between devices, local(): every = lax.all_gather(own, ('samp', 'chan'), axis=0, tiled=True)  38.3 us
    ppermute x7, starting transfers between devices, ring_reduce_scatter(): fa = lax.ppermute(fa, axis, fwd) + take(pos - 1 - step + 2 * n, 0, h)  11.5 us
    ppermute x7, starting transfers between devices, ring_reduce_scatter(): ba = lax.ppermute(ba, axis, bwd) + take(pos + 1 + step, h, x.shape[-1])  9.9 us
    concatenate x1, local copies, waits for them, and re-layouts, local(): both = jnp.concatenate([in_part, out_part], axis=1).reshape(samples, -1)  9.06 us
    another operation x1, local copies, waits for them, and re-layouts, ring_reduce_scatter(): blocks = x.reshape(n, -1, x.shape[-1])  8.93 us
  transfers between devices with their start and end apart: 15, of which 14 were waited for; matrix products, arithmetic and copies ran while one was open for 0% of the time, Pallas kernels for 0%

profile of v4, /device:TPU:0, one launch (start us, length us, event | category | flops | bytes accessed | tf_op | source)
XLA Modules:
  0.0 373.5 jit_solution(6319873031166899417)
XLA Ops:
  7.2 1.4 dynamic_slice.95
  17.9 1.9 fusion.11
  37.7 0.8 add_convert_fusion
  38.5 0.1 copy.16
  38.6 4.5 %copy.11 = bf16[128,32,784]{0,1,2:T(8,128)(2,1)S(1)} copy(bf16[128,32,784]{0,2,1:T(8,128)(2,1)} %param.6) | data formatting | bytes 12845056 | tf_op args[0]
  43.1 0.6 convolution_bitcast_fusion
  43.7 2.7 fusion.12
  46.4 3.4 pad_maximum_fusion
  49.8 9.1 %copy.14 = f32[128,64,196]{2,1,0:T(8,128)} copy(f32[128,64,196]{0,1,2:T(8,128)} %pad_maximum_fusion) | data formatting | bytes 12845056 | tf_op jit(solution)/shard_map/concatenate | solution.py:138
  58.9 8.9 %reshape_reshape.3 = f32[8,16,12544]{2,1,0:T(8,128)} reshape(f32[128,64,196]{2,1,0:T(8,128)} %copy.14) | data formatting | bytes 12845056 | tf_op jit(solution)/shard_map/reshape;reshape | solution.py:117
  76.8 5.1 %dynamic-slice_bitcast_fusion.7 = (f32[16,12544]{1,0:T(8,128)S(1)}, f32[16,12544]{1,0:T(8,128)S(1)}, f32[16,12544]{1,0:T(8,128)S(1)}, f32[16,12544]{1,0:T(8,128)...) fusion(f32[8,16,12544]{2,1,0:T(8,128)} %reshape_reshape.3, ...), kind=kLoop, calls=%fused_computation.13 | loop fusion | bytes 22478904 | tf_op jit(solution)/shard_map/jit(dynamic_index_in_dim)/squeeze | solution.py:123
  81.9 2.9 collective-permute-start.7
  84.8 9.5 %collective-permute-done.7 = f32[16,6272]{1,0:T(8,128)S(1)} collective-permute-done((f32[16,6272]{1,0:T(8,128)S(1)}, f32[16,6272]{1,0:T(8,128)S(1)}, u32[]{:S(2)}, u32[]{:S(2)}) %collective-permute-start.7) | collective-permute-done | bytes 401440 | tf_op jit(solution)/shard_map/ppermute | solution.py:130
  94.3 1.6 collective-permute-start.8
  95.9 8.9 %collective-permute-done.8 = f32[16,6272]{1,0:T(8,128)S(1)} collective-permute-done((f32[16,6272]{1,0:T(8,128)S(1)}, f32[16,6272]{1,0:T(8,128)S(1)}, u32[]{:S(2)}, u32[]{:S(2)}) %collective-permute-start.8) | collective-permute-done | bytes 401440 | tf_op jit(solution)/shard_map/ppermute | solution.py:130
  104.9 1.3 collective-permute-start.9
  106.2 8.3 %collective-permute-done.9 = f32[16,6272]{1,0:T(8,128)S(1)} collective-permute-done((f32[16,6272]{1,0:T(8,128)S(1)}, f32[16,6272]{1,0:T(8,128)S(1)}, u32[]{:S(2)}, u32[]{:S(2)}) %collective-permute-start.9) | collective-permute-done | bytes 401440 | tf_op jit(solution)/shard_map/ppermute | solution.py:130
  114.6 1.1 collective-permute-start.10
  115.7 8.3 %collective-permute-done.10 = f32[16,6272]{1,0:T(8,128)S(1)} collective-permute-done((f32[16,6272]{1,0:T(8,128)S(1)}, f32[16,6272]{1,0:T(8,128)S(1)}, u32[]{:S(2)}, u32[]{:S(2)}) %collective-permute-start.10) | collective-permute-done | bytes 401440 | tf_op jit(solution)/shard_map/ppermute | solution.py:130
  124.0 1.1 collective-permute-start.11
  125.2 8.6 %collective-permute-done.11 = f32[16,6272]{1,0:T(8,128)S(1)} collective-permute-done((f32[16,6272]{1,0:T(8,128)S(1)}, f32[16,6272]{1,0:T(8,128)S(1)}, u32[]{:S(2)}, u32[]{:S(2)}) %collective-permute-start.11) | collective-permute-done | bytes 401440 | tf_op jit(solution)/shard_map/ppermute | solution.py:130
  133.8 1.3 collective-permute-start.12
  135.2 6.6 %collective-permute-done.12 = f32[16,6272]{1,0:T(8,128)S(1)} collective-permute-done((f32[16,6272]{1,0:T(8,128)S(1)}, f32[16,6272]{1,0:T(8,128)S(1)}, u32[]{:S(2)}, u32[]{:S(2)}) %collective-permute-start.12) | collective-permute-done | bytes 401440 | tf_op jit(solution)/shard_map/ppermute | solution.py:130
  141.7 0.1 fusion.10
  141.8 1.5 collective-permute-start
  143.3 10.5 %collective-permute-done = f32[16,6272]{1,0:T(8,128)S(1)} collective-permute-done((f32[16,6272]{1,0:T(8,128)S(1)}, f32[16,6272]{1,0:T(8,128)S(1)}, u32[]{:S(2)}, u32[]{:S(2)}) %collective-permute-start) | collective-permute-done | bytes 401440 | tf_op jit(solution)/shard_map/ppermute | solution.py:129
  153.9 1.7 collective-permute-start.1
  155.6 9.7 %collective-permute-done.1 = f32[16,6272]{1,0:T(8,128)S(1)} collective-permute-done((f32[16,6272]{1,0:T(8,128)S(1)}, f32[16,6272]{1,0:T(8,128)S(1)}, u32[]{:S(2)}, u32[]{:S(2)}) %collective-permute-start.1) | collective-permute-done | bytes 401440 | tf_op jit(solution)/shard_map/ppermute | solution.py:129
  165.3 1.7 collective-permute-start.2
  167.0 8.9 %collective-permute-done.2 = f32[16,6272]{1,0:T(8,128)S(1)} collective-permute-done((f32[16,6272]{1,0:T(8,128)S(1)}, f32[16,6272]{1,0:T(8,128)S(1)}, u32[]{:S(2)}, u32[]{:S(2)}) %collective-permute-start.2) | collective-permute-done | bytes 401440 | tf_op jit(solution)/shard_map/ppermute | solution.py:129
  175.9 1.6 collective-permute-start.3
  177.5 8.0 %collective-permute-done.3 = f32[16,6272]{1,0:T(8,128)S(1)} collective-permute-done((f32[16,6272]{1,0:T(8,128)S(1)}, f32[16,6272]{1,0:T(8,128)S(1)}, u32[]{:S(2)}, u32[]{:S(2)}) %collective-permute-start.3) | collective-permute-done | bytes 401440 | tf_op jit(solution)/shard_map/ppermute | solution.py:129
  185.6 1.6 collective-permute-start.4
  187.2 7.6 %collective-permute-done.4 = f32[16,6272]{1,0:T(8,128)S(1)} collective-permute-done((f32[16,6272]{1,0:T(8,128)S(1)}, f32[16,6272]{1,0:T(8,128)S(1)}, u32[]{:S(2)}, u32[]{:S(2)}) %collective-permute-start.4) | collective-permute-done | bytes 401440 | tf_op jit(solution)/shard_map/ppermute | solution.py:129
  194.8 1.6 collective-permute-start.5
  196.4 0.5 collective-permute-start.13
  196.9 5.9 %collective-permute-done.5 = f32[16,6272]{1,0:T(8,128)S(1)} collective-permute-done((f32[16,6272]{1,0:T(8,128)S(1)}, f32[16,6272]{1,0:T(8,128)S(1)}, u32[]{:S(2)}, u32[]{:S(2)}) %collective-permute-start.5) | collective-permute-done | bytes 401440 | tf_op jit(solution)/shard_map/ppermute | solution.py:129
  202.9 1.7 collective-permute-start.6
  204.6 6.4 %collective-permute-done.6 = f32[16,6272]{1,0:T(8,128)S(1)} collective-permute-done((f32[16,6272]{1,0:T(8,128)S(1)}, f32[16,6272]{1,0:T(8,128)S(1)}, u32[]{:S(2)}, u32[]{:S(2)}) %collective-permute-start.6) | collective-permute-done | bytes 401440 | tf_op jit(solution)/shard_map/ppermute | solution.py:129
  211.0 0.1 slice_add_fusion.7
  211.2 1.5 reshape.56
  212.7 0.7 convolution_multiply_fusion
  213.3 0.8 reshape.57
  214.1 0.8 broadcast_in_dim_reshape.3
  214.9 38.3 %all-gather.2.cloned.1.call-done = f32[256,1024]{1,0:T(8,128)} async-done(((f32[16,1024]{1,0:T(8,128)}), f32[256,1024]{1,0:T(8,128)}) %all-gather.2.cloned.1.call-update) | async-done | bytes 1048592 | tf_op jit(solution)/shard_map/all_gather | solution.py:144
  253.2 7.1 %convert_add_fusion = f32[1024,1024]{1,0:T(8,128)} fusion(f32[256,1024]{1,0:T(8,128)} %all-gather.2.cloned.1.call-done), kind=kOutput, calls=%fused_computation.1 | convolution fusion | flops 3225419776 | bytes 5242880 | tf_op jit(solution)/shard_map/nk,nm->km/dot_general | solution.py:148
  260.3 105.5 %shard_map.77 = f32[8,128,1024]{2,1,0:T(8,128)S(1)} custom-call(f32[8,128,1024]{2,1,0:T(8,128)} %bitcast.72), custom_call_target="tpu_custom_call" | custom-call | tf_op jit(solution)/shard_map/pallas_call | solution.py:63
  365.8 0.8 constant_dynamic-slice_fusion
  (22 shorter events, 0.8 us)
Async XLA Ops:
  7.2 35.9 %copy-start = (bf16[128,32,196]{0,1,2:T(8,128)(2,1)S(1)}, bf16[128,32,196]{0,1,2:T(8,128)(2,1)}, u32[]{:S(2)}) copy-start(bf16[128,32,196]{0,1,2:T(8,128)(2,1)} %param.7) | copy-start | bytes 4816900
  7.2 246.0 %all-gather.2.cloned.1.call-start = ((), (), s32[]{:S(2)}) async-start(), calls=%async_computation | async-start | bytes 1114112 | tf_op jit(solution)/shard_map/all_gather | solution.py:144
  38.6 4.5 %copy-start.2 = (s32[32,32]{1,0:T(8,128)S(1)}, s32[32,32]{1,0:T(8,128)}, u32[]{:S(2)}) copy-start(s32[32,32]{1,0:T(8,128)} %param.9) | copy-start | bytes 12292
  81.9 12.4 %collective-permute-start.7 = (f32[16,6272]{1,0:T(8,128)S(1)}, f32[16,6272]{1,0:T(8,128)S(1)}, u32[]{:S(2)}, u32[]{:S(2)}) collective-permute-start(f32[16,6272]{1,0:T(8,128)S(1)} %slice.80), channel_id=1, source_target_pairs={{4,0},{8,4},{12,8},{14,12},{10,14},{6,10},{2,6},{0,2},{5,1},{9,5},... | collective-permute-start | bytes 1204232 | tf_op jit(solution)/shard_map/ppermute | solution.py:130
  94.3 10.5 %collective-permute-start.8 = (f32[16,6272]{1,0:T(8,128)S(1)}, f32[16,6272]{1,0:T(8,128)S(1)}, u32[]{:S(2)}, u32[]{:S(2)}) collective-permute-start(f32[16,6272]{1,0:T(8,128)S(1)} %slice_add_fusion.6), channel_id=1, source_target_pairs={{4,0},{8,4},{12,8},{14,12},{10,14},{6,10},{2,6},{0,2},{5,1},{9,5},... | collective-permute-start | bytes 1204232 | tf_op jit(solution)/shard_map/ppermute | solution.py:130
  104.9 9.6 %collective-permute-start.9 = (f32[16,6272]{1,0:T(8,128)S(1)}, f32[16,6272]{1,0:T(8,128)S(1)}, u32[]{:S(2)}, u32[]{:S(2)}) collective-permute-start(f32[16,6272]{1,0:T(8,128)S(1)} %slice_add_fusion.5), channel_id=1, source_target_pairs={{4,0},{8,4},{12,8},{14,12},{10,14},{6,10},{2,6},{0,2},{5,1},{9,5},... | collective-permute-start | bytes 1204232 | tf_op jit(solution)/shard_map/ppermute | solution.py:130
  114.6 9.4 %collective-permute-start.10 = (f32[16,6272]{1,0:T(8,128)S(1)}, f32[16,6272]{1,0:T(8,128)S(1)}, u32[]{:S(2)}, u32[]{:S(2)}) collective-permute-start(f32[16,6272]{1,0:T(8,128)S(1)} %slice_add_fusion.4), channel_id=1, source_target_pairs={{4,0},{8,4},{12,8},{14,12},{10,14},{6,10},{2,6},{0,2},{5,1},{9,5},... | collective-permute-start | bytes 1204232 | tf_op jit(solution)/shard_map/ppermute | solution.py:130
  124.0 9.7 %collective-permute-start.11 = (f32[16,6272]{1,0:T(8,128)S(1)}, f32[16,6272]{1,0:T(8,128)S(1)}, u32[]{:S(2)}, u32[]{:S(2)}) collective-permute-start(f32[16,6272]{1,0:T(8,128)S(1)} %slice_add_fusion.3), channel_id=1, source_target_pairs={{4,0},{8,4},{12,8},{14,12},{10,14},{6,10},{2,6},{0,2},{5,1},{9,5},... | collective-permute-start | bytes 1204232 | tf_op jit(solution)/shard_map/ppermute | solution.py:130
  133.8 7.9 %collective-permute-start.12 = (f32[16,6272]{1,0:T(8,128)S(1)}, f32[16,6272]{1,0:T(8,128)S(1)}, u32[]{:S(2)}, u32[]{:S(2)}) collective-permute-start(f32[16,6272]{1,0:T(8,128)S(1)} %slice_add_fusion.2), channel_id=1, source_target_pairs={{4,0},{8,4},{12,8},{14,12},{10,14},{6,10},{2,6},{0,2},{5,1},{9,5},... | collective-permute-start | bytes 1204232 | tf_op jit(solution)/shard_map/ppermute | solution.py:130
  141.8 12.0 %collective-permute-start = (f32[16,6272]{1,0:T(8,128)S(1)}, f32[16,6272]{1,0:T(8,128)S(1)}, u32[]{:S(2)}, u32[]{:S(2)}) collective-permute-start(f32[16,6272]{1,0:T(8,128)S(1)} %get-tuple-element.18), channel_id=1, source_target_pairs={{0,4},{4,8},{8,12},{12,14},{14,10},{10,6},{6,2},{2,0},{1,5},{5,9},... | collective-permute-start | bytes 1204232 | tf_op jit(solution)/shard_map/ppermute | solution.py:129
  153.9 11.4 %collective-permute-start.1 = (f32[16,6272]{1,0:T(8,128)S(1)}, f32[16,6272]{1,0:T(8,128)S(1)}, u32[]{:S(2)}, u32[]{:S(2)}) collective-permute-start(f32[16,6272]{1,0:T(8,128)S(1)} %slice_add_fusion.13), channel_id=1, source_target_pairs={{0,4},{4,8},{8,12},{12,14},{14,10},{10,6},{6,2},{2,0},{1,5},{5,9},... | collective-permute-start | bytes 1204232 | tf_op jit(solution)/shard_map/ppermute | solution.py:129
  165.3 10.5 %collective-permute-start.2 = (f32[16,6272]{1,0:T(8,128)S(1)}, f32[16,6272]{1,0:T(8,128)S(1)}, u32[]{:S(2)}, u32[]{:S(2)}) collective-permute-start(f32[16,6272]{1,0:T(8,128)S(1)} %slice_add_fusion.12), channel_id=1, source_target_pairs={{0,4},{4,8},{8,12},{12,14},{14,10},{10,6},{6,2},{2,0},{1,5},{5,9},... | collective-permute-start | bytes 1204232 | tf_op jit(solution)/shard_map/ppermute | solution.py:129
  175.9 9.6 %collective-permute-start.3 = (f32[16,6272]{1,0:T(8,128)S(1)}, f32[16,6272]{1,0:T(8,128)S(1)}, u32[]{:S(2)}, u32[]{:S(2)}) collective-permute-start(f32[16,6272]{1,0:T(8,128)S(1)} %slice_add_fusion.11), channel_id=1, source_target_pairs={{0,4},{4,8},{8,12},{12,14},{14,10},{10,6},{6,2},{2,0},{1,5},{5,9},... | collective-permute-start | bytes 1204232 | tf_op jit(solution)/shard_map/ppermute | solution.py:129
  185.6 9.2 %collective-permute-start.4 = (f32[16,6272]{1,0:T(8,128)S(1)}, f32[16,6272]{1,0:T(8,128)S(1)}, u32[]{:S(2)}, u32[]{:S(2)}) collective-permute-start(f32[16,6272]{1,0:T(8,128)S(1)} %slice_add_fusion.10), channel_id=1, source_target_pairs={{0,4},{4,8},{8,12},{12,14},{14,10},{10,6},{6,2},{2,0},{1,5},{5,9},... | collective-permute-start | bytes 1204232 | tf_op jit(solution)/shard_map/ppermute | solution.py:129
  194.8 8.0 %collective-permute-start.5 = (f32[16,6272]{1,0:T(8,128)S(1)}, f32[16,6272]{1,0:T(8,128)S(1)}, u32[]{:S(2)}, u32[]{:S(2)}) collective-permute-start(f32[16,6272]{1,0:T(8,128)S(1)} %slice_add_fusion.9), channel_id=1, source_target_pairs={{0,4},{4,8},{8,12},{12,14},{14,10},{10,6},{6,2},{2,0},{1,5},{5,9},... | collective-permute-start | bytes 1204232 | tf_op jit(solution)/shard_map/ppermute | solution.py:129
  196.4 8.2 %collective-permute-start.13 = (f32[16,6272]{1,0:T(8,128)S(1)}, f32[16,6272]{1,0:T(8,128)S(1)}, u32[]{:S(2)}, u32[]{:S(2)}) collective-permute-start(f32[16,6272]{1,0:T(8,128)S(1)} %get-tuple-element.19), channel_id=1, source_target_pairs={{4,0},{8,4},{12,8},{14,12},{10,14},{6,10},{2,6},{0,2},{5,1},{9,5},... | collective-permute-start | bytes 1204232 | tf_op jit(solution)/shard_map/ppermute | solution.py:130
  202.9 8.1 %collective-permute-start.6 = (f32[16,6272]{1,0:T(8,128)S(1)}, f32[16,6272]{1,0:T(8,128)S(1)}, u32[]{:S(2)}, u32[]{:S(2)}) collective-permute-start(f32[16,6272]{1,0:T(8,128)S(1)} %slice_add_fusion.8), channel_id=1, source_target_pairs={{0,4},{4,8},{8,12},{12,14},{14,10},{10,6},{6,2},{2,0},{1,5},{5,9},... | collective-permute-start | bytes 1204232 | tf_op jit(solution)/shard_map/ppermute | solution.py:129
  260.3 106.3 %copy-start.1 = (bf16[128,32,196]{0,1,2:T(8,128)(2,1)S(1)}, bf16[128,32,196]{0,1,2:T(8,128)(2,1)}, u32[]{:S(2)}) copy-start(bf16[128,32,196]{0,1,2:T(8,128)(2,1)} %param.7) | copy-start | bytes 4816900
Sparse Core Ops, SparseCore 0:
  214.2 38.9 all-gather.1

commit v5 on v3

--- a/solution.py
+++ b/solution.py
@@ -103,12 +103,48 @@
     return outer.reshape(outer.shape[0], -1)
 
 
+def _ring_order(n):
+    if n % 2:
+        return list(range(n))
+    return list(range(0, n, 2)) + list(range(n - 1, 0, -2))
+
+
+def ring_reduce_scatter(x, axis, pair):
+    n = lax.axis_size(axis)
+    order = _ring_order(n)
+    me = lax.axis_index(pair)
+    pos = jnp.asarray([order.index(c) for c in range(n)], jnp.int32)[lax.axis_index(axis)]
+    owner = jnp.asarray(order, jnp.int32)
+    h = x.shape[-1] // 2
+    swap = [(0, 1), (1, 0)]
+    keep = jnp.where(me == 0, x[:, :h], x[:, h:])
+    give = jnp.where(me == 0, x[:, h:], x[:, :h])
+    both = jnp.stack([keep, lax.ppermute(give, pair, swap)])
+    blocks = both.reshape(2, n, -1, h)
+    ring = []
+    for q in range(n):
+        ring.append((order[q] * 2, order[(q + 1) % n] * 2))
+        ring.append((order[(q + 1) % n] * 2 + 1, order[q] * 2 + 1))
+    sign = 1 - 2 * me
+
+    def take(step):
+        q = (pos - sign * (1 + step) + 2 * n) % n
+        return lax.dynamic_index_in_dim(blocks, owner[q], 1, keepdims=False)
+
+    acc = take(0)
+    for step in range(1, n):
+        acc = lax.ppermute(acc, (axis, pair), ring) + take(step)
+    back = lax.ppermute(acc[1], pair, swap)
+    return jnp.where(me == 0, jnp.concatenate([acc[0], back], axis=-1),
+                     jnp.concatenate([back, acc[0]], axis=-1))
+
+
 def local(images, out_grads, in_signs, out_signs):
     samples = images.shape[0]
     in_part, out_part = project(images, out_grads, in_signs, out_signs)
     width_in = in_part.shape[1]
     both = jnp.concatenate([in_part, out_part], axis=1).reshape(samples, -1)
-    both = lax.psum_scatter(both, "chan", scatter_dimension=0, tiled=True)
+    both = ring_reduce_scatter(both, "chan", "samp")
     both = both.reshape(both.shape[0], -1, in_part.shape[2])
     in_sum = both[:, :width_in]
     out_sum = both[:, width_in:]

time: 326 us -> 317 us (0.972)
  waiting for transfers between devices: 159 us -> 97.7 us
  between operations: 14.1 us -> 34.5 us
  starting transfers between devices: 0.08 us -> 16.1 us
  other arithmetic: 3.45 us -> 18.4 us
    reduce_scatter x1 -> x0, waiting for transfers between devices: 123 us -> none  [local(): both = lax.psum_scatter(both, 'chan', scatter_dimension=0, tiled=True)]
    ppermute x0 -> x9, waiting for transfers between devices: none -> 58.6 us  [the longest x7 57.6 us: ring_reduce_scatter(): acc = lax.ppermute(acc, (axis, pair), ring) + take(step)]
    unnamed x9 -> x13, local copies, waits for them, and re-layouts: 25.3 us -> 4.51 us
    ppermute x0 -> x9, starting transfers between devices: none -> 16.1 us  [the longest x7 15.5 us: ring_reduce_scatter(): acc = lax.ppermute(acc, (axis, pair), ring) + take(step)]
    add x0 -> x7, other arithmetic: none -> 8.64 us  [ring_reduce_scatter(): acc = lax.ppermute(acc, (axis, pair), ring) + take(step)]
    concatenate x0 -> x3, local copies, waits for them, and re-layouts: none -> 7.92 us  [the longest x1 6.44 us: local(): both = jnp.concatenate([in_part, out_part], axis=1).reshape(samples, -1)]
    select_n x0 -> x2, other arithmetic: none -> 6.04 us  [the longest x1 5.93 us: ring_reduce_scatter(): give = jnp.where(me == 0, x[:, h:], x[:, :h])]
    ppermute x0 -> x1, local copies, waits for them, and re-layouts: none -> 5.43 us  [ring_reduce_scatter(): both = jnp.stack([keep, lax.ppermute(give, pair, swap)])]
  transfers between devices with their start and end apart: 2 -> 10, of which waited for: 2 -> 9; matrix products, arithmetic and copies ran while one was open for 0% -> 2% of each run, Pallas kernels for 0% -> 0%
where the time goes in v5:
time: 317 us; the launch traced here: 316 us
  Pallas kernels  105 us (33%)
  waiting for transfers between devices  97.7 us (31%)
  between operations  34.5 us (11%)
  local copies, waits for them, and re-layouts  32.3 us (10%)
  other arithmetic  18.4 us (6%)
  starting transfers between devices  16.1 us (5%)
  matrix products  11 us (3%)
    pallas_call x1, Pallas kernels, cholesky_upper(): pl.pallas_call(functools.partial(_chol_kernel, nb=nb, b=b), out_shape=jax...  105 us
    ppermute x7, waiting for transfers between devices, ring_reduce_scatter(): acc = lax.ppermute(acc, (axis, pair), ring) + take(step)  57.6 us
    all_gather x1, waiting for transfers between devices, local(): every = lax.all_gather(own, ('samp', 'chan'), axis=0, tiled=True)  39.1 us
    ppermute x7, starting transfers between devices, ring_reduce_scatter(): acc = lax.ppermute(acc, (axis, pair), ring) + take(step)  15.5 us
    add x7, other arithmetic, ring_reduce_scatter(): acc = lax.ppermute(acc, (axis, pair), ring) + take(step)  8.64 us
    reshape x1, local copies, waits for them, and re-layouts, local(): both = jnp.concatenate([in_part, out_part], axis=1).reshape(samples, -1)  7.23 us
    dot_general x1, matrix products, local(): jnp.einsum('nk,nm->km', every, every, precision=lax.Precision.HIGHEST)  7.1 us
    concatenate x1, local copies, waits for them, and re-layouts, local(): both = jnp.concatenate([in_part, out_part], axis=1).reshape(samples, -1)  6.44 us
  transfers between devices with their start and end apart: 10, of which 9 were waited for; matrix products, arithmetic and copies ran while one was open for 2% of the time, Pallas kernels for 0%

profile of v5, /device:TPU:0, one launch (start us, length us, event | category | flops | bytes accessed | tf_op | source)
XLA Modules:
  0.0 315.6 jit_solution(2742017878330212922)
XLA Ops:
  7.2 0.9 add_convert_fusion
  8.2 0.1 copy.30
  8.3 4.5 %copy.23 = bf16[128,32,784]{0,1,2:T(8,128)(2,1)S(1)} copy(bf16[128,32,784]{0,2,1:T(8,128)(2,1)} %param.6) | data formatting | bytes 12845056 | tf_op args[0]
  12.8 0.6 convolution_bitcast_fusion
  13.4 2.7 fusion.35
  16.1 0.9 pad_maximum_fusion
  16.9 6.4 %copy.26 = f32[128,64,196]{0,2,1:T(8,128)} copy(f32[128,64,196]{0,1,2:T(8,128)S(1)} %pad_maximum_fusion) | data formatting | bytes 12845056 | tf_op jit(solution)/shard_map/concatenate | solution.py:146
  23.4 7.2 %reshape.40 = f32[128,12544]{0,1:T(8,128)} reshape(f32[128,64,196]{0,2,1:T(8,128)} %copy.26) | data formatting | bytes 12845056 | tf_op jit(solution)/shard_map/reshape | solution.py:146
  30.6 5.9 %slice_select_fusion = (f32[128,6272]{0,1:T(8,128)}, f32[128,6272]{0,1:T(8,128)}) fusion(f32[128,12544]{0,1:T(8,128)} %reshape.40, pred[]{:T(512)S(6)} %eq.17), kind=kLoop, calls=%fused_computation.19 | loop fusion | flops 1605632 | bytes 12845057 | tf_op jit(solution)/shard_map/jit(_where)/select_n | solution.py:121
  36.6 0.5 collective-permute-start
  37.0 0.6 dynamic_slice.55
  42.9 0.7 fusion.34
  44.8 3.4 %copy.27 = f32[128,6272]{1,0:T(8,128)S(1)} copy(f32[128,6272]{0,1:T(8,128)} %get-tuple-element.3) | data formatting | bytes 6422528 | tf_op jit(solution)/shard_map/jit(_where)/select_n | solution.py:120
  48.7 5.4 %copy.28 = f32[128,6272]{1,0:T(8,128)} copy(f32[128,6272]{0,1:T(8,128)} %collective-permute-done) | data formatting | bytes 6422528 | tf_op jit(solution)/shard_map/ppermute | solution.py:122
  54.2 1.9 fusion.4
  56.1 2.6 collective-permute-start.1
  60.6 8.5 %collective-permute-done.1 = f32[2,16,6272]{2,1,0:T(8,128)} collective-permute-done((f32[2,16,6272]{2,1,0:T(8,128)}, f32[2,16,6272]{2,1,0:T(8,128)}, u32[]{:S(2)}, u32[]{:S(2)}) %collective-permute-start.1) | collective-permute-done | bytes 802848 | tf_op jit(solution)/shard_map/ppermute | solution.py:136
  69.1 1.4 fusion.7
  70.5 2.1 collective-permute-start.2
  74.4 8.4 %collective-permute-done.2 = f32[2,16,6272]{2,1,0:T(8,128)S(1)} collective-permute-done((f32[2,16,6272]{2,1,0:T(8,128)S(1)}, f32[2,16,6272]{2,1,0:T(8,128)S(1)}, u32[]{:S(2)}, u32[]{:S(2)}) %collective-permute-start.2) | collective-permute-done | bytes 802848 | tf_op jit(solution)/shard_map/ppermute | solution.py:136
  82.7 1.2 fusion.10
  84.0 2.1 collective-permute-start.3
  88.2 8.0 %collective-permute-done.3 = f32[2,16,6272]{2,1,0:T(8,128)S(1)} collective-permute-done((f32[2,16,6272]{2,1,0:T(8,128)S(1)}, f32[2,16,6272]{2,1,0:T(8,128)S(1)}, u32[]{:S(2)}, u32[]{:S(2)}) %collective-permute-start.3) | collective-permute-done | bytes 802848 | tf_op jit(solution)/shard_map/ppermute | solution.py:136
  96.2 1.2 fusion.13
  97.4 2.1 collective-permute-start.4
  101.2 8.4 %collective-permute-done.4 = f32[2,16,6272]{2,1,0:T(8,128)S(1)} collective-permute-done((f32[2,16,6272]{2,1,0:T(8,128)S(1)}, f32[2,16,6272]{2,1,0:T(8,128)S(1)}, u32[]{:S(2)}, u32[]{:S(2)}) %collective-permute-start.4) | collective-permute-done | bytes 802848 | tf_op jit(solution)/shard_map/ppermute | solution.py:136
  109.6 1.2 fusion.16
  110.8 2.1 collective-permute-start.5
  114.9 8.1 %collective-permute-done.5 = f32[2,16,6272]{2,1,0:T(8,128)S(1)} collective-permute-done((f32[2,16,6272]{2,1,0:T(8,128)S(1)}, f32[2,16,6272]{2,1,0:T(8,128)S(1)}, u32[]{:S(2)}, u32[]{:S(2)}) %collective-permute-start.5) | collective-permute-done | bytes 802848 | tf_op jit(solution)/shard_map/ppermute | solution.py:136
  123.0 1.2 fusion.19
  124.2 2.1 collective-permute-start.6
  128.4 8.1 %collective-permute-done.6 = f32[2,16,6272]{2,1,0:T(8,128)S(1)} collective-permute-done((f32[2,16,6272]{2,1,0:T(8,128)S(1)}, f32[2,16,6272]{2,1,0:T(8,128)S(1)}, u32[]{:S(2)}, u32[]{:S(2)}) %collective-permute-start.6) | collective-permute-done | bytes 802848 | tf_op jit(solution)/shard_map/ppermute | solution.py:136
  136.4 1.2 fusion.22
  137.6 2.3 collective-permute-start.7
  141.9 8.1 %collective-permute-done.7 = f32[2,16,6272]{2,1,0:T(8,128)S(1)} collective-permute-done((f32[2,16,6272]{2,1,0:T(8,128)S(1)}, f32[2,16,6272]{2,1,0:T(8,128)S(1)}, u32[]{:S(2)}, u32[]{:S(2)}) %collective-permute-start.7) | collective-permute-done | bytes 802848 | tf_op jit(solution)/shard_map/ppermute | solution.py:136
  150.0 1.2 fusion.2
  151.3 0.1 collective-permute-start.8
  151.4 0.7 concatenate.17
  152.1 1.0 collective-permute-done.8
  153.1 0.7 concatenate.18
  153.8 0.1 maximum_select_fusion
  154.0 0.7 convolution_multiply_fusion
  154.6 0.8 reshape.41
  155.4 0.8 broadcast_in_dim_reshape.3
  156.2 39.1 %all-gather.2.cloned.1.call-done = f32[256,1024]{1,0:T(8,128)} async-done(((f32[16,1024]{1,0:T(8,128)}), f32[256,1024]{1,0:T(8,128)}) %all-gather.2.cloned.1.call-update) | async-done | bytes 1048592 | tf_op jit(solution)/shard_map/all_gather | solution.py:152
  195.3 7.1 %convert_add_fusion = f32[1024,1024]{1,0:T(8,128)} fusion(f32[256,1024]{1,0:T(8,128)} %all-gather.2.cloned.1.call-done), kind=kOutput, calls=%fused_computation.17 | convolution fusion | flops 3225419776 | bytes 5242880 | tf_op jit(solution)/shard_map/nk,nm->km/dot_general | solution.py:156
  202.4 105.5 %shard_map.77 = f32[8,128,1024]{2,1,0:T(8,128)S(1)} custom-call(f32[8,128,1024]{2,1,0:T(8,128)} %bitcast.77), custom_call_target="tpu_custom_call" | custom-call | tf_op jit(solution)/shard_map/pallas_call | solution.py:63
  307.9 0.9 constant_dynamic-slice_fusion
  (16 shorter events, 0.1 us)
Async XLA Ops:
  7.2 5.6 %copy-start = (bf16[128,32,196]{0,1,2:T(8,128)(2,1)S(1)}, bf16[128,32,196]{0,1,2:T(8,128)(2,1)}, u32[]{:S(2)}) copy-start(bf16[128,32,196]{0,1,2:T(8,128)(2,1)} %param.7) | copy-start | bytes 4816900
  7.2 188.1 %all-gather.2.cloned.1.call-start = ((), (), s32[]{:S(2)}) async-start(), calls=%async_computation | async-start | bytes 1114112 | tf_op jit(solution)/shard_map/all_gather | solution.py:152
  8.3 4.5 %copy-start.4 = (s32[32,32]{1,0:T(8,128)S(1)}, s32[32,32]{1,0:T(8,128)}, u32[]{:S(2)}) copy-start(s32[32,32]{1,0:T(8,128)} %param.9) | copy-start | bytes 12292
  30.6 6.4 %copy-start.5 = (s32[8]{0:T(128)S(1)}, s32[8]{0:T(128)}, u32[]{:S(2)}) copy-start(s32[8]{0:T(128)} %constant.110.clone) | copy-start | bytes 100
  30.6 12.3 %copy-start.3 = (s32[8]{0:T(128)S(1)}, s32[8]{0:T(128)}, u32[]{:S(2)}) copy-start(s32[8]{0:T(128)} %constant.111.clone) | copy-start | bytes 100
  36.6 12.2 %collective-permute-start = (f32[128,6272]{0,1:T(8,128)}, f32[128,6272]{0,1:T(8,128)}, u32[]{:S(2)}, u32[]{:S(2)}) collective-permute-start(f32[128,6272]{0,1:T(8,128)} %get-tuple-element.2), channel_id=1, source_target_pairs={{0,1},{1,0},{2,3},{3,2},{4,5},{5,4},{6,7},{7,6},{8,9},{9,8},{10,11... | collective-permute-start | bytes 9633800 | tf_op jit(solution)/shard_map/ppermute | solution.py:122
  48.2 8.0 %copy-start.2 = (f32[128,6272]{1,0:T(8,128)}, f32[128,6272]{1,0:T(8,128)S(1)}, u32[]{:S(2)}) copy-start(f32[128,6272]{1,0:T(8,128)S(1)} %copy.27) | copy-start | bytes 9633796
  56.1 13.0 %collective-permute-start.1 = (f32[2,16,6272]{2,1,0:T(8,128)}, f32[2,16,6272]{2,1,0:T(8,128)}, u32[]{:S(2)}, u32[]{:S(2)}) collective-permute-start(f32[2,16,6272]{2,1,0:T(8,128)} %fusion.4), channel_id=1, source_target_pairs={{0,4},{5,1},{4,8},{9,5},{8,12},{13,9},{12,14},{15,13},{14,10},{11,... | collective-permute-start | bytes 2408456 | tf_op jit(solution)/shard_map/ppermute | solution.py:136
  70.5 12.2 %collective-permute-start.2 = (f32[2,16,6272]{2,1,0:T(8,128)S(1)}, f32[2,16,6272]{2,1,0:T(8,128)S(1)}, u32[]{:S(2)}, u32[]{:S(2)}) collective-permute-start(f32[2,16,6272]{2,1,0:T(8,128)S(1)} %fusion.7), channel_id=1, source_target_pairs={{0,4},{5,1},{4,8},{9,5},{8,12},{13,9},{12,14},{15,13},{14,10},{11,... | collective-permute-start | bytes 2408456 | tf_op jit(solution)/shard_map/ppermute | solution.py:136
  84.0 12.2 %collective-permute-start.3 = (f32[2,16,6272]{2,1,0:T(8,128)S(1)}, f32[2,16,6272]{2,1,0:T(8,128)S(1)}, u32[]{:S(2)}, u32[]{:S(2)}) collective-permute-start(f32[2,16,6272]{2,1,0:T(8,128)S(1)} %fusion.10), channel_id=1, source_target_pairs={{0,4},{5,1},{4,8},{9,5},{8,12},{13,9},{12,14},{15,13},{14,10},{11,... | collective-permute-start | bytes 2408456 | tf_op jit(solution)/shard_map/ppermute | solution.py:136
  97.4 12.2 %collective-permute-start.4 = (f32[2,16,6272]{2,1,0:T(8,128)S(1)}, f32[2,16,6272]{2,1,0:T(8,128)S(1)}, u32[]{:S(2)}, u32[]{:S(2)}) collective-permute-start(f32[2,16,6272]{2,1,0:T(8,128)S(1)} %fusion.13), channel_id=1, source_target_pairs={{0,4},{5,1},{4,8},{9,5},{8,12},{13,9},{12,14},{15,13},{14,10},{11,... | collective-permute-start | bytes 2408456 | tf_op jit(solution)/shard_map/ppermute | solution.py:136
  110.8 12.2 %collective-permute-start.5 = (f32[2,16,6272]{2,1,0:T(8,128)S(1)}, f32[2,16,6272]{2,1,0:T(8,128)S(1)}, u32[]{:S(2)}, u32[]{:S(2)}) collective-permute-start(f32[2,16,6272]{2,1,0:T(8,128)S(1)} %fusion.16), channel_id=1, source_target_pairs={{0,4},{5,1},{4,8},{9,5},{8,12},{13,9},{12,14},{15,13},{14,10},{11,... | collective-permute-start | bytes 2408456 | tf_op jit(solution)/shard_map/ppermute | solution.py:136
  124.2 12.2 %collective-permute-start.6 = (f32[2,16,6272]{2,1,0:T(8,128)S(1)}, f32[2,16,6272]{2,1,0:T(8,128)S(1)}, u32[]{:S(2)}, u32[]{:S(2)}) collective-permute-start(f32[2,16,6272]{2,1,0:T(8,128)S(1)} %fusion.19), channel_id=1, source_target_pairs={{0,4},{5,1},{4,8},{9,5},{8,12},{13,9},{12,14},{15,13},{14,10},{11,... | collective-permute-start | bytes 2408456 | tf_op jit(solution)/shard_map/ppermute | solution.py:136
  137.6 12.4 %collective-permute-start.7 = (f32[2,16,6272]{2,1,0:T(8,128)S(1)}, f32[2,16,6272]{2,1,0:T(8,128)S(1)}, u32[]{:S(2)}, u32[]{:S(2)}) collective-permute-start(f32[2,16,6272]{2,1,0:T(8,128)S(1)} %fusion.22), channel_id=1, source_target_pairs={{0,4},{5,1},{4,8},{9,5},{8,12},{13,9},{12,14},{15,13},{14,10},{11,... | collective-permute-start | bytes 2408456 | tf_op jit(solution)/shard_map/ppermute | solution.py:136
  151.3 1.8 collective-permute-start.8
  202.4 106.3 %copy-start.1 = (bf16[128,32,196]{0,1,2:T(8,128)(2,1)S(1)}, bf16[128,32,196]{0,1,2:T(8,128)(2,1)}, u32[]{:S(2)}) copy-start(bf16[128,32,196]{0,1,2:T(8,128)(2,1)} %param.7) | copy-start | bytes 4816900
Sparse Core Ops, SparseCore 0:
  155.5 39.7 all-gather.1

commit v6 on v5

--- a/solution.py
+++ b/solution.py
@@ -115,12 +115,7 @@
     me = lax.axis_index(pair)
     pos = jnp.asarray([order.index(c) for c in range(n)], jnp.int32)[lax.axis_index(axis)]
     owner = jnp.asarray(order, jnp.int32)
-    h = x.shape[-1] // 2
-    swap = [(0, 1), (1, 0)]
-    keep = jnp.where(me == 0, x[:, :h], x[:, h:])
-    give = jnp.where(me == 0, x[:, h:], x[:, :h])
-    both = jnp.stack([keep, lax.ppermute(give, pair, swap)])
-    blocks = both.reshape(2, n, -1, h)
+    blocks = x.reshape(n, -1, x.shape[-1])
     ring = []
     for q in range(n):
         ring.append((order[q] * 2, order[(q + 1) % n] * 2))
@@ -129,14 +124,12 @@
 
     def take(step):
         q = (pos - sign * (1 + step) + 2 * n) % n
-        return lax.dynamic_index_in_dim(blocks, owner[q], 1, keepdims=False)
+        return lax.dynamic_index_in_dim(blocks, owner[q], 0, keepdims=False)
 
     acc = take(0)
     for step in range(1, n):
         acc = lax.ppermute(acc, (axis, pair), ring) + take(step)
-    back = lax.ppermute(acc[1], pair, swap)
-    return jnp.where(me == 0, jnp.concatenate([acc[0], back], axis=-1),
-                     jnp.concatenate([back, acc[0]], axis=-1))
+    return acc
 
 
 def local(images, out_grads, in_signs, out_signs):

time: 317 us -> 312 us (0.984)
  other arithmetic: 18.4 us -> 12.3 us
    another operation x0 -> x1, local copies, waits for them, and re-layouts: none -> 8.92 us  [ring_reduce_scatter(): blocks = x.reshape(n, -1, x.shape[-1])]
    select_n x2 -> x0, other arithmetic: 6.04 us -> none  [the longest x1 5.93 us: ring_reduce_scatter(): give = jnp.where(me == 0, x[:, h:], x[:, :h])]
    reshape x1, local copies, waits for them, and re-layouts: 7.23 us -> 1.51 us  [local(): both = both.reshape(both.shape[0], -1, in_part.shape[2])]
    ppermute x1 -> x0, local copies, waits for them, and re-layouts: 5.43 us -> none  [ring_reduce_scatter(): both = jnp.stack([keep, lax.ppermute(give, pair, swap)])]
    select_n x1 -> x0, local copies, waits for them, and re-layouts: 3.39 us -> none  [ring_reduce_scatter(): keep = jnp.where(me == 0, x[:, :h], x[:, h:])]
    unnamed x13 -> x7, local copies, waits for them, and re-layouts: 4.51 us -> 7.21 us
  transfers between devices with their start and end apart: 10 -> 8, of which waited for: 9 -> 8; matrix products, arithmetic and copies ran while one was open for 2% -> 0% of each run, Pallas kernels for 0% -> 0%
where the time goes in v6:
time: 312 us; the launch traced here: 311 us
  Pallas kernels  105 us (34%)
  waiting for transfers between devices  96.9 us (31%)
  between operations  34.3 us (11%)
  local copies, waits for them, and re-layouts  33.4 us (11%)
  starting transfers between devices  15.8 us (5%)
  matrix products  13.2 us (4%)
  other arithmetic  12.3 us (4%)
    pallas_call x1, Pallas kernels, cholesky_upper(): pl.pallas_call(functools.partial(_chol_kernel, nb=nb, b=b), out_shape=jax...  105 us
    ppermute x7, waiting for transfers between devices, ring_reduce_scatter(): acc = lax.ppermute(acc, (axis, pair), ring) + take(step)  57.8 us
    all_gather x1, waiting for transfers between devices, local(): every = lax.all_gather(own, ('samp', 'chan'), axis=0, tiled=True)  39.1 us
    ppermute x7, starting transfers between devices, ring_reduce_scatter(): acc = lax.ppermute(acc, (axis, pair), ring) + take(step)  15.8 us
    concatenate x1, local copies, waits for them, and re-layouts, local(): both = jnp.concatenate([in_part, out_part], axis=1).reshape(samples, -1)  9.08 us
    another operation x1, local copies, waits for them, and re-layouts, ring_reduce_scatter(): blocks = x.reshape(n, -1, x.shape[-1])  8.92 us
    add x7, other arithmetic, ring_reduce_scatter(): acc = lax.ppermute(acc, (axis, pair), ring) + take(step)  8.79 us
    unnamed x7, local copies, waits for them, and re-layouts  7.21 us
  transfers between devices with their start and end apart: 8, of which 8 were waited for; matrix products, arithmetic and copies ran while one was open for 0% of the time, Pallas kernels for 0%

profile of v6, /device:TPU:0, one launch (start us, length us, event | category | flops | bytes accessed | tf_op | source)
XLA Modules:
  0.0 311.3 jit_solution(395758398743335846)
XLA Ops:
  7.2 0.0 copy-start
  7.2 0.0 all-gather.2.cloned.1.call-start
  7.2 1.4 dynamic_slice.55
  13.9 1.6 fusion.10
  16.6 0.0 copy-start.1
  16.7 0.0 copy-start.2
  16.7 7.2 %copy.11 = bf16[128,32,784]{0,1,2:T(8,128)(2,1)} copy(bf16[128,32,784]{0,2,1:T(8,128)(2,1)} %param.6) | data formatting | bytes 12845056 | tf_op args[0]
  23.9 0.0 copy-done.1
  23.9 0.1 copy.16
  24.0 0.0 copy-done
  24.0 0.0 copy-done.2
  24.0 0.6 convolution_bitcast_fusion
  24.7 4.8 %fusion.11 = f32[128,32,14,14]{0,1,3,2:T(8,128)S(1)} fusion(bf16[128,32,28,28]{0,1,3,2:T(8,128)(2,1)} %bitcast.42, bf16[32,3,3,32]{0,3,2,1:T(8,128)(2,1)S(1)} %bitcast.44), kind=kOutput, calls=%fused_computation.28 | convolution fusion | flops 440664064 | bytes 9652224 | tf_op jit(solution)/shard_map/conv_general_dilated | solution.py:82
  29.5 3.5 %pad_maximum_fusion = f32[128,64,196]{0,1,2:T(8,128)} fusion(f32[128,32,196]{0,1,2:T(8,128)S(1)} %convolution_bitcast_fusion, f32[128,32,196]{0,1,2:T(8,128)S(1)} %bitcast.43), kind=kLoop, calls=%fused_computation | loop fusion | flops 1605632 | bytes 12845056 | tf_op jit(solution)/shard_map/concatenate | solution.py:139
  32.9 9.1 %copy.14 = f32[128,64,196]{2,1,0:T(8,128)} copy(f32[128,64,196]{0,1,2:T(8,128)} %pad_maximum_fusion) | data formatting | bytes 12845056 | tf_op jit(solution)/shard_map/concatenate | solution.py:139
  42.0 8.9 %reshape_reshape.3 = f32[8,16,12544]{2,1,0:T(8,128)} reshape(f32[128,64,196]{2,1,0:T(8,128)} %copy.14) | data formatting | bytes 12845056 | tf_op jit(solution)/shard_map/reshape;reshape | solution.py:118
  51.5 1.2 dynamic-slice_bitcast_fusion
  52.7 3.0 collective-permute-start
  57.6 8.3 %collective-permute-done = f32[16,12544]{1,0:T(8,128)S(1)} collective-permute-done((f32[16,12544]{1,0:T(8,128)S(1)}, f32[16,12544]{1,0:T(8,128)S(1)}, u32[]{:S(2)}, u32[]{:S(2)}) %collective-permute-start) | collective-permute-done | bytes 802848 | tf_op jit(solution)/shard_map/ppermute | solution.py:131
  65.9 1.2 bitcast_add_fusion.6
  67.1 2.1 collective-permute-start.1
  71.1 8.2 %collective-permute-done.1 = f32[16,12544]{1,0:T(8,128)S(1)} collective-permute-done((f32[16,12544]{1,0:T(8,128)S(1)}, f32[16,12544]{1,0:T(8,128)S(1)}, u32[]{:S(2)}, u32[]{:S(2)}) %collective-permute-start.1) | collective-permute-done | bytes 802848 | tf_op jit(solution)/shard_map/ppermute | solution.py:131
  79.3 1.2 bitcast_add_fusion.5
  80.5 2.1 collective-permute-start.2
  84.3 8.4 %collective-permute-done.2 = f32[16,12544]{1,0:T(8,128)S(1)} collective-permute-done((f32[16,12544]{1,0:T(8,128)S(1)}, f32[16,12544]{1,0:T(8,128)S(1)}, u32[]{:S(2)}, u32[]{:S(2)}) %collective-permute-start.2) | collective-permute-done | bytes 802848 | tf_op jit(solution)/shard_map/ppermute | solution.py:131
  92.8 1.2 bitcast_add_fusion.4
  94.0 2.1 collective-permute-start.3
  98.0 8.2 %collective-permute-done.3 = f32[16,12544]{1,0:T(8,128)S(1)} collective-permute-done((f32[16,12544]{1,0:T(8,128)S(1)}, f32[16,12544]{1,0:T(8,128)S(1)}, u32[]{:S(2)}, u32[]{:S(2)}) %collective-permute-start.3) | collective-permute-done | bytes 802848 | tf_op jit(solution)/shard_map/ppermute | solution.py:131
  106.2 1.2 bitcast_add_fusion.3
  107.4 2.1 collective-permute-start.4
  111.5 8.2 %collective-permute-done.4 = f32[16,12544]{1,0:T(8,128)S(1)} collective-permute-done((f32[16,12544]{1,0:T(8,128)S(1)}, f32[16,12544]{1,0:T(8,128)S(1)}, u32[]{:S(2)}, u32[]{:S(2)}) %collective-permute-start.4) | collective-permute-done | bytes 802848 | tf_op jit(solution)/shard_map/ppermute | solution.py:131
  119.6 1.2 bitcast_add_fusion.2
  120.9 2.1 collective-permute-start.5
  124.9 8.2 %collective-permute-done.5 = f32[16,12544]{1,0:T(8,128)S(1)} collective-permute-done((f32[16,12544]{1,0:T(8,128)S(1)}, f32[16,12544]{1,0:T(8,128)S(1)}, u32[]{:S(2)}, u32[]{:S(2)}) %collective-permute-start.5) | collective-permute-done | bytes 802848 | tf_op jit(solution)/shard_map/ppermute | solution.py:131
  133.1 1.2 bitcast_add_fusion.1
  134.3 2.3 collective-permute-start.6
  138.5 8.3 %collective-permute-done.6 = f32[16,12544]{1,0:T(8,128)} collective-permute-done((f32[16,12544]{1,0:T(8,128)S(1)}, f32[16,12544]{1,0:T(8,128)}, u32[]{:S(2)}, u32[]{:S(2)}) %collective-permute-start.6) | collective-permute-done | bytes 802848 | tf_op jit(solution)/shard_map/ppermute | solution.py:131
  146.8 1.5 bitcast_add_fusion
  148.3 1.5 reshape.28
  149.8 0.7 convolution_multiply_fusion
  150.5 0.8 reshape.29
  151.2 0.0 all-gather.2.cloned.1.call-update
  151.3 0.8 broadcast_in_dim_reshape.3
  152.0 39.1 %all-gather.2.cloned.1.call-done = f32[256,1024]{1,0:T(8,128)} async-done(((f32[16,1024]{1,0:T(8,128)}), f32[256,1024]{1,0:T(8,128)}) %all-gather.2.cloned.1.call-update) | async-done | bytes 1048592 | tf_op jit(solution)/shard_map/all_gather | solution.py:145
  191.1 7.1 %convert_add_fusion = f32[1024,1024]{1,0:T(8,128)} fusion(f32[256,1024]{1,0:T(8,128)} %all-gather.2.cloned.1.call-done), kind=kOutput, calls=%fused_computation.1 | convolution fusion | flops 3225419776 | bytes 5242880 | tf_op jit(solution)/shard_map/nk,nm->km/dot_general | solution.py:149
  198.2 105.4 %shard_map.77 = f32[8,128,1024]{2,1,0:T(8,128)S(1)} custom-call(f32[8,128,1024]{2,1,0:T(8,128)} %bitcast.41), custom_call_target="tpu_custom_call" | custom-call | tf_op jit(solution)/shard_map/pallas_call | solution.py:63
  303.6 0.8 constant_dynamic-slice_fusion
  (1 shorter events, 0.0 us)
Async XLA Ops:
  7.2 16.8 %copy-start = (bf16[128,32,196]{0,1,2:T(8,128)(2,1)S(1)}, bf16[128,32,196]{0,1,2:T(8,128)(2,1)}, u32[]{:S(2)}) copy-start(bf16[128,32,196]{0,1,2:T(8,128)(2,1)} %param.7) | copy-start | bytes 4816900
  7.2 183.9 %all-gather.2.cloned.1.call-start = ((), (), s32[]{:S(2)}) async-start(), calls=%async_computation | async-start | bytes 1114112 | tf_op jit(solution)/shard_map/all_gather | solution.py:145
  16.6 7.2 %copy-start.1 = (s32[32,288]{1,0:T(8,128)S(1)}, s32[32,288]{1,0:T(8,128)}, u32[]{:S(2)}) copy-start(s32[32,288]{1,0:T(8,128)} %param.8) | copy-start | bytes 110596
  16.7 7.4 %copy-start.2 = (s32[32,32]{1,0:T(8,128)S(1)}, s32[32,32]{1,0:T(8,128)}, u32[]{:S(2)}) copy-start(s32[32,32]{1,0:T(8,128)} %param.9) | copy-start | bytes 12292
  52.7 13.2 %collective-permute-start = (f32[16,12544]{1,0:T(8,128)S(1)}, f32[16,12544]{1,0:T(8,128)S(1)}, u32[]{:S(2)}, u32[]{:S(2)}) collective-permute-start(f32[16,12544]{1,0:T(8,128)S(1)} %dynamic-slice_bitcast_fusion), channel_id=1, source_target_pairs={{0,4},{5,1},{4,8},{9,5},{8,12},{13,9},{12,14},{15,13},{14,10},{11,... | collective-permute-start | bytes 2408456 | tf_op jit(solution)/shard_map/ppermute | solution.py:131
  67.1 12.2 %collective-permute-start.1 = (f32[16,12544]{1,0:T(8,128)S(1)}, f32[16,12544]{1,0:T(8,128)S(1)}, u32[]{:S(2)}, u32[]{:S(2)}) collective-permute-start(f32[16,12544]{1,0:T(8,128)S(1)} %bitcast_add_fusion.6), channel_id=1, source_target_pairs={{0,4},{5,1},{4,8},{9,5},{8,12},{13,9},{12,14},{15,13},{14,10},{11,... | collective-permute-start | bytes 2408456 | tf_op jit(solution)/shard_map/ppermute | solution.py:131
  80.5 12.2 %collective-permute-start.2 = (f32[16,12544]{1,0:T(8,128)S(1)}, f32[16,12544]{1,0:T(8,128)S(1)}, u32[]{:S(2)}, u32[]{:S(2)}) collective-permute-start(f32[16,12544]{1,0:T(8,128)S(1)} %bitcast_add_fusion.5), channel_id=1, source_target_pairs={{0,4},{5,1},{4,8},{9,5},{8,12},{13,9},{12,14},{15,13},{14,10},{11,... | collective-permute-start | bytes 2408456 | tf_op jit(solution)/shard_map/ppermute | solution.py:131
  94.0 12.2 %collective-permute-start.3 = (f32[16,12544]{1,0:T(8,128)S(1)}, f32[16,12544]{1,0:T(8,128)S(1)}, u32[]{:S(2)}, u32[]{:S(2)}) collective-permute-start(f32[16,12544]{1,0:T(8,128)S(1)} %bitcast_add_fusion.4), channel_id=1, source_target_pairs={{0,4},{5,1},{4,8},{9,5},{8,12},{13,9},{12,14},{15,13},{14,10},{11,... | collective-permute-start | bytes 2408456 | tf_op jit(solution)/shard_map/ppermute | solution.py:131
  107.4 12.2 %collective-permute-start.4 = (f32[16,12544]{1,0:T(8,128)S(1)}, f32[16,12544]{1,0:T(8,128)S(1)}, u32[]{:S(2)}, u32[]{:S(2)}) collective-permute-start(f32[16,12544]{1,0:T(8,128)S(1)} %bitcast_add_fusion.3), channel_id=1, source_target_pairs={{0,4},{5,1},{4,8},{9,5},{8,12},{13,9},{12,14},{15,13},{14,10},{11,... | collective-permute-start | bytes 2408456 | tf_op jit(solution)/shard_map/ppermute | solution.py:131
  120.9 12.2 %collective-permute-start.5 = (f32[16,12544]{1,0:T(8,128)S(1)}, f32[16,12544]{1,0:T(8,128)S(1)}, u32[]{:S(2)}, u32[]{:S(2)}) collective-permute-start(f32[16,12544]{1,0:T(8,128)S(1)} %bitcast_add_fusion.2), channel_id=1, source_target_pairs={{0,4},{5,1},{4,8},{9,5},{8,12},{13,9},{12,14},{15,13},{14,10},{11,... | collective-permute-start | bytes 2408456 | tf_op jit(solution)/shard_map/ppermute | solution.py:131
  134.3 12.5 %collective-permute-start.6 = (f32[16,12544]{1,0:T(8,128)S(1)}, f32[16,12544]{1,0:T(8,128)}, u32[]{:S(2)}, u32[]{:S(2)}) collective-permute-start(f32[16,12544]{1,0:T(8,128)S(1)} %bitcast_add_fusion.1), channel_id=1, source_target_pairs={{0,4},{5,1},{4,8},{9,5},{8,12},{13,9},{12,14},{15,13},{14,10},{11,... | collective-permute-start | bytes 2408456 | tf_op jit(solution)/shard_map/ppermute | solution.py:131
Sparse Core Ops, SparseCore 0:
  151.4 39.6 all-gather.1

commit v7 on v6

--- a/solution.py
+++ b/solution.py
@@ -132,6 +132,20 @@
     return acc
 
 
+def doubling_gather(x, axes):
+    size = 1
+    for a in axes:
+        size *= lax.axis_size(a)
+    if size & (size - 1):
+        return lax.all_gather(x, axes, axis=0, tiled=True)
+    k = 1
+    while k < size:
+        other = lax.ppermute(x, axes, [(i, i ^ k) for i in range(size)])
+        x = jnp.concatenate([x, other], axis=0)
+        k *= 2
+    return x
+
+
 def local(images, out_grads, in_signs, out_signs):
     samples = images.shape[0]
     in_part, out_part = project(images, out_grads, in_signs, out_signs)
@@ -142,7 +156,7 @@
     in_sum = both[:, :width_in]
     out_sum = both[:, width_in:]
     own = sketch(in_sum, out_sum, C)
-    every = lax.all_gather(own, ("samp", "chan"), axis=0, tiled=True)
+    every = doubling_gather(own, ("chan", "samp"))
     batch_total = samples * lax.axis_size("samp")
     width = every.shape[1]
     identity_mat = jnp.eye(width, dtype=jnp.float32)

time: 312 us -> 297 us (0.952)
  between operations: 34.3 us -> 21.3 us
  waiting for transfers between devices: 96.9 us -> 90 us
  starting transfers between devices: 15.8 us -> 22.4 us
    all_gather x1 -> x0, waiting for transfers between devices: 39.1 us -> none  [local(): every = lax.all_gather(own, ('samp', 'chan'), axis=0, tiled=True)]
    ppermute x0 -> x4, waiting for transfers between devices: none -> 32.5 us  [doubling_gather(): other = lax.ppermute(x, axes, [(i, i ^ k) for i in range(size)])]
    ppermute x0 -> x4, starting transfers between devices: none -> 6.56 us  [doubling_gather(): other = lax.ppermute(x, axes, [(i, i ^ k) for i in range(size)])]
    unnamed x7 -> x13, local copies, waits for them, and re-layouts: 7.21 us -> 7.25 us
  transfers between devices with their start and end apart: 8 -> 11, of which waited for: 8 -> 11; matrix products, arithmetic and copies ran while one was open for 0% -> 0% of each run, Pallas kernels for 0% -> 0%
where the time goes in v7:
time: 297 us; the launch traced here: 296 us
  Pallas kernels  105 us (35%)
  waiting for transfers between devices  90 us (30%)
  local copies, waits for them, and re-layouts  32.9 us (11%)
  starting transfers between devices  22.4 us (8%)
  between operations  21.3 us (7%)
  other arithmetic  12.1 us (4%)
  matrix products  11.7 us (4%)
    pallas_call x1, Pallas kernels, cholesky_upper(): pl.pallas_call(functools.partial(_chol_kernel, nb=nb, b=b), out_shape=jax...  105 us
    ppermute x7, waiting for transfers between devices, ring_reduce_scatter(): acc = lax.ppermute(acc, (axis, pair), ring) + take(step)  57.5 us
    ppermute x4, waiting for transfers between devices, doubling_gather(): other = lax.ppermute(x, axes, [(i, i ^ k) for i in range(size)])  32.5 us
    ppermute x7, starting transfers between devices, ring_reduce_scatter(): acc = lax.ppermute(acc, (axis, pair), ring) + take(step)  15.8 us
    concatenate x1, local copies, waits for them, and re-layouts, local(): both = jnp.concatenate([in_part, out_part], axis=1).reshape(samples, -1)  9.06 us
    another operation x1, local copies, waits for them, and re-layouts, ring_reduce_scatter(): blocks = x.reshape(n, -1, x.shape[-1])  8.95 us
    add x7, other arithmetic, ring_reduce_scatter(): acc = lax.ppermute(acc, (axis, pair), ring) + take(step)  8.55 us
    unnamed x13, local copies, waits for them, and re-layouts  7.25 us
  transfers between devices with their start and end apart: 11, of which 11 were waited for; matrix products, arithmetic and copies ran while one was open for 0% of the time, Pallas kernels for 0%

profile of v7, /device:TPU:0, one launch (start us, length us, event | category | flops | bytes accessed | tf_op | source)
XLA Modules:
  0.0 295.7 jit_solution(13364664281269049490)
XLA Ops:
  0.6 0.0 copy-start
  0.7 1.4 dynamic_slice.55
  7.3 1.7 fusion.10
  10.4 0.0 copy-start.2
  10.4 7.2 %copy.11 = bf16[128,32,784]{0,1,2:T(8,128)(2,1)} copy(bf16[128,32,784]{0,2,1:T(8,128)(2,1)} %param.6) | data formatting | bytes 12845056 | tf_op args[0]
  17.6 0.1 copy.16
  17.7 0.6 convolution_bitcast_fusion
  18.4 4.8 %fusion.11 = f32[128,32,14,14]{0,1,3,2:T(8,128)S(1)} fusion(bf16[128,32,28,28]{0,1,3,2:T(8,128)(2,1)} %bitcast.42, bf16[32,3,3,32]{0,3,2,1:T(8,128)(2,1)S(1)} %bitcast.44), kind=kOutput, calls=%fused_computation.36 | convolution fusion | flops 440664064 | bytes 9652224 | tf_op jit(solution)/shard_map/conv_general_dilated | solution.py:82
  23.2 3.5 %pad_maximum_fusion = f32[128,64,196]{0,1,2:T(8,128)} fusion(f32[128,32,196]{0,1,2:T(8,128)S(1)} %convolution_bitcast_fusion, f32[128,32,196]{0,1,2:T(8,128)S(1)} %bitcast.43), kind=kLoop, calls=%fused_computation | loop fusion | flops 1605632 | bytes 12845056 | tf_op jit(solution)/shard_map/concatenate | solution.py:153
  26.6 9.1 %copy.14 = f32[128,64,196]{2,1,0:T(8,128)} copy(f32[128,64,196]{0,1,2:T(8,128)} %pad_maximum_fusion) | data formatting | bytes 12845056 | tf_op jit(solution)/shard_map/concatenate | solution.py:153
  35.7 9.0 %reshape_reshape.3 = f32[8,16,12544]{2,1,0:T(8,128)} reshape(f32[128,64,196]{2,1,0:T(8,128)} %copy.14) | data formatting | bytes 12845056 | tf_op jit(solution)/shard_map/reshape;reshape | solution.py:118
  45.4 1.2 dynamic-slice_bitcast_fusion
  46.6 3.1 %collective-permute-start = (f32[16,12544]{1,0:T(8,128)S(1)}, f32[16,12544]{1,0:T(8,128)S(1)}, u32[]{:S(2)}, u32[]{:S(2)}) collective-permute-start(f32[16,12544]{1,0:T(8,128)S(1)} %dynamic-slice_bitcast_fusion), channel_id=1, source_target_pairs={{0,4},{5,1},{4,8},{9,5},{8,12},{13,9},{12,14},{15,13},{14,10},{11,... | collective-permute-start | bytes 2408456 | tf_op jit(solution)/shard_map/ppermute | solution.py:131
  51.5 8.2 %collective-permute-done = f32[16,12544]{1,0:T(8,128)S(1)} collective-permute-done((f32[16,12544]{1,0:T(8,128)S(1)}, f32[16,12544]{1,0:T(8,128)S(1)}, u32[]{:S(2)}, u32[]{:S(2)}) %collective-permute-start) | collective-permute-done | bytes 802848 | tf_op jit(solution)/shard_map/ppermute | solution.py:131
  59.7 1.2 bitcast_add_fusion.6
  60.9 2.1 collective-permute-start.1
  64.8 8.4 %collective-permute-done.1 = f32[16,12544]{1,0:T(8,128)S(1)} collective-permute-done((f32[16,12544]{1,0:T(8,128)S(1)}, f32[16,12544]{1,0:T(8,128)S(1)}, u32[]{:S(2)}, u32[]{:S(2)}) %collective-permute-start.1) | collective-permute-done | bytes 802848 | tf_op jit(solution)/shard_map/ppermute | solution.py:131
  73.2 1.2 bitcast_add_fusion.5
  74.4 2.1 collective-permute-start.2
  78.4 8.2 %collective-permute-done.2 = f32[16,12544]{1,0:T(8,128)S(1)} collective-permute-done((f32[16,12544]{1,0:T(8,128)S(1)}, f32[16,12544]{1,0:T(8,128)S(1)}, u32[]{:S(2)}, u32[]{:S(2)}) %collective-permute-start.2) | collective-permute-done | bytes 802848 | tf_op jit(solution)/shard_map/ppermute | solution.py:131
  86.6 1.2 bitcast_add_fusion.4
  87.8 2.1 collective-permute-start.3
  91.8 8.2 %collective-permute-done.3 = f32[16,12544]{1,0:T(8,128)S(1)} collective-permute-done((f32[16,12544]{1,0:T(8,128)S(1)}, f32[16,12544]{1,0:T(8,128)S(1)}, u32[]{:S(2)}, u32[]{:S(2)}) %collective-permute-start.3) | collective-permute-done | bytes 802848 | tf_op jit(solution)/shard_map/ppermute | solution.py:131
  100.0 1.2 bitcast_add_fusion.3
  101.3 2.1 collective-permute-start.4
  105.3 8.2 %collective-permute-done.4 = f32[16,12544]{1,0:T(8,128)S(1)} collective-permute-done((f32[16,12544]{1,0:T(8,128)S(1)}, f32[16,12544]{1,0:T(8,128)S(1)}, u32[]{:S(2)}, u32[]{:S(2)}) %collective-permute-start.4) | collective-permute-done | bytes 802848 | tf_op jit(solution)/shard_map/ppermute | solution.py:131
  113.5 1.2 bitcast_add_fusion.2
  114.7 2.1 collective-permute-start.5
  118.7 8.2 %collective-permute-done.5 = f32[16,12544]{1,0:T(8,128)S(1)} collective-permute-done((f32[16,12544]{1,0:T(8,128)S(1)}, f32[16,12544]{1,0:T(8,128)S(1)}, u32[]{:S(2)}, u32[]{:S(2)}) %collective-permute-start.5) | collective-permute-done | bytes 802848 | tf_op jit(solution)/shard_map/ppermute | solution.py:131
  126.9 1.2 bitcast_add_fusion.1
  128.2 2.1 collective-permute-start.6
  132.2 8.2 %collective-permute-done.6 = f32[16,12544]{1,0:T(8,128)S(1)} collective-permute-done((f32[16,12544]{1,0:T(8,128)S(1)}, f32[16,12544]{1,0:T(8,128)S(1)}, u32[]{:S(2)}, u32[]{:S(2)}) %collective-permute-start.6) | collective-permute-done | bytes 802848 | tf_op jit(solution)/shard_map/ppermute | solution.py:131
  140.4 1.2 bitcast_add_fusion
  141.6 1.5 reshape.28
  143.1 0.7 convolution_multiply_fusion
  143.8 0.1 reshape.29
  143.9 0.1 collective-permute-start.7
  144.0 1.2 collective-permute-done.7
  145.2 2.1 collective-permute-start.8
  147.3 3.8 %collective-permute-done.8 = f32[32,1024]{1,0:T(8,128)S(1)} collective-permute-done((f32[32,1024]{1,0:T(8,128)S(1)}, f32[32,1024]{1,0:T(8,128)S(1)}, u32[]{:S(2)}, u32[]{:S(2)}) %collective-permute-start.8) | collective-permute-done | bytes 131104 | tf_op jit(solution)/shard_map/ppermute | solution.py:143
  151.2 1.9 collective-permute-start.9
  153.0 6.1 %collective-permute-done.9 = f32[64,1024]{1,0:T(8,128)S(1)} collective-permute-done((f32[64,1024]{1,0:T(8,128)S(1)}, f32[64,1024]{1,0:T(8,128)S(1)}, u32[]{:S(2)}, u32[]{:S(2)}) %collective-permute-start.9) | collective-permute-done | bytes 262176 | tf_op jit(solution)/shard_map/ppermute | solution.py:143
  159.1 2.5 collective-permute-start.10
  161.7 0.8 broadcast_in_dim_reshape.3
  162.5 21.4 %collective-permute-done.10 = f32[128,1024]{1,0:T(8,128)S(1)} collective-permute-done((f32[128,1024]{1,0:T(8,128)S(1)}, f32[128,1024]{1,0:T(8,128)S(1)}, u32[]{:S(2)}, u32[]{:S(2)}) %collective-permute-start.10) | collective-permute-done | bytes 524320 | tf_op jit(solution)/shard_map/ppermute | solution.py:143
  183.9 5.6 %convert_add_fusion = f32[1024,1024]{1,0:T(8,128)} fusion(f32[256,1024]{1,0:T(8,128)S(1)} %constant_dynamic-update-slice_fusion), kind=kOutput, calls=%fused_computation.1 | convolution fusion | flops 3225419776 | bytes 5242880 | tf_op jit(solution)/shard_map/nk,nm->km/dot_general | solution.py:163
  189.6 105.3 %shard_map.77 = f32[8,128,1024]{2,1,0:T(8,128)S(1)} custom-call(f32[8,128,1024]{2,1,0:T(8,128)} %bitcast.41), custom_call_target="tpu_custom_call" | custom-call | tf_op jit(solution)/shard_map/pallas_call | solution.py:63
  294.9 0.8 constant_dynamic-slice_fusion
  (15 shorter events, 0.2 us)
Async XLA Ops:
  0.6 17.1 %copy-start = (bf16[128,32,196]{0,1,2:T(8,128)(2,1)S(1)}, bf16[128,32,196]{0,1,2:T(8,128)(2,1)}, u32[]{:S(2)}) copy-start(bf16[128,32,196]{0,1,2:T(8,128)(2,1)} %param.7) | copy-start | bytes 4816900
  10.4 7.2 %copy-start.2 = (s32[32,288]{1,0:T(8,128)S(1)}, s32[32,288]{1,0:T(8,128)}, u32[]{:S(2)}) copy-start(s32[32,288]{1,0:T(8,128)} %param.8) | copy-start | bytes 110596
  10.4 7.3 %copy-start.3 = (s32[32,32]{1,0:T(8,128)S(1)}, s32[32,32]{1,0:T(8,128)}, u32[]{:S(2)}) copy-start(s32[32,32]{1,0:T(8,128)} %param.9) | copy-start | bytes 12292
  46.6 13.2 %collective-permute-start = (f32[16,12544]{1,0:T(8,128)S(1)}, f32[16,12544]{1,0:T(8,128)S(1)}, u32[]{:S(2)}, u32[]{:S(2)}) collective-permute-start(f32[16,12544]{1,0:T(8,128)S(1)} %dynamic-slice_bitcast_fusion), channel_id=1, source_target_pairs={{0,4},{5,1},{4,8},{9,5},{8,12},{13,9},{12,14},{15,13},{14,10},{11,... | collective-permute-start | bytes 2408456 | tf_op jit(solution)/shard_map/ppermute | solution.py:131
  60.9 12.2 %collective-permute-start.1 = (f32[16,12544]{1,0:T(8,128)S(1)}, f32[16,12544]{1,0:T(8,128)S(1)}, u32[]{:S(2)}, u32[]{:S(2)}) collective-permute-start(f32[16,12544]{1,0:T(8,128)S(1)} %bitcast_add_fusion.6), channel_id=1, source_target_pairs={{0,4},{5,1},{4,8},{9,5},{8,12},{13,9},{12,14},{15,13},{14,10},{11,... | collective-permute-start | bytes 2408456 | tf_op jit(solution)/shard_map/ppermute | solution.py:131
  74.4 12.2 %collective-permute-start.2 = (f32[16,12544]{1,0:T(8,128)S(1)}, f32[16,12544]{1,0:T(8,128)S(1)}, u32[]{:S(2)}, u32[]{:S(2)}) collective-permute-start(f32[16,12544]{1,0:T(8,128)S(1)} %bitcast_add_fusion.5), channel_id=1, source_target_pairs={{0,4},{5,1},{4,8},{9,5},{8,12},{13,9},{12,14},{15,13},{14,10},{11,... | collective-permute-start | bytes 2408456 | tf_op jit(solution)/shard_map/ppermute | solution.py:131
  87.8 12.2 %collective-permute-start.3 = (f32[16,12544]{1,0:T(8,128)S(1)}, f32[16,12544]{1,0:T(8,128)S(1)}, u32[]{:S(2)}, u32[]{:S(2)}) collective-permute-start(f32[16,12544]{1,0:T(8,128)S(1)} %bitcast_add_fusion.4), channel_id=1, source_target_pairs={{0,4},{5,1},{4,8},{9,5},{8,12},{13,9},{12,14},{15,13},{14,10},{11,... | collective-permute-start | bytes 2408456 | tf_op jit(solution)/shard_map/ppermute | solution.py:131
  101.3 12.2 %collective-permute-start.4 = (f32[16,12544]{1,0:T(8,128)S(1)}, f32[16,12544]{1,0:T(8,128)S(1)}, u32[]{:S(2)}, u32[]{:S(2)}) collective-permute-start(f32[16,12544]{1,0:T(8,128)S(1)} %bitcast_add_fusion.3), channel_id=1, source_target_pairs={{0,4},{5,1},{4,8},{9,5},{8,12},{13,9},{12,14},{15,13},{14,10},{11,... | collective-permute-start | bytes 2408456 | tf_op jit(solution)/shard_map/ppermute | solution.py:131
  114.7 12.2 %collective-permute-start.5 = (f32[16,12544]{1,0:T(8,128)S(1)}, f32[16,12544]{1,0:T(8,128)S(1)}, u32[]{:S(2)}, u32[]{:S(2)}) collective-permute-start(f32[16,12544]{1,0:T(8,128)S(1)} %bitcast_add_fusion.2), channel_id=1, source_target_pairs={{0,4},{5,1},{4,8},{9,5},{8,12},{13,9},{12,14},{15,13},{14,10},{11,... | collective-permute-start | bytes 2408456 | tf_op jit(solution)/shard_map/ppermute | solution.py:131
  128.2 12.2 %collective-permute-start.6 = (f32[16,12544]{1,0:T(8,128)S(1)}, f32[16,12544]{1,0:T(8,128)S(1)}, u32[]{:S(2)}, u32[]{:S(2)}) collective-permute-start(f32[16,12544]{1,0:T(8,128)S(1)} %bitcast_add_fusion.1), channel_id=1, source_target_pairs={{0,4},{5,1},{4,8},{9,5},{8,12},{13,9},{12,14},{15,13},{14,10},{11,... | collective-permute-start | bytes 2408456 | tf_op jit(solution)/shard_map/ppermute | solution.py:131
  143.9 1.3 collective-permute-start.7
  145.2 5.9 %collective-permute-start.8 = (f32[32,1024]{1,0:T(8,128)S(1)}, f32[32,1024]{1,0:T(8,128)S(1)}, u32[]{:S(2)}, u32[]{:S(2)}) collective-permute-start(f32[32,1024]{1,0:T(8,128)S(1)} %pad_maximum_fusion.3), channel_id=1, source_target_pairs={{0,2},{1,3},{2,0},{3,1},{4,6},{5,7},{6,4},{7,5},{8,10},{9,11},{10,... | collective-permute-start | bytes 393224 | tf_op jit(solution)/shard_map/ppermute | solution.py:143
  151.2 7.9 %collective-permute-start.9 = (f32[64,1024]{1,0:T(8,128)S(1)}, f32[64,1024]{1,0:T(8,128)S(1)}, u32[]{:S(2)}, u32[]{:S(2)}) collective-permute-start(f32[64,1024]{1,0:T(8,128)S(1)} %pad_maximum_fusion.2), channel_id=1, source_target_pairs={{0,4},{1,5},{2,6},{3,7},{4,0},{5,1},{6,2},{7,3},{8,12},{9,13},{10,... | collective-permute-start | bytes 786440 | tf_op jit(solution)/shard_map/ppermute | solution.py:143
  159.1 24.8 %collective-permute-start.10 = (f32[128,1024]{1,0:T(8,128)S(1)}, f32[128,1024]{1,0:T(8,128)S(1)}, u32[]{:S(2)}, u32[]{:S(2)}) collective-permute-start(f32[128,1024]{1,0:T(8,128)S(1)} %pad_maximum_fusion.1), channel_id=1, source_target_pairs={{0,8},{1,9},{2,10},{3,11},{4,12},{5,13},{6,14},{7,15},{8,0},{9,1},... | collective-permute-start | bytes 1572872 | tf_op jit(solution)/shard_map/ppermute | solution.py:143
  189.6 106.1 %copy-start.1 = (bf16[128,32,196]{0,1,2:T(8,128)(2,1)S(1)}, bf16[128,32,196]{0,1,2:T(8,128)(2,1)}, u32[]{:S(2)}) copy-start(bf16[128,32,196]{0,1,2:T(8,128)(2,1)} %param.7) | copy-start | bytes 4816900

commit v8 on v7

--- a/solution.py
+++ b/solution.py
@@ -138,11 +138,11 @@
         size *= lax.axis_size(a)
     if size & (size - 1):
         return lax.all_gather(x, axes, axis=0, tiled=True)
-    k = 1
-    while k < size:
+    k = size // 2
+    while k:
         other = lax.ppermute(x, axes, [(i, i ^ k) for i in range(size)])
         x = jnp.concatenate([x, other], axis=0)
-        k *= 2
+        k //= 2
     return x
 
 

time: 297 us -> 276 us (0.929)
  waiting for transfers between devices: 90 us -> 68.4 us
    ppermute x4, waiting for transfers between devices: 32.5 us -> 10.9 us  [doubling_gather(): other = lax.ppermute(x, axes, [(i, i ^ k) for i in range(size)])]
where the time goes in v8:
time: 276 us; the launch traced here: 275 us
  Pallas kernels  105 us (38%)
  waiting for transfers between devices  68.4 us (25%)
  local copies, waits for them, and re-layouts  32.9 us (12%)
  starting transfers between devices  22.9 us (8%)
  between operations  21.3 us (8%)
  other arithmetic  12.1 us (4%)
  matrix products  11.7 us (4%)
    pallas_call x1, Pallas kernels, cholesky_upper(): pl.pallas_call(functools.partial(_chol_kernel, nb=nb, b=b), out_shape=jax...  105 us
    ppermute x7, waiting for transfers between devices, ring_reduce_scatter(): acc = lax.ppermute(acc, (axis, pair), ring) + take(step)  57.5 us
    ppermute x7, starting transfers between devices, ring_reduce_scatter(): acc = lax.ppermute(acc, (axis, pair), ring) + take(step)  15.8 us
    ppermute x4, waiting for transfers between devices, doubling_gather(): other = lax.ppermute(x, axes, [(i, i ^ k) for i in range(size)])  10.9 us
    concatenate x1, local copies, waits for them, and re-layouts, local(): both = jnp.concatenate([in_part, out_part], axis=1).reshape(samples, -1)  9.06 us
    another operation x1, local copies, waits for them, and re-layouts, ring_reduce_scatter(): blocks = x.reshape(n, -1, x.shape[-1])  8.95 us
    add x7, other arithmetic, ring_reduce_scatter(): acc = lax.ppermute(acc, (axis, pair), ring) + take(step)  8.55 us
    unnamed x13, local copies, waits for them, and re-layouts  7.25 us
  transfers between devices with their start and end apart: 11, of which 11 were waited for; matrix products, arithmetic and copies ran while one was open for 0% of the time, Pallas kernels for 0%

profile of v8, /device:TPU:0, one launch (start us, length us, event | category | flops | bytes accessed | tf_op | source)
XLA Modules:
  0.0 274.6 jit_solution(5549271406167740246)
XLA Ops:
  0.6 0.0 copy-start
  0.7 1.4 dynamic_slice.55
  7.3 1.7 fusion.10
  10.4 0.0 copy-start.3
  10.4 7.2 %copy.11 = bf16[128,32,784]{0,1,2:T(8,128)(2,1)} copy(bf16[128,32,784]{0,2,1:T(8,128)(2,1)} %param.6) | data formatting | bytes 12845056 | tf_op args[0]
  17.6 0.1 copy.16
  17.7 0.6 convolution_bitcast_fusion
  18.4 4.8 %fusion.11 = f32[128,32,14,14]{0,1,3,2:T(8,128)S(1)} fusion(bf16[128,32,28,28]{0,1,3,2:T(8,128)(2,1)} %bitcast.42, bf16[32,3,3,32]{0,3,2,1:T(8,128)(2,1)S(1)} %bitcast.44), kind=kOutput, calls=%fused_computation.36 | convolution fusion | flops 440664064 | bytes 9652224 | tf_op jit(solution)/shard_map/conv_general_dilated | solution.py:82
  23.2 3.5 %pad_maximum_fusion = f32[128,64,196]{0,1,2:T(8,128)} fusion(f32[128,32,196]{0,1,2:T(8,128)S(1)} %convolution_bitcast_fusion, f32[128,32,196]{0,1,2:T(8,128)S(1)} %bitcast.43), kind=kLoop, calls=%fused_computation | loop fusion | flops 1605632 | bytes 12845056 | tf_op jit(solution)/shard_map/concatenate | solution.py:153
  26.6 9.1 %copy.14 = f32[128,64,196]{2,1,0:T(8,128)} copy(f32[128,64,196]{0,1,2:T(8,128)} %pad_maximum_fusion) | data formatting | bytes 12845056 | tf_op jit(solution)/shard_map/concatenate | solution.py:153
  35.7 9.0 %reshape_reshape.3 = f32[8,16,12544]{2,1,0:T(8,128)} reshape(f32[128,64,196]{2,1,0:T(8,128)} %copy.14) | data formatting | bytes 12845056 | tf_op jit(solution)/shard_map/reshape;reshape | solution.py:118
  45.4 1.2 dynamic-slice_bitcast_fusion
  46.6 3.1 %collective-permute-start = (f32[16,12544]{1,0:T(8,128)S(1)}, f32[16,12544]{1,0:T(8,128)S(1)}, u32[]{:S(2)}, u32[]{:S(2)}) collective-permute-start(f32[16,12544]{1,0:T(8,128)S(1)} %dynamic-slice_bitcast_fusion), channel_id=1, source_target_pairs={{0,4},{5,1},{4,8},{9,5},{8,12},{13,9},{12,14},{15,13},{14,10},{11,... | collective-permute-start | bytes 2408456 | tf_op jit(solution)/shard_map/ppermute | solution.py:131
  51.5 8.2 %collective-permute-done = f32[16,12544]{1,0:T(8,128)S(1)} collective-permute-done((f32[16,12544]{1,0:T(8,128)S(1)}, f32[16,12544]{1,0:T(8,128)S(1)}, u32[]{:S(2)}, u32[]{:S(2)}) %collective-permute-start) | collective-permute-done | bytes 802848 | tf_op jit(solution)/shard_map/ppermute | solution.py:131
  59.7 1.2 bitcast_add_fusion.6
  60.9 2.1 collective-permute-start.1
  64.8 8.4 %collective-permute-done.1 = f32[16,12544]{1,0:T(8,128)S(1)} collective-permute-done((f32[16,12544]{1,0:T(8,128)S(1)}, f32[16,12544]{1,0:T(8,128)S(1)}, u32[]{:S(2)}, u32[]{:S(2)}) %collective-permute-start.1) | collective-permute-done | bytes 802848 | tf_op jit(solution)/shard_map/ppermute | solution.py:131
  73.2 1.2 bitcast_add_fusion.5
  74.4 2.1 collective-permute-start.2
  78.4 8.2 %collective-permute-done.2 = f32[16,12544]{1,0:T(8,128)S(1)} collective-permute-done((f32[16,12544]{1,0:T(8,128)S(1)}, f32[16,12544]{1,0:T(8,128)S(1)}, u32[]{:S(2)}, u32[]{:S(2)}) %collective-permute-start.2) | collective-permute-done | bytes 802848 | tf_op jit(solution)/shard_map/ppermute | solution.py:131
  86.6 1.2 bitcast_add_fusion.4
  87.8 2.1 collective-permute-start.3
  91.8 8.2 %collective-permute-done.3 = f32[16,12544]{1,0:T(8,128)S(1)} collective-permute-done((f32[16,12544]{1,0:T(8,128)S(1)}, f32[16,12544]{1,0:T(8,128)S(1)}, u32[]{:S(2)}, u32[]{:S(2)}) %collective-permute-start.3) | collective-permute-done | bytes 802848 | tf_op jit(solution)/shard_map/ppermute | solution.py:131
  100.0 1.2 bitcast_add_fusion.3
  101.3 2.1 collective-permute-start.4
  105.3 8.2 %collective-permute-done.4 = f32[16,12544]{1,0:T(8,128)S(1)} collective-permute-done((f32[16,12544]{1,0:T(8,128)S(1)}, f32[16,12544]{1,0:T(8,128)S(1)}, u32[]{:S(2)}, u32[]{:S(2)}) %collective-permute-start.4) | collective-permute-done | bytes 802848 | tf_op jit(solution)/shard_map/ppermute | solution.py:131
  113.5 1.2 bitcast_add_fusion.2
  114.7 2.1 collective-permute-start.5
  118.7 8.2 %collective-permute-done.5 = f32[16,12544]{1,0:T(8,128)S(1)} collective-permute-done((f32[16,12544]{1,0:T(8,128)S(1)}, f32[16,12544]{1,0:T(8,128)S(1)}, u32[]{:S(2)}, u32[]{:S(2)}) %collective-permute-start.5) | collective-permute-done | bytes 802848 | tf_op jit(solution)/shard_map/ppermute | solution.py:131
  126.9 1.2 bitcast_add_fusion.1
  128.2 2.1 collective-permute-start.6
  132.2 8.2 %collective-permute-done.6 = f32[16,12544]{1,0:T(8,128)S(1)} collective-permute-done((f32[16,12544]{1,0:T(8,128)S(1)}, f32[16,12544]{1,0:T(8,128)S(1)}, u32[]{:S(2)}, u32[]{:S(2)}) %collective-permute-start.6) | collective-permute-done | bytes 802848 | tf_op jit(solution)/shard_map/ppermute | solution.py:131
  140.4 1.2 bitcast_add_fusion
  141.6 1.5 reshape.28
  143.1 0.7 convolution_multiply_fusion
  143.8 0.1 reshape.29
  143.9 3.1 %collective-permute-start.7 = (f32[16,1024]{1,0:T(8,128)S(1)}, f32[16,1024]{1,0:T(8,128)S(1)}, u32[]{:S(2)}, u32[]{:S(2)}) collective-permute-start(f32[16,1024]{1,0:T(8,128)S(1)} %reshape.29), channel_id=1, source_target_pairs={{0,8},{1,9},{2,10},{3,11},{4,12},{5,13},{6,14},{7,15},{8,0},{9,1},... | collective-permute-start | bytes 196616 | tf_op jit(solution)/shard_map/ppermute | solution.py:143
  147.1 2.2 collective-permute-done.7
  149.3 2.0 collective-permute-start.8
  151.3 3.1 %collective-permute-done.8 = f32[32,1024]{1,0:T(8,128)S(1)} collective-permute-done((f32[32,1024]{1,0:T(8,128)S(1)}, f32[32,1024]{1,0:T(8,128)S(1)}, u32[]{:S(2)}, u32[]{:S(2)}) %collective-permute-start.8) | collective-permute-done | bytes 131104 | tf_op jit(solution)/shard_map/ppermute | solution.py:143
  154.4 1.9 collective-permute-start.9
  156.3 4.5 %collective-permute-done.9 = f32[64,1024]{1,0:T(8,128)S(1)} collective-permute-done((f32[64,1024]{1,0:T(8,128)S(1)}, f32[64,1024]{1,0:T(8,128)S(1)}, u32[]{:S(2)}, u32[]{:S(2)}) %collective-permute-start.9) | collective-permute-done | bytes 262176 | tf_op jit(solution)/shard_map/ppermute | solution.py:143
  160.9 0.1 collective-permute-start.10
  160.9 0.8 broadcast_in_dim_reshape.3
  161.8 1.1 collective-permute-done.10
  162.9 5.6 %convert_add_fusion = f32[1024,1024]{1,0:T(8,128)} fusion(f32[256,1024]{1,0:T(8,128)S(1)} %constant_dynamic-update-slice_fusion), kind=kOutput, calls=%fused_computation.1 | convolution fusion | flops 3225419776 | bytes 5242880 | tf_op jit(solution)/shard_map/nk,nm->km/dot_general | solution.py:163
  168.5 105.3 %shard_map.77 = f32[8,128,1024]{2,1,0:T(8,128)S(1)} custom-call(f32[8,128,1024]{2,1,0:T(8,128)} %bitcast.41), custom_call_target="tpu_custom_call" | custom-call | tf_op jit(solution)/shard_map/pallas_call | solution.py:63
  273.8 0.8 constant_dynamic-slice_fusion
  (15 shorter events, 0.2 us)
Async XLA Ops:
  0.6 17.1 %copy-start = (bf16[128,32,196]{0,1,2:T(8,128)(2,1)S(1)}, bf16[128,32,196]{0,1,2:T(8,128)(2,1)}, u32[]{:S(2)}) copy-start(bf16[128,32,196]{0,1,2:T(8,128)(2,1)} %param.7) | copy-start | bytes 4816900
  10.4 7.2 %copy-start.2 = (s32[32,288]{1,0:T(8,128)S(1)}, s32[32,288]{1,0:T(8,128)}, u32[]{:S(2)}) copy-start(s32[32,288]{1,0:T(8,128)} %param.8) | copy-start | bytes 110596
  10.4 7.3 %copy-start.3 = (s32[32,32]{1,0:T(8,128)S(1)}, s32[32,32]{1,0:T(8,128)}, u32[]{:S(2)}) copy-start(s32[32,32]{1,0:T(8,128)} %param.9) | copy-start | bytes 12292
  46.6 13.2 %collective-permute-start = (f32[16,12544]{1,0:T(8,128)S(1)}, f32[16,12544]{1,0:T(8,128)S(1)}, u32[]{:S(2)}, u32[]{:S(2)}) collective-permute-start(f32[16,12544]{1,0:T(8,128)S(1)} %dynamic-slice_bitcast_fusion), channel_id=1, source_target_pairs={{0,4},{5,1},{4,8},{9,5},{8,12},{13,9},{12,14},{15,13},{14,10},{11,... | collective-permute-start | bytes 2408456 | tf_op jit(solution)/shard_map/ppermute | solution.py:131
  60.9 12.2 %collective-permute-start.1 = (f32[16,12544]{1,0:T(8,128)S(1)}, f32[16,12544]{1,0:T(8,128)S(1)}, u32[]{:S(2)}, u32[]{:S(2)}) collective-permute-start(f32[16,12544]{1,0:T(8,128)S(1)} %bitcast_add_fusion.6), channel_id=1, source_target_pairs={{0,4},{5,1},{4,8},{9,5},{8,12},{13,9},{12,14},{15,13},{14,10},{11,... | collective-permute-start | bytes 2408456 | tf_op jit(solution)/shard_map/ppermute | solution.py:131
  74.4 12.2 %collective-permute-start.2 = (f32[16,12544]{1,0:T(8,128)S(1)}, f32[16,12544]{1,0:T(8,128)S(1)}, u32[]{:S(2)}, u32[]{:S(2)}) collective-permute-start(f32[16,12544]{1,0:T(8,128)S(1)} %bitcast_add_fusion.5), channel_id=1, source_target_pairs={{0,4},{5,1},{4,8},{9,5},{8,12},{13,9},{12,14},{15,13},{14,10},{11,... | collective-permute-start | bytes 2408456 | tf_op jit(solution)/shard_map/ppermute | solution.py:131
  87.8 12.2 %collective-permute-start.3 = (f32[16,12544]{1,0:T(8,128)S(1)}, f32[16,12544]{1,0:T(8,128)S(1)}, u32[]{:S(2)}, u32[]{:S(2)}) collective-permute-start(f32[16,12544]{1,0:T(8,128)S(1)} %bitcast_add_fusion.4), channel_id=1, source_target_pairs={{0,4},{5,1},{4,8},{9,5},{8,12},{13,9},{12,14},{15,13},{14,10},{11,... | collective-permute-start | bytes 2408456 | tf_op jit(solution)/shard_map/ppermute | solution.py:131
  101.3 12.2 %collective-permute-start.4 = (f32[16,12544]{1,0:T(8,128)S(1)}, f32[16,12544]{1,0:T(8,128)S(1)}, u32[]{:S(2)}, u32[]{:S(2)}) collective-permute-start(f32[16,12544]{1,0:T(8,128)S(1)} %bitcast_add_fusion.3), channel_id=1, source_target_pairs={{0,4},{5,1},{4,8},{9,5},{8,12},{13,9},{12,14},{15,13},{14,10},{11,... | collective-permute-start | bytes 2408456 | tf_op jit(solution)/shard_map/ppermute | solution.py:131
  114.7 12.2 %collective-permute-start.5 = (f32[16,12544]{1,0:T(8,128)S(1)}, f32[16,12544]{1,0:T(8,128)S(1)}, u32[]{:S(2)}, u32[]{:S(2)}) collective-permute-start(f32[16,12544]{1,0:T(8,128)S(1)} %bitcast_add_fusion.2), channel_id=1, source_target_pairs={{0,4},{5,1},{4,8},{9,5},{8,12},{13,9},{12,14},{15,13},{14,10},{11,... | collective-permute-start | bytes 2408456 | tf_op jit(solution)/shard_map/ppermute | solution.py:131
  128.2 12.2 %collective-permute-start.6 = (f32[16,12544]{1,0:T(8,128)S(1)}, f32[16,12544]{1,0:T(8,128)S(1)}, u32[]{:S(2)}, u32[]{:S(2)}) collective-permute-start(f32[16,12544]{1,0:T(8,128)S(1)} %bitcast_add_fusion.1), channel_id=1, source_target_pairs={{0,4},{5,1},{4,8},{9,5},{8,12},{13,9},{12,14},{15,13},{14,10},{11,... | collective-permute-start | bytes 2408456 | tf_op jit(solution)/shard_map/ppermute | solution.py:131
  143.9 5.4 %collective-permute-start.7 = (f32[16,1024]{1,0:T(8,128)S(1)}, f32[16,1024]{1,0:T(8,128)S(1)}, u32[]{:S(2)}, u32[]{:S(2)}) collective-permute-start(f32[16,1024]{1,0:T(8,128)S(1)} %reshape.29), channel_id=1, source_target_pairs={{0,8},{1,9},{2,10},{3,11},{4,12},{5,13},{6,14},{7,15},{8,0},{9,1},... | collective-permute-start | bytes 196616 | tf_op jit(solution)/shard_map/ppermute | solution.py:143
  149.3 5.0 %collective-permute-start.8 = (f32[32,1024]{1,0:T(8,128)S(1)}, f32[32,1024]{1,0:T(8,128)S(1)}, u32[]{:S(2)}, u32[]{:S(2)}) collective-permute-start(f32[32,1024]{1,0:T(8,128)S(1)} %pad_maximum_fusion.3), channel_id=1, source_target_pairs={{0,4},{1,5},{2,6},{3,7},{4,0},{5,1},{6,2},{7,3},{8,12},{9,13},{10,... | collective-permute-start | bytes 393224 | tf_op jit(solution)/shard_map/ppermute | solution.py:143
  154.4 6.4 %collective-permute-start.9 = (f32[64,1024]{1,0:T(8,128)S(1)}, f32[64,1024]{1,0:T(8,128)S(1)}, u32[]{:S(2)}, u32[]{:S(2)}) collective-permute-start(f32[64,1024]{1,0:T(8,128)S(1)} %pad_maximum_fusion.2), channel_id=1, source_target_pairs={{0,2},{1,3},{2,0},{3,1},{4,6},{5,7},{6,4},{7,5},{8,10},{9,11},{10,... | collective-permute-start | bytes 786440 | tf_op jit(solution)/shard_map/ppermute | solution.py:143
  160.9 2.0 collective-permute-start.10
  168.5 106.1 %copy-start.1 = (bf16[128,32,196]{0,1,2:T(8,128)(2,1)S(1)}, bf16[128,32,196]{0,1,2:T(8,128)(2,1)}, u32[]{:S(2)}) copy-start(bf16[128,32,196]{0,1,2:T(8,128)(2,1)} %param.7) | copy-start | bytes 4816900

commit v9 on v8

--- a/solution.py
+++ b/solution.py
@@ -150,9 +150,11 @@
     samples = images.shape[0]
     in_part, out_part = project(images, out_grads, in_signs, out_signs)
     width_in = in_part.shape[1]
-    both = jnp.concatenate([in_part, out_part], axis=1).reshape(samples, -1)
+    cells = in_part.shape[2]
+    both = jnp.concatenate([jnp.transpose(in_part, (2, 1, 0)), jnp.transpose(out_part, (2, 1, 0))], axis=1)
+    both = both.reshape(-1, samples).T
     both = ring_reduce_scatter(both, "chan", "samp")
-    both = both.reshape(both.shape[0], -1, in_part.shape[2])
+    both = jnp.transpose(both.reshape(both.shape[0], cells, -1), (0, 2, 1))
     in_sum = both[:, :width_in]
     out_sum = both[:, width_in:]
     own = sketch(in_sum, out_sum, C)

time: 276 us -> 269 us (0.975)
  local copies, waits for them, and re-layouts: 32.9 us -> 24.6 us
    reshape x1 -> x3, local copies, waits for them, and re-layouts: 1.51 us -> 11.2 us  [the longest x1 8.05 us: local(): both = both.reshape(-1, samples).T]
    concatenate x1 -> x0, local copies, waits for them, and re-layouts: 9.06 us -> none  [local(): both = jnp.concatenate([in_part, out_part], axis=1).reshape(samples, -1)]
    another operation x1 -> x0, local copies, waits for them, and re-layouts: 8.95 us -> none  [ring_reduce_scatter(): blocks = x.reshape(n, -1, x.shape[-1])]
    unnamed x13 -> x11, local copies, waits for them, and re-layouts: 7.25 us -> 7.24 us
where the time goes in v9:
time: 269 us; the launch traced here: 268 us
  Pallas kernels  105 us (39%)
  waiting for transfers between devices  68.3 us (25%)
  local copies, waits for them, and re-layouts  24.6 us (9%)
  starting transfers between devices  23 us (9%)
  between operations  21.2 us (8%)
  matrix products  13 us (5%)
  other arithmetic  12.9 us (5%)
    pallas_call x1, Pallas kernels, cholesky_upper(): pl.pallas_call(functools.partial(_chol_kernel, nb=nb, b=b), out_shape=jax...  105 us
    ppermute x7, waiting for transfers between devices, ring_reduce_scatter(): acc = lax.ppermute(acc, (axis, pair), ring) + take(step)  57.4 us
    ppermute x7, starting transfers between devices, ring_reduce_scatter(): acc = lax.ppermute(acc, (axis, pair), ring) + take(step)  15.9 us
    ppermute x4, waiting for transfers between devices, doubling_gather(): other = lax.ppermute(x, axes, [(i, i ^ k) for i in range(size)])  10.9 us
    add x7, other arithmetic, ring_reduce_scatter(): acc = lax.ppermute(acc, (axis, pair), ring) + take(step)  9.45 us
    reshape x1, local copies, waits for them, and re-layouts, local(): both = both.reshape(-1, samples).T  8.05 us
    unnamed x11, local copies, waits for them, and re-layouts  7.24 us
    ppermute x4, starting transfers between devices, doubling_gather(): other = lax.ppermute(x, axes, [(i, i ^ k) for i in range(size)])  7.11 us
  transfers between devices with their start and end apart: 11, of which 11 were waited for; matrix products, arithmetic and copies ran while one was open for 0% of the time, Pallas kernels for 0%

profile of v9, /device:TPU:0, one launch (start us, length us, event | category | flops | bytes accessed | tf_op | source)
XLA Modules:
  0.0 268.0 jit_solution(7247814714907928438)
XLA Ops:
  0.6 0.0 copy-start
  0.6 1.4 dynamic_slice.55
  7.3 1.7 fusion.10
  10.2 0.0 copy-start.1
  10.3 7.2 %copy.11 = bf16[128,32,784]{0,1,2:T(8,128)(2,1)} copy(bf16[128,32,784]{0,2,1:T(8,128)(2,1)} %param.6) | data formatting | bytes 12845056 | tf_op args[0]
  17.4 0.1 copy.17
  17.6 4.8 %fusion.11 = f32[128,32,14,14]{0,1,3,2:T(8,128)S(1)} fusion(bf16[128,32,28,28]{0,1,3,2:T(8,128)(2,1)} %bitcast.58, bf16[32,3,3,32]{0,3,2,1:T(8,128)(2,1)S(1)} %bitcast.61), kind=kOutput, calls=%fused_computation.36 | convolution fusion | flops 440664064 | bytes 9652224 | tf_op jit(solution)/shard_map/conv_general_dilated | solution.py:82
  22.4 0.6 convolution_bitcast_fusion
  23.0 3.4 %pad_maximum_fusion = f32[196,64,128]{2,1,0:T(8,128)} fusion(f32[196,32,128]{2,1,0:T(8,128)S(1)} %convolution_bitcast_fusion, f32[196,32,128]{2,1,0:T(8,128)S(1)} %bitcast.60), kind=kLoop, calls=%fused_computation | loop fusion | flops 1605632 | bytes 12845056 | tf_op jit(solution)/shard_map/concatenate | solution.py:154
  26.4 8.1 %copy.14 = f32[12544,128]{0,1:T(8,128)} copy(f32[12544,128]{1,0:T(8,128)} %bitcast.56) | data formatting | bytes 12845056 | tf_op jit(solution)/shard_map/reshape | solution.py:155
  35.1 1.2 dynamic-slice_bitcast_fusion
  36.3 3.1 %collective-permute-start = (f32[16,12544]{1,0:T(8,128)S(1)}, f32[16,12544]{1,0:T(8,128)S(1)}, u32[]{:S(2)}, u32[]{:S(2)}) collective-permute-start(f32[16,12544]{1,0:T(8,128)S(1)} %dynamic-slice_bitcast_fusion), channel_id=1, source_target_pairs={{0,4},{5,1},{4,8},{9,5},{8,12},{13,9},{12,14},{15,13},{14,10},{11,... | collective-permute-start | bytes 2408456 | tf_op jit(solution)/shard_map/ppermute | solution.py:131
  41.2 8.2 %collective-permute-done = f32[16,12544]{1,0:T(8,128)S(1)} collective-permute-done((f32[16,12544]{1,0:T(8,128)S(1)}, f32[16,12544]{1,0:T(8,128)S(1)}, u32[]{:S(2)}, u32[]{:S(2)}) %collective-permute-start) | collective-permute-done | bytes 802848 | tf_op jit(solution)/shard_map/ppermute | solution.py:131
  49.4 1.2 bitcast_add_fusion.6
  50.7 2.1 collective-permute-start.1
  54.5 8.4 %collective-permute-done.1 = f32[16,12544]{1,0:T(8,128)S(1)} collective-permute-done((f32[16,12544]{1,0:T(8,128)S(1)}, f32[16,12544]{1,0:T(8,128)S(1)}, u32[]{:S(2)}, u32[]{:S(2)}) %collective-permute-start.1) | collective-permute-done | bytes 802848 | tf_op jit(solution)/shard_map/ppermute | solution.py:131
  62.9 1.2 bitcast_add_fusion.5
  64.1 2.1 collective-permute-start.2
  68.1 8.3 %collective-permute-done.2 = f32[16,12544]{1,0:T(8,128)S(1)} collective-permute-done((f32[16,12544]{1,0:T(8,128)S(1)}, f32[16,12544]{1,0:T(8,128)S(1)}, u32[]{:S(2)}, u32[]{:S(2)}) %collective-permute-start.2) | collective-permute-done | bytes 802848 | tf_op jit(solution)/shard_map/ppermute | solution.py:131
  76.3 1.2 bitcast_add_fusion.4
  77.5 2.1 collective-permute-start.3
  81.5 8.2 %collective-permute-done.3 = f32[16,12544]{1,0:T(8,128)S(1)} collective-permute-done((f32[16,12544]{1,0:T(8,128)S(1)}, f32[16,12544]{1,0:T(8,128)S(1)}, u32[]{:S(2)}, u32[]{:S(2)}) %collective-permute-start.3) | collective-permute-done | bytes 802848 | tf_op jit(solution)/shard_map/ppermute | solution.py:131
  89.8 1.2 bitcast_add_fusion.3
  91.0 2.1 collective-permute-start.4
  95.1 8.1 %collective-permute-done.4 = f32[16,12544]{1,0:T(8,128)S(1)} collective-permute-done((f32[16,12544]{1,0:T(8,128)S(1)}, f32[16,12544]{1,0:T(8,128)S(1)}, u32[]{:S(2)}, u32[]{:S(2)}) %collective-permute-start.4) | collective-permute-done | bytes 802848 | tf_op jit(solution)/shard_map/ppermute | solution.py:131
  103.2 1.2 bitcast_add_fusion.2
  104.4 2.1 collective-permute-start.5
  108.6 8.0 %collective-permute-done.5 = f32[16,12544]{1,0:T(8,128)S(1)} collective-permute-done((f32[16,12544]{1,0:T(8,128)S(1)}, f32[16,12544]{1,0:T(8,128)S(1)}, u32[]{:S(2)}, u32[]{:S(2)}) %collective-permute-start.5) | collective-permute-done | bytes 802848 | tf_op jit(solution)/shard_map/ppermute | solution.py:131
  116.7 1.2 bitcast_add_fusion.1
  117.9 2.1 collective-permute-start.6
  122.0 8.1 %collective-permute-done.6 = f32[16,12544]{1,0:T(8,128)S(1)} collective-permute-done((f32[16,12544]{1,0:T(8,128)S(1)}, f32[16,12544]{1,0:T(8,128)S(1)}, u32[]{:S(2)}, u32[]{:S(2)}) %collective-permute-start.6) | collective-permute-done | bytes 802848 | tf_op jit(solution)/shard_map/ppermute | solution.py:131
  130.1 2.1 bitcast_add_fusion
  132.2 1.6 reshape.36
  133.8 1.6 copy.15
  135.4 1.9 convolution_multiply_fusion
  137.2 0.1 reshape.37
  137.4 3.2 %collective-permute-start.7 = (f32[16,1024]{1,0:T(8,128)S(1)}, f32[16,1024]{1,0:T(8,128)S(1)}, u32[]{:S(2)}, u32[]{:S(2)}) collective-permute-start(f32[16,1024]{1,0:T(8,128)S(1)} %reshape.37), channel_id=1, source_target_pairs={{0,8},{1,9},{2,10},{3,11},{4,12},{5,13},{6,14},{7,15},{8,0},{9,1},... | collective-permute-start | bytes 196616 | tf_op jit(solution)/shard_map/ppermute | solution.py:143
  140.5 2.2 collective-permute-done.7
  142.8 2.0 collective-permute-start.8
  144.8 3.1 %collective-permute-done.8 = f32[32,1024]{1,0:T(8,128)S(1)} collective-permute-done((f32[32,1024]{1,0:T(8,128)S(1)}, f32[32,1024]{1,0:T(8,128)S(1)}, u32[]{:S(2)}, u32[]{:S(2)}) %collective-permute-start.8) | collective-permute-done | bytes 131104 | tf_op jit(solution)/shard_map/ppermute | solution.py:143
  147.8 1.9 collective-permute-start.9
  149.8 4.5 %collective-permute-done.9 = f32[64,1024]{1,0:T(8,128)S(1)} collective-permute-done((f32[64,1024]{1,0:T(8,128)S(1)}, f32[64,1024]{1,0:T(8,128)S(1)}, u32[]{:S(2)}, u32[]{:S(2)}) %collective-permute-start.9) | collective-permute-done | bytes 262176 | tf_op jit(solution)/shard_map/ppermute | solution.py:143
  154.3 0.1 collective-permute-start.10
  154.4 0.8 broadcast_in_dim_reshape.3
  155.3 1.1 collective-permute-done.10
  156.4 5.7 %convert_add_fusion = f32[1024,1024]{1,0:T(8,128)} fusion(f32[256,1024]{1,0:T(8,128)S(1)} %constant_dynamic-update-slice_fusion), kind=kOutput, calls=%fused_computation.1 | convolution fusion | flops 3225419776 | bytes 5242880 | tf_op jit(solution)/shard_map/nk,nm->km/dot_general | solution.py:165
  162.0 105.1 %shard_map.77 = f32[8,128,1024]{2,1,0:T(8,128)S(1)} custom-call(f32[8,128,1024]{2,1,0:T(8,128)} %bitcast.57), custom_call_target="tpu_custom_call" | custom-call | tf_op jit(solution)/shard_map/pallas_call | solution.py:63
  267.2 0.8 constant_dynamic-slice_fusion
  (13 shorter events, 0.2 us)
Async XLA Ops:
  0.6 21.8 %copy-start = (bf16[128,32,196]{0,1,2:T(8,128)(2,1)S(1)}, bf16[128,32,196]{0,1,2:T(8,128)(2,1)}, u32[]{:S(2)}) copy-start(bf16[128,32,196]{0,1,2:T(8,128)(2,1)} %param.7) | copy-start | bytes 4816900
  10.2 7.2 %copy-start.1 = (s32[32,288]{1,0:T(8,128)S(1)}, s32[32,288]{1,0:T(8,128)}, u32[]{:S(2)}) copy-start(s32[32,288]{1,0:T(8,128)} %param.8) | copy-start | bytes 110596
  17.6 4.8 %copy-start.2 = (s32[32,32]{1,0:T(8,128)S(1)}, s32[32,32]{1,0:T(8,128)}, u32[]{:S(2)}) copy-start(s32[32,32]{1,0:T(8,128)} %param.9) | copy-start | bytes 12292
  36.3 13.2 %collective-permute-start = (f32[16,12544]{1,0:T(8,128)S(1)}, f32[16,12544]{1,0:T(8,128)S(1)}, u32[]{:S(2)}, u32[]{:S(2)}) collective-permute-start(f32[16,12544]{1,0:T(8,128)S(1)} %dynamic-slice_bitcast_fusion), channel_id=1, source_target_pairs={{0,4},{5,1},{4,8},{9,5},{8,12},{13,9},{12,14},{15,13},{14,10},{11,... | collective-permute-start | bytes 2408456 | tf_op jit(solution)/shard_map/ppermute | solution.py:131
  50.7 12.2 %collective-permute-start.1 = (f32[16,12544]{1,0:T(8,128)S(1)}, f32[16,12544]{1,0:T(8,128)S(1)}, u32[]{:S(2)}, u32[]{:S(2)}) collective-permute-start(f32[16,12544]{1,0:T(8,128)S(1)} %bitcast_add_fusion.6), channel_id=1, source_target_pairs={{0,4},{5,1},{4,8},{9,5},{8,12},{13,9},{12,14},{15,13},{14,10},{11,... | collective-permute-start | bytes 2408456 | tf_op jit(solution)/shard_map/ppermute | solution.py:131
  64.1 12.2 %collective-permute-start.2 = (f32[16,12544]{1,0:T(8,128)S(1)}, f32[16,12544]{1,0:T(8,128)S(1)}, u32[]{:S(2)}, u32[]{:S(2)}) collective-permute-start(f32[16,12544]{1,0:T(8,128)S(1)} %bitcast_add_fusion.5), channel_id=1, source_target_pairs={{0,4},{5,1},{4,8},{9,5},{8,12},{13,9},{12,14},{15,13},{14,10},{11,... | collective-permute-start | bytes 2408456 | tf_op jit(solution)/shard_map/ppermute | solution.py:131
  77.5 12.2 %collective-permute-start.3 = (f32[16,12544]{1,0:T(8,128)S(1)}, f32[16,12544]{1,0:T(8,128)S(1)}, u32[]{:S(2)}, u32[]{:S(2)}) collective-permute-start(f32[16,12544]{1,0:T(8,128)S(1)} %bitcast_add_fusion.4), channel_id=1, source_target_pairs={{0,4},{5,1},{4,8},{9,5},{8,12},{13,9},{12,14},{15,13},{14,10},{11,... | collective-permute-start | bytes 2408456 | tf_op jit(solution)/shard_map/ppermute | solution.py:131
  91.0 12.2 %collective-permute-start.4 = (f32[16,12544]{1,0:T(8,128)S(1)}, f32[16,12544]{1,0:T(8,128)S(1)}, u32[]{:S(2)}, u32[]{:S(2)}) collective-permute-start(f32[16,12544]{1,0:T(8,128)S(1)} %bitcast_add_fusion.3), channel_id=1, source_target_pairs={{0,4},{5,1},{4,8},{9,5},{8,12},{13,9},{12,14},{15,13},{14,10},{11,... | collective-permute-start | bytes 2408456 | tf_op jit(solution)/shard_map/ppermute | solution.py:131
  104.4 12.2 %collective-permute-start.5 = (f32[16,12544]{1,0:T(8,128)S(1)}, f32[16,12544]{1,0:T(8,128)S(1)}, u32[]{:S(2)}, u32[]{:S(2)}) collective-permute-start(f32[16,12544]{1,0:T(8,128)S(1)} %bitcast_add_fusion.2), channel_id=1, source_target_pairs={{0,4},{5,1},{4,8},{9,5},{8,12},{13,9},{12,14},{15,13},{14,10},{11,... | collective-permute-start | bytes 2408456 | tf_op jit(solution)/shard_map/ppermute | solution.py:131
  117.9 12.2 %collective-permute-start.6 = (f32[16,12544]{1,0:T(8,128)S(1)}, f32[16,12544]{1,0:T(8,128)S(1)}, u32[]{:S(2)}, u32[]{:S(2)}) collective-permute-start(f32[16,12544]{1,0:T(8,128)S(1)} %bitcast_add_fusion.1), channel_id=1, source_target_pairs={{0,4},{5,1},{4,8},{9,5},{8,12},{13,9},{12,14},{15,13},{14,10},{11,... | collective-permute-start | bytes 2408456 | tf_op jit(solution)/shard_map/ppermute | solution.py:131
  137.4 5.4 %collective-permute-start.7 = (f32[16,1024]{1,0:T(8,128)S(1)}, f32[16,1024]{1,0:T(8,128)S(1)}, u32[]{:S(2)}, u32[]{:S(2)}) collective-permute-start(f32[16,1024]{1,0:T(8,128)S(1)} %reshape.37), channel_id=1, source_target_pairs={{0,8},{1,9},{2,10},{3,11},{4,12},{5,13},{6,14},{7,15},{8,0},{9,1},... | collective-permute-start | bytes 196616 | tf_op jit(solution)/shard_map/ppermute | solution.py:143
  142.8 5.0 %collective-permute-start.8 = (f32[32,1024]{1,0:T(8,128)S(1)}, f32[32,1024]{1,0:T(8,128)S(1)}, u32[]{:S(2)}, u32[]{:S(2)}) collective-permute-start(f32[32,1024]{1,0:T(8,128)S(1)} %pad_maximum_fusion.3), channel_id=1, source_target_pairs={{0,4},{1,5},{2,6},{3,7},{4,0},{5,1},{6,2},{7,3},{8,12},{9,13},{10,... | collective-permute-start | bytes 393224 | tf_op jit(solution)/shard_map/ppermute | solution.py:143
  147.8 6.4 %collective-permute-start.9 = (f32[64,1024]{1,0:T(8,128)S(1)}, f32[64,1024]{1,0:T(8,128)S(1)}, u32[]{:S(2)}, u32[]{:S(2)}) collective-permute-start(f32[64,1024]{1,0:T(8,128)S(1)} %pad_maximum_fusion.2), channel_id=1, source_target_pairs={{0,2},{1,3},{2,0},{3,1},{4,6},{5,7},{6,4},{7,5},{8,10},{9,11},{10,... | collective-permute-start | bytes 786440 | tf_op jit(solution)/shard_map/ppermute | solution.py:143
  154.3 2.0 collective-permute-start.10

commit v10 on v9

--- a/solution.py
+++ b/solution.py
@@ -25,9 +25,15 @@
     return x[:, :b], x[:, b:]
 
 
-def _chol_kernel(a_ref, r_ref, w_ref, *, nb, b):
+def _chol_kernel(f_ref, r_ref, w_ref, *, nb, b, scale):
     n = nb * b
-    w_ref[...] = a_ref[...]
+    f = f_ref[...]
+    eye = jnp.eye(b, dtype=jnp.float32)
+    for i in range(nb):
+        g = lax.dot_general(f[:, i * b:(i + 1) * b], f, (((0,), (0,)), ((), ())), precision=HI,
+                            preferred_element_type=jnp.float32) * scale
+        w_ref[i] = g
+        w_ref[i, :, i * b:(i + 1) * b] = g[:, i * b:(i + 1) * b] + eye
 
     def step(k, carry):
         wk = w_ref[k]
@@ -56,19 +62,18 @@
     lax.fori_loop(0, nb, step, 0)
 
 
-def cholesky_upper(a, b=128, interpret=False):
-    n = a.shape[0]
+def damped_cholesky(f, scale, b=128, interpret=False):
+    n = f.shape[1]
     nb = n // b
-    a3 = a.reshape(nb, b, n)
     out = pl.pallas_call(
-        functools.partial(_chol_kernel, nb=nb, b=b),
+        functools.partial(_chol_kernel, nb=nb, b=b, scale=scale),
         out_shape=jax.ShapeDtypeStruct((nb, b, n), jnp.float32),
         in_specs=[pl.BlockSpec(memory_space=pltpu.VMEM)],
         out_specs=pl.BlockSpec(memory_space=pltpu.VMEM),
         scratch_shapes=[pltpu.VMEM((nb, b, n), jnp.float32)],
         compiler_params=pltpu.CompilerParams(vmem_limit_bytes=48 * 1024 * 1024),
         interpret=interpret,
-    )(a3)
+    )(f)
     return out.reshape(n, n)
 
 
@@ -161,9 +166,7 @@
     every = doubling_gather(own, ("chan", "samp"))
     batch_total = samples * lax.axis_size("samp")
     width = every.shape[1]
-    identity_mat = jnp.eye(width, dtype=jnp.float32)
-    gram = jnp.einsum("nk,nm->km", every, every, precision=lax.Precision.HIGHEST) / batch_total
-    factor = cholesky_upper(gram + identity_mat)
+    factor = damped_cholesky(every, 1.0 / batch_total)
     chan_count = lax.axis_size("chan")
     rows_here = width // chan_count
     r_rows = lax.dynamic_slice_in_dim(factor, lax.axis_index("chan") * rows_here, rows_here, 0)

time: 269 us -> 265 us (0.985)
  matrix products: 13 us -> 7.26 us
    dot_general x1 -> x0, matrix products: 5.69 us -> none  [local(): jnp.einsum('nk,nm->km', every, every, precision=lax.Precision.HIGHEST)]
where the time goes in v10:
time: 265 us; the launch traced here: 264 us
  Pallas kernels  107 us (40%)
  waiting for transfers between devices  68.2 us (26%)
  local copies, waits for them, and re-layouts  24.6 us (9%)
  starting transfers between devices  23.2 us (9%)
  between operations  21.2 us (8%)
  other arithmetic  12.9 us (5%)
  matrix products  7.26 us (3%)
    pallas_call x1, Pallas kernels, damped_cholesky(): pl.pallas_call(functools.partial(_chol_kernel, nb=nb, b=b, scale=scale),...  107 us
    ppermute x7, waiting for transfers between devices, ring_reduce_scatter(): acc = lax.ppermute(acc, (axis, pair), ring) + take(step)  57.3 us
    ppermute x7, starting transfers between devices, ring_reduce_scatter(): acc = lax.ppermute(acc, (axis, pair), ring) + take(step)  16.1 us
    ppermute x4, waiting for transfers between devices, doubling_gather(): other = lax.ppermute(x, axes, [(i, i ^ k) for i in range(size)])  10.9 us
    add x7, other arithmetic, ring_reduce_scatter(): acc = lax.ppermute(acc, (axis, pair), ring) + take(step)  9.45 us
    reshape x1, local copies, waits for them, and re-layouts, local(): both = both.reshape(-1, samples).T  8.05 us
    unnamed x11, local copies, waits for them, and re-layouts  7.24 us
    ppermute x4, starting transfers between devices, doubling_gather(): other = lax.ppermute(x, axes, [(i, i ^ k) for i in range(size)])  7.11 us
  transfers between devices with their start and end apart: 11, of which 11 were waited for; matrix products, arithmetic and copies ran while one was open for 0% of the time, Pallas kernels for 0%

profile of v10, /device:TPU:0, one launch (start us, length us, event | category | flops | bytes accessed | tf_op | source)
XLA Modules:
  0.0 263.9 jit_solution(13190161683506331488)
XLA Ops:
  0.6 0.0 copy-start
  0.6 1.4 dynamic_slice.55
  7.3 1.7 fusion.10
  10.2 0.0 copy-start.1
  10.3 7.2 %copy.11 = bf16[128,32,784]{0,1,2:T(8,128)(2,1)} copy(bf16[128,32,784]{0,2,1:T(8,128)(2,1)} %param.6) | data formatting | bytes 12845056 | tf_op args[0]
  17.4 0.0 copy-done.1
  17.5 0.1 copy.17
  17.6 4.8 %fusion.11 = f32[128,32,14,14]{0,1,3,2:T(8,128)S(1)} fusion(bf16[128,32,28,28]{0,1,3,2:T(8,128)(2,1)} %bitcast.54, bf16[32,3,3,32]{0,3,2,1:T(8,128)(2,1)S(1)} %bitcast.57), kind=kOutput, calls=%fused_computation.34 | convolution fusion | flops 440664064 | bytes 9652224 | tf_op jit(solution)/shard_map/conv_general_dilated | solution.py:87
  22.4 0.6 convolution_bitcast_fusion
  23.0 3.4 %pad_maximum_fusion = f32[196,64,128]{2,1,0:T(8,128)} fusion(f32[196,32,128]{2,1,0:T(8,128)S(1)} %convolution_bitcast_fusion, f32[196,32,128]{2,1,0:T(8,128)S(1)} %bitcast.56), kind=kLoop, calls=%fused_computation | loop fusion | flops 1605632 | bytes 12845056 | tf_op jit(solution)/shard_map/concatenate | solution.py:159
  26.4 8.1 %copy.14 = f32[12544,128]{0,1:T(8,128)} copy(f32[12544,128]{1,0:T(8,128)} %bitcast.53) | data formatting | bytes 12845056 | tf_op jit(solution)/shard_map/reshape | solution.py:160
  35.1 1.2 dynamic-slice_bitcast_fusion
  36.3 3.1 %collective-permute-start = (f32[16,12544]{1,0:T(8,128)S(1)}, f32[16,12544]{1,0:T(8,128)S(1)}, u32[]{:S(2)}, u32[]{:S(2)}) collective-permute-start(f32[16,12544]{1,0:T(8,128)S(1)} %dynamic-slice_bitcast_fusion), channel_id=1, source_target_pairs={{0,4},{5,1},{4,8},{9,5},{8,12},{13,9},{12,14},{15,13},{14,10},{11,... | collective-permute-start | bytes 2408456 | tf_op jit(solution)/shard_map/ppermute | solution.py:136
  41.2 8.2 %collective-permute-done = f32[16,12544]{1,0:T(8,128)S(1)} collective-permute-done((f32[16,12544]{1,0:T(8,128)S(1)}, f32[16,12544]{1,0:T(8,128)S(1)}, u32[]{:S(2)}, u32[]{:S(2)}) %collective-permute-start) | collective-permute-done | bytes 802848 | tf_op jit(solution)/shard_map/ppermute | solution.py:136
  49.4 1.2 bitcast_add_fusion.6
  50.7 2.1 collective-permute-start.1
  54.5 8.4 %collective-permute-done.1 = f32[16,12544]{1,0:T(8,128)S(1)} collective-permute-done((f32[16,12544]{1,0:T(8,128)S(1)}, f32[16,12544]{1,0:T(8,128)S(1)}, u32[]{:S(2)}, u32[]{:S(2)}) %collective-permute-start.1) | collective-permute-done | bytes 802848 | tf_op jit(solution)/shard_map/ppermute | solution.py:136
  62.9 1.2 bitcast_add_fusion.5
  64.1 2.1 collective-permute-start.2
  68.1 8.2 %collective-permute-done.2 = f32[16,12544]{1,0:T(8,128)S(1)} collective-permute-done((f32[16,12544]{1,0:T(8,128)S(1)}, f32[16,12544]{1,0:T(8,128)S(1)}, u32[]{:S(2)}, u32[]{:S(2)}) %collective-permute-start.2) | collective-permute-done | bytes 802848 | tf_op jit(solution)/shard_map/ppermute | solution.py:136
  76.3 1.2 bitcast_add_fusion.4
  77.5 2.1 collective-permute-start.3
  81.5 8.2 %collective-permute-done.3 = f32[16,12544]{1,0:T(8,128)S(1)} collective-permute-done((f32[16,12544]{1,0:T(8,128)S(1)}, f32[16,12544]{1,0:T(8,128)S(1)}, u32[]{:S(2)}, u32[]{:S(2)}) %collective-permute-start.3) | collective-permute-done | bytes 802848 | tf_op jit(solution)/shard_map/ppermute | solution.py:136
  89.8 1.2 bitcast_add_fusion.3
  91.0 2.1 collective-permute-start.4
  95.1 8.1 %collective-permute-done.4 = f32[16,12544]{1,0:T(8,128)S(1)} collective-permute-done((f32[16,12544]{1,0:T(8,128)S(1)}, f32[16,12544]{1,0:T(8,128)S(1)}, u32[]{:S(2)}, u32[]{:S(2)}) %collective-permute-start.4) | collective-permute-done | bytes 802848 | tf_op jit(solution)/shard_map/ppermute | solution.py:136
  103.2 1.2 bitcast_add_fusion.2
  104.4 2.1 collective-permute-start.5
  108.6 8.0 %collective-permute-done.5 = f32[16,12544]{1,0:T(8,128)S(1)} collective-permute-done((f32[16,12544]{1,0:T(8,128)S(1)}, f32[16,12544]{1,0:T(8,128)S(1)}, u32[]{:S(2)}, u32[]{:S(2)}) %collective-permute-start.5) | collective-permute-done | bytes 802848 | tf_op jit(solution)/shard_map/ppermute | solution.py:136
  116.6 1.2 bitcast_add_fusion.1
  117.9 2.3 collective-permute-start.6
  122.1 8.1 %collective-permute-done.6 = f32[16,12544]{1,0:T(8,128)S(1)} collective-permute-done((f32[16,12544]{1,0:T(8,128)S(1)}, f32[16,12544]{1,0:T(8,128)S(1)}, u32[]{:S(2)}, u32[]{:S(2)}) %collective-permute-start.6) | collective-permute-done | bytes 802848 | tf_op jit(solution)/shard_map/ppermute | solution.py:136
  130.3 2.1 bitcast_add_fusion
  132.4 1.6 reshape.33
  134.0 1.6 copy.15
  135.5 1.9 convolution_multiply_fusion
  137.4 0.1 reshape.34
  137.5 3.2 %collective-permute-start.7 = (f32[16,1024]{1,0:T(8,128)S(1)}, f32[16,1024]{1,0:T(8,128)S(1)}, u32[]{:S(2)}, u32[]{:S(2)}) collective-permute-start(f32[16,1024]{1,0:T(8,128)S(1)} %reshape.34), channel_id=1, source_target_pairs={{0,8},{1,9},{2,10},{3,11},{4,12},{5,13},{6,14},{7,15},{8,0},{9,1},... | collective-permute-start | bytes 196616 | tf_op jit(solution)/shard_map/ppermute | solution.py:148
  140.7 2.2 collective-permute-done.7
  143.0 2.0 collective-permute-start.8
  144.9 3.1 %collective-permute-done.8 = f32[32,1024]{1,0:T(8,128)S(1)} collective-permute-done((f32[32,1024]{1,0:T(8,128)S(1)}, f32[32,1024]{1,0:T(8,128)S(1)}, u32[]{:S(2)}, u32[]{:S(2)}) %collective-permute-start.8) | collective-permute-done | bytes 131104 | tf_op jit(solution)/shard_map/ppermute | solution.py:148
  148.0 1.9 collective-permute-start.9
  149.9 4.5 %collective-permute-done.9 = f32[64,1024]{1,0:T(8,128)S(1)} collective-permute-done((f32[64,1024]{1,0:T(8,128)S(1)}, f32[64,1024]{1,0:T(8,128)S(1)}, u32[]{:S(2)}, u32[]{:S(2)}) %collective-permute-start.9) | collective-permute-done | bytes 262176 | tf_op jit(solution)/shard_map/ppermute | solution.py:148
  154.5 0.1 collective-permute-start.10
  154.6 0.8 broadcast_in_dim_reshape.3
  155.4 1.1 collective-permute-done.10
  156.5 106.5 %shard_map.77 = f32[8,128,1024]{2,1,0:T(8,128)S(1)} custom-call(f32[256,1024]{1,0:T(8,128)S(1)} %constant_dynamic-update-slice_fusion.f_ref), custom_call_target="tpu_custom_call" | custom-call | tf_op jit(solution)/shard_map/pallas_call | solution.py:68
  263.1 0.8 constant_dynamic-slice_fusion
  (12 shorter events, 0.2 us)
Async XLA Ops:
  0.6 21.8 %copy-start = (bf16[128,32,196]{0,1,2:T(8,128)(2,1)S(1)}, bf16[128,32,196]{0,1,2:T(8,128)(2,1)}, u32[]{:S(2)}) copy-start(bf16[128,32,196]{0,1,2:T(8,128)(2,1)} %param.7) | copy-start | bytes 4816900
  10.2 7.2 %copy-start.1 = (s32[32,288]{1,0:T(8,128)S(1)}, s32[32,288]{1,0:T(8,128)}, u32[]{:S(2)}) copy-start(s32[32,288]{1,0:T(8,128)} %param.8) | copy-start | bytes 110596
  17.4 5.0 %copy-start.2 = (s32[32,32]{1,0:T(8,128)S(1)}, s32[32,32]{1,0:T(8,128)}, u32[]{:S(2)}) copy-start(s32[32,32]{1,0:T(8,128)} %param.9) | copy-start | bytes 12292
  36.3 13.2 %collective-permute-start = (f32[16,12544]{1,0:T(8,128)S(1)}, f32[16,12544]{1,0:T(8,128)S(1)}, u32[]{:S(2)}, u32[]{:S(2)}) collective-permute-start(f32[16,12544]{1,0:T(8,128)S(1)} %dynamic-slice_bitcast_fusion), channel_id=1, source_target_pairs={{0,4},{5,1},{4,8},{9,5},{8,12},{13,9},{12,14},{15,13},{14,10},{11,... | collective-permute-start | bytes 2408456 | tf_op jit(solution)/shard_map/ppermute | solution.py:136
  50.7 12.2 %collective-permute-start.1 = (f32[16,12544]{1,0:T(8,128)S(1)}, f32[16,12544]{1,0:T(8,128)S(1)}, u32[]{:S(2)}, u32[]{:S(2)}) collective-permute-start(f32[16,12544]{1,0:T(8,128)S(1)} %bitcast_add_fusion.6), channel_id=1, source_target_pairs={{0,4},{5,1},{4,8},{9,5},{8,12},{13,9},{12,14},{15,13},{14,10},{11,... | collective-permute-start | bytes 2408456 | tf_op jit(solution)/shard_map/ppermute | solution.py:136
  64.1 12.2 %collective-permute-start.2 = (f32[16,12544]{1,0:T(8,128)S(1)}, f32[16,12544]{1,0:T(8,128)S(1)}, u32[]{:S(2)}, u32[]{:S(2)}) collective-permute-start(f32[16,12544]{1,0:T(8,128)S(1)} %bitcast_add_fusion.5), channel_id=1, source_target_pairs={{0,4},{5,1},{4,8},{9,5},{8,12},{13,9},{12,14},{15,13},{14,10},{11,... | collective-permute-start | bytes 2408456 | tf_op jit(solution)/shard_map/ppermute | solution.py:136
  77.5 12.2 %collective-permute-start.3 = (f32[16,12544]{1,0:T(8,128)S(1)}, f32[16,12544]{1,0:T(8,128)S(1)}, u32[]{:S(2)}, u32[]{:S(2)}) collective-permute-start(f32[16,12544]{1,0:T(8,128)S(1)} %bitcast_add_fusion.4), channel_id=1, source_target_pairs={{0,4},{5,1},{4,8},{9,5},{8,12},{13,9},{12,14},{15,13},{14,10},{11,... | collective-permute-start | bytes 2408456 | tf_op jit(solution)/shard_map/ppermute | solution.py:136
  91.0 12.2 %collective-permute-start.4 = (f32[16,12544]{1,0:T(8,128)S(1)}, f32[16,12544]{1,0:T(8,128)S(1)}, u32[]{:S(2)}, u32[]{:S(2)}) collective-permute-start(f32[16,12544]{1,0:T(8,128)S(1)} %bitcast_add_fusion.3), channel_id=1, source_target_pairs={{0,4},{5,1},{4,8},{9,5},{8,12},{13,9},{12,14},{15,13},{14,10},{11,... | collective-permute-start | bytes 2408456 | tf_op jit(solution)/shard_map/ppermute | solution.py:136
  104.4 12.2 %collective-permute-start.5 = (f32[16,12544]{1,0:T(8,128)S(1)}, f32[16,12544]{1,0:T(8,128)S(1)}, u32[]{:S(2)}, u32[]{:S(2)}) collective-permute-start(f32[16,12544]{1,0:T(8,128)S(1)} %bitcast_add_fusion.2), channel_id=1, source_target_pairs={{0,4},{5,1},{4,8},{9,5},{8,12},{13,9},{12,14},{15,13},{14,10},{11,... | collective-permute-start | bytes 2408456 | tf_op jit(solution)/shard_map/ppermute | solution.py:136
  117.9 12.4 %collective-permute-start.6 = (f32[16,12544]{1,0:T(8,128)S(1)}, f32[16,12544]{1,0:T(8,128)S(1)}, u32[]{:S(2)}, u32[]{:S(2)}) collective-permute-start(f32[16,12544]{1,0:T(8,128)S(1)} %bitcast_add_fusion.1), channel_id=1, source_target_pairs={{0,4},{5,1},{4,8},{9,5},{8,12},{13,9},{12,14},{15,13},{14,10},{11,... | collective-permute-start | bytes 2408456 | tf_op jit(solution)/shard_map/ppermute | solution.py:136
  137.5 5.4 %collective-permute-start.7 = (f32[16,1024]{1,0:T(8,128)S(1)}, f32[16,1024]{1,0:T(8,128)S(1)}, u32[]{:S(2)}, u32[]{:S(2)}) collective-permute-start(f32[16,1024]{1,0:T(8,128)S(1)} %reshape.34), channel_id=1, source_target_pairs={{0,8},{1,9},{2,10},{3,11},{4,12},{5,13},{6,14},{7,15},{8,0},{9,1},... | collective-permute-start | bytes 196616 | tf_op jit(solution)/shard_map/ppermute | solution.py:148
  143.0 5.0 %collective-permute-start.8 = (f32[32,1024]{1,0:T(8,128)S(1)}, f32[32,1024]{1,0:T(8,128)S(1)}, u32[]{:S(2)}, u32[]{:S(2)}) collective-permute-start(f32[32,1024]{1,0:T(8,128)S(1)} %pad_maximum_fusion.3), channel_id=1, source_target_pairs={{0,4},{1,5},{2,6},{3,7},{4,0},{5,1},{6,2},{7,3},{8,12},{9,13},{10,... | collective-permute-start | bytes 393224 | tf_op jit(solution)/shard_map/ppermute | solution.py:148
  148.0 6.4 %collective-permute-start.9 = (f32[64,1024]{1,0:T(8,128)S(1)}, f32[64,1024]{1,0:T(8,128)S(1)}, u32[]{:S(2)}, u32[]{:S(2)}) collective-permute-start(f32[64,1024]{1,0:T(8,128)S(1)} %pad_maximum_fusion.2), channel_id=1, source_target_pairs={{0,2},{1,3},{2,0},{3,1},{4,6},{5,7},{6,4},{7,5},{8,10},{9,11},{10,... | collective-permute-start | bytes 786440 | tf_op jit(solution)/shard_map/ppermute | solution.py:148
  154.5 2.0 collective-permute-start.10

commit v11 on v10

--- a/solution.py
+++ b/solution.py
@@ -25,7 +25,7 @@
     return x[:, :b], x[:, b:]
 
 
-def _chol_kernel(f_ref, r_ref, w_ref, *, nb, b, scale):
+def _chol_kernel(f_ref, c_ref, o_ref, w_ref, r_ref, *, nb, b, scale):
     n = nb * b
     f = f_ref[...]
     eye = jnp.eye(b, dtype=jnp.float32)
@@ -48,7 +48,7 @@
             pj = pfull[:, j * b:(j + 1) * b]
             blocks.append(jnp.where(j > k, pj, jnp.where(j == k, rkk, 0.0)))
             pblocks.append(jnp.where(j > k, pj, 0.0))
-        r_ref[k] = jnp.concatenate(blocks, axis=1)
+        r_ref[pl.ds(pl.multiple_of(k * b, b), b), :] = jnp.concatenate(blocks, axis=1)
         p = jnp.concatenate(pblocks, axis=1)
         for i in range(1, nb):
             @pl.when(i > k)
@@ -60,21 +60,23 @@
         return carry
 
     lax.fori_loop(0, nb, step, 0)
+    rows = o_ref.shape[0]
+    o_ref[...] = r_ref[pl.ds(pl.multiple_of(c_ref[0] * rows, 8), rows), :]
 
 
-def damped_cholesky(f, scale, b=128, interpret=False):
+def damped_cholesky(f, scale, part, parts, b=128, interpret=False):
     n = f.shape[1]
     nb = n // b
-    out = pl.pallas_call(
+    rows = n // parts
+    return pl.pallas_call(
         functools.partial(_chol_kernel, nb=nb, b=b, scale=scale),
-        out_shape=jax.ShapeDtypeStruct((nb, b, n), jnp.float32),
-        in_specs=[pl.BlockSpec(memory_space=pltpu.VMEM)],
+        out_shape=jax.ShapeDtypeStruct((rows, n), jnp.float32),
+        in_specs=[pl.BlockSpec(memory_space=pltpu.VMEM), pl.BlockSpec(memory_space=pltpu.SMEM)],
         out_specs=pl.BlockSpec(memory_space=pltpu.VMEM),
-        scratch_shapes=[pltpu.VMEM((nb, b, n), jnp.float32)],
+        scratch_shapes=[pltpu.VMEM((nb, b, n), jnp.float32), pltpu.VMEM((n, n), jnp.float32)],
         compiler_params=pltpu.CompilerParams(vmem_limit_bytes=48 * 1024 * 1024),
         interpret=interpret,
-    )(f)
-    return out.reshape(n, n)
+    )(f, jnp.reshape(part, (1,)).astype(jnp.int32))
 
 
 def project(images, out_grads, in_signs, out_signs):
@@ -166,10 +168,7 @@
     every = doubling_gather(own, ("chan", "samp"))
     batch_total = samples * lax.axis_size("samp")
     width = every.shape[1]
-    factor = damped_cholesky(every, 1.0 / batch_total)
-    chan_count = lax.axis_size("chan")
-    rows_here = width // chan_count
-    r_rows = lax.dynamic_slice_in_dim(factor, lax.axis_index("chan") * rows_here, rows_here, 0)
+    r_rows = damped_cholesky(every, 1.0 / batch_total, lax.axis_index("chan"), lax.axis_size("chan"))
     return (own[None], r_rows)
 
 

time: 265 us -> 265 us (level)
  no operation moved by 1% of the time
where the time goes in v11:
time: 265 us; the launch traced here: 264 us
  Pallas kernels  107 us (40%)
  waiting for transfers between devices  68.4 us (26%)
  local copies, waits for them, and re-layouts  23.7 us (9%)
  starting transfers between devices  23.2 us (9%)
  between operations  21.2 us (8%)
  other arithmetic  12.9 us (5%)
  matrix products  7.26 us (3%)
    pallas_call x1, Pallas kernels, damped_cholesky(): pl.pallas_call(functools.partial(_chol_kernel, nb=nb, b=b, scale=scale),...  107 us
    ppermute x7, waiting for transfers between devices, ring_reduce_scatter(): acc = lax.ppermute(acc, (axis, pair), ring) + take(step)  57.5 us
    ppermute x7, starting transfers between devices, ring_reduce_scatter(): acc = lax.ppermute(acc, (axis, pair), ring) + take(step)  16.1 us
    ppermute x4, waiting for transfers between devices, doubling_gather(): other = lax.ppermute(x, axes, [(i, i ^ k) for i in range(size)])  10.9 us
    add x7, other arithmetic, ring_reduce_scatter(): acc = lax.ppermute(acc, (axis, pair), ring) + take(step)  9.45 us
    reshape x1, local copies, waits for them, and re-layouts, local(): both = both.reshape(-1, samples).T  8.05 us
    unnamed x11, local copies, waits for them, and re-layouts  7.24 us
    ppermute x4, starting transfers between devices, doubling_gather(): other = lax.ppermute(x, axes, [(i, i ^ k) for i in range(size)])  7.1 us
  transfers between devices with their start and end apart: 11, of which 11 were waited for; matrix products, arithmetic and copies ran while one was open for 0% of the time, Pallas kernels for 0%

profile of v11, /device:TPU:0, one launch (start us, length us, event | category | flops | bytes accessed | tf_op | source)
XLA Modules:
  0.0 264.1 jit_solution(654747505137883595)
XLA Ops:
  0.6 0.0 copy-start
  0.6 1.4 dynamic_slice.52
  7.3 1.7 fusion.10
  10.4 0.0 copy-start.1
  10.4 7.2 %copy.11 = bf16[128,32,784]{0,1,2:T(8,128)(2,1)} copy(bf16[128,32,784]{0,2,1:T(8,128)(2,1)} %param.6) | data formatting | bytes 12845056 | tf_op args[0]
  17.6 0.1 copy.17
  17.7 4.8 %fusion.11 = f32[128,32,14,14]{0,1,3,2:T(8,128)S(1)} fusion(bf16[128,32,28,28]{0,1,3,2:T(8,128)(2,1)} %bitcast.53, bf16[32,3,3,32]{0,3,2,1:T(8,128)(2,1)S(1)} %bitcast.56), kind=kOutput, calls=%fused_computation.33 | convolution fusion | flops 440664064 | bytes 9652224 | tf_op jit(solution)/shard_map/conv_general_dilated | solution.py:89
  22.5 0.0 copy-done
  22.5 0.0 copy-done.2
  22.5 0.6 convolution_bitcast_fusion
  23.2 3.4 %pad_maximum_fusion = f32[196,64,128]{2,1,0:T(8,128)} fusion(f32[196,32,128]{2,1,0:T(8,128)S(1)} %convolution_bitcast_fusion, f32[196,32,128]{2,1,0:T(8,128)S(1)} %bitcast.55), kind=kLoop, calls=%fused_computation | loop fusion | flops 1605632 | bytes 12845056 | tf_op jit(solution)/shard_map/concatenate | solution.py:161
  26.5 8.1 %copy.14 = f32[12544,128]{0,1:T(8,128)} copy(f32[12544,128]{1,0:T(8,128)} %bitcast.52) | data formatting | bytes 12845056 | tf_op jit(solution)/shard_map/reshape | solution.py:162
  35.3 1.2 dynamic-slice_bitcast_fusion
  36.5 3.1 %collective-permute-start = (f32[16,12544]{1,0:T(8,128)S(1)}, f32[16,12544]{1,0:T(8,128)S(1)}, u32[]{:S(2)}, u32[]{:S(2)}) collective-permute-start(f32[16,12544]{1,0:T(8,128)S(1)} %dynamic-slice_bitcast_fusion), channel_id=1, source_target_pairs={{0,4},{5,1},{4,8},{9,5},{8,12},{13,9},{12,14},{15,13},{14,10},{11,... | collective-permute-start | bytes 2408456 | tf_op jit(solution)/shard_map/ppermute | solution.py:138
  41.4 8.2 %collective-permute-done = f32[16,12544]{1,0:T(8,128)S(1)} collective-permute-done((f32[16,12544]{1,0:T(8,128)S(1)}, f32[16,12544]{1,0:T(8,128)S(1)}, u32[]{:S(2)}, u32[]{:S(2)}) %collective-permute-start) | collective-permute-done | bytes 802848 | tf_op jit(solution)/shard_map/ppermute | solution.py:138
  49.6 1.2 bitcast_add_fusion.6
  50.9 2.1 collective-permute-start.1
  54.9 8.2 %collective-permute-done.1 = f32[16,12544]{1,0:T(8,128)S(1)} collective-permute-done((f32[16,12544]{1,0:T(8,128)S(1)}, f32[16,12544]{1,0:T(8,128)S(1)}, u32[]{:S(2)}, u32[]{:S(2)}) %collective-permute-start.1) | collective-permute-done | bytes 802848 | tf_op jit(solution)/shard_map/ppermute | solution.py:138
  63.1 1.2 bitcast_add_fusion.5
  64.3 2.1 collective-permute-start.2
  68.2 8.4 %collective-permute-done.2 = f32[16,12544]{1,0:T(8,128)S(1)} collective-permute-done((f32[16,12544]{1,0:T(8,128)S(1)}, f32[16,12544]{1,0:T(8,128)S(1)}, u32[]{:S(2)}, u32[]{:S(2)}) %collective-permute-start.2) | collective-permute-done | bytes 802848 | tf_op jit(solution)/shard_map/ppermute | solution.py:138
  76.5 1.2 bitcast_add_fusion.4
  77.7 2.1 collective-permute-start.3
  81.7 8.2 %collective-permute-done.3 = f32[16,12544]{1,0:T(8,128)S(1)} collective-permute-done((f32[16,12544]{1,0:T(8,128)S(1)}, f32[16,12544]{1,0:T(8,128)S(1)}, u32[]{:S(2)}, u32[]{:S(2)}) %collective-permute-start.3) | collective-permute-done | bytes 802848 | tf_op jit(solution)/shard_map/ppermute | solution.py:138
  90.0 1.2 bitcast_add_fusion.3
  91.2 2.1 collective-permute-start.4
  95.3 8.1 %collective-permute-done.4 = f32[16,12544]{1,0:T(8,128)S(1)} collective-permute-done((f32[16,12544]{1,0:T(8,128)S(1)}, f32[16,12544]{1,0:T(8,128)S(1)}, u32[]{:S(2)}, u32[]{:S(2)}) %collective-permute-start.4) | collective-permute-done | bytes 802848 | tf_op jit(solution)/shard_map/ppermute | solution.py:138
  103.4 1.2 bitcast_add_fusion.2
  104.6 2.1 collective-permute-start.5
  108.6 8.2 %collective-permute-done.5 = f32[16,12544]{1,0:T(8,128)S(1)} collective-permute-done((f32[16,12544]{1,0:T(8,128)S(1)}, f32[16,12544]{1,0:T(8,128)S(1)}, u32[]{:S(2)}, u32[]{:S(2)}) %collective-permute-start.5) | collective-permute-done | bytes 802848 | tf_op jit(solution)/shard_map/ppermute | solution.py:138
  116.8 1.2 bitcast_add_fusion.1
  118.1 2.3 collective-permute-start.6
  122.3 8.1 %collective-permute-done.6 = f32[16,12544]{1,0:T(8,128)S(1)} collective-permute-done((f32[16,12544]{1,0:T(8,128)S(1)}, f32[16,12544]{1,0:T(8,128)S(1)}, u32[]{:S(2)}, u32[]{:S(2)}) %collective-permute-start.6) | collective-permute-done | bytes 802848 | tf_op jit(solution)/shard_map/ppermute | solution.py:138
  130.5 2.1 bitcast_add_fusion
  132.6 1.6 reshape.33
  134.2 1.6 copy.15
  135.7 1.9 convolution_multiply_fusion
  137.6 0.1 reshape.34
  137.7 3.2 %collective-permute-start.7 = (f32[16,1024]{1,0:T(8,128)S(1)}, f32[16,1024]{1,0:T(8,128)S(1)}, u32[]{:S(2)}, u32[]{:S(2)}) collective-permute-start(f32[16,1024]{1,0:T(8,128)S(1)} %reshape.34), channel_id=1, source_target_pairs={{0,8},{1,9},{2,10},{3,11},{4,12},{5,13},{6,14},{7,15},{8,0},{9,1},... | collective-permute-start | bytes 196616 | tf_op jit(solution)/shard_map/ppermute | solution.py:150
  140.9 2.2 collective-permute-done.7
  143.2 2.0 collective-permute-start.8
  145.1 3.1 %collective-permute-done.8 = f32[32,1024]{1,0:T(8,128)S(1)} collective-permute-done((f32[32,1024]{1,0:T(8,128)S(1)}, f32[32,1024]{1,0:T(8,128)S(1)}, u32[]{:S(2)}, u32[]{:S(2)}) %collective-permute-start.8) | collective-permute-done | bytes 131104 | tf_op jit(solution)/shard_map/ppermute | solution.py:150
  148.2 1.9 collective-permute-start.9
  150.1 4.5 %collective-permute-done.9 = f32[64,1024]{1,0:T(8,128)S(1)} collective-permute-done((f32[64,1024]{1,0:T(8,128)S(1)}, f32[64,1024]{1,0:T(8,128)S(1)}, u32[]{:S(2)}, u32[]{:S(2)}) %collective-permute-start.9) | collective-permute-done | bytes 262176 | tf_op jit(solution)/shard_map/ppermute | solution.py:150
  154.7 0.1 collective-permute-start.10
  154.8 0.8 broadcast_in_dim_reshape.3
  155.6 1.1 collective-permute-done.10
  156.7 107.4 %shard_map.77 = f32[128,1024]{1,0:T(8,128)} custom-call(f32[256,1024]{1,0:T(8,128)S(1)} %constant_dynamic-update-slice_fusion.f_ref, s32[1]{0:T(128)} %bitcast.28.c_ref), custom_call_target="tpu_custom_call" | custom-call | tf_op jit(solution)/shard_map/pallas_call | solution.py:71
  (11 shorter events, 0.2 us)
Async XLA Ops:
  0.6 21.9 %copy-start = (bf16[128,32,196]{0,1,2:T(8,128)(2,1)S(1)}, bf16[128,32,196]{0,1,2:T(8,128)(2,1)}, u32[]{:S(2)}) copy-start(bf16[128,32,196]{0,1,2:T(8,128)(2,1)} %param.7) | copy-start | bytes 4816900
  10.4 7.2 %copy-start.1 = (s32[32,288]{1,0:T(8,128)S(1)}, s32[32,288]{1,0:T(8,128)}, u32[]{:S(2)}) copy-start(s32[32,288]{1,0:T(8,128)} %param.8) | copy-start | bytes 110596
  17.6 5.0 %copy-start.2 = (s32[32,32]{1,0:T(8,128)S(1)}, s32[32,32]{1,0:T(8,128)}, u32[]{:S(2)}) copy-start(s32[32,32]{1,0:T(8,128)} %param.9) | copy-start | bytes 12292
  36.5 13.2 %collective-permute-start = (f32[16,12544]{1,0:T(8,128)S(1)}, f32[16,12544]{1,0:T(8,128)S(1)}, u32[]{:S(2)}, u32[]{:S(2)}) collective-permute-start(f32[16,12544]{1,0:T(8,128)S(1)} %dynamic-slice_bitcast_fusion), channel_id=1, source_target_pairs={{0,4},{5,1},{4,8},{9,5},{8,12},{13,9},{12,14},{15,13},{14,10},{11,... | collective-permute-start | bytes 2408456 | tf_op jit(solution)/shard_map/ppermute | solution.py:138
  50.9 12.2 %collective-permute-start.1 = (f32[16,12544]{1,0:T(8,128)S(1)}, f32[16,12544]{1,0:T(8,128)S(1)}, u32[]{:S(2)}, u32[]{:S(2)}) collective-permute-start(f32[16,12544]{1,0:T(8,128)S(1)} %bitcast_add_fusion.6), channel_id=1, source_target_pairs={{0,4},{5,1},{4,8},{9,5},{8,12},{13,9},{12,14},{15,13},{14,10},{11,... | collective-permute-start | bytes 2408456 | tf_op jit(solution)/shard_map/ppermute | solution.py:138
  64.3 12.2 %collective-permute-start.2 = (f32[16,12544]{1,0:T(8,128)S(1)}, f32[16,12544]{1,0:T(8,128)S(1)}, u32[]{:S(2)}, u32[]{:S(2)}) collective-permute-start(f32[16,12544]{1,0:T(8,128)S(1)} %bitcast_add_fusion.5), channel_id=1, source_target_pairs={{0,4},{5,1},{4,8},{9,5},{8,12},{13,9},{12,14},{15,13},{14,10},{11,... | collective-permute-start | bytes 2408456 | tf_op jit(solution)/shard_map/ppermute | solution.py:138
  77.7 12.2 %collective-permute-start.3 = (f32[16,12544]{1,0:T(8,128)S(1)}, f32[16,12544]{1,0:T(8,128)S(1)}, u32[]{:S(2)}, u32[]{:S(2)}) collective-permute-start(f32[16,12544]{1,0:T(8,128)S(1)} %bitcast_add_fusion.4), channel_id=1, source_target_pairs={{0,4},{5,1},{4,8},{9,5},{8,12},{13,9},{12,14},{15,13},{14,10},{11,... | collective-permute-start | bytes 2408456 | tf_op jit(solution)/shard_map/ppermute | solution.py:138
  91.2 12.2 %collective-permute-start.4 = (f32[16,12544]{1,0:T(8,128)S(1)}, f32[16,12544]{1,0:T(8,128)S(1)}, u32[]{:S(2)}, u32[]{:S(2)}) collective-permute-start(f32[16,12544]{1,0:T(8,128)S(1)} %bitcast_add_fusion.3), channel_id=1, source_target_pairs={{0,4},{5,1},{4,8},{9,5},{8,12},{13,9},{12,14},{15,13},{14,10},{11,... | collective-permute-start | bytes 2408456 | tf_op jit(solution)/shard_map/ppermute | solution.py:138
  104.6 12.2 %collective-permute-start.5 = (f32[16,12544]{1,0:T(8,128)S(1)}, f32[16,12544]{1,0:T(8,128)S(1)}, u32[]{:S(2)}, u32[]{:S(2)}) collective-permute-start(f32[16,12544]{1,0:T(8,128)S(1)} %bitcast_add_fusion.2), channel_id=1, source_target_pairs={{0,4},{5,1},{4,8},{9,5},{8,12},{13,9},{12,14},{15,13},{14,10},{11,... | collective-permute-start | bytes 2408456 | tf_op jit(solution)/shard_map/ppermute | solution.py:138
  118.1 12.4 %collective-permute-start.6 = (f32[16,12544]{1,0:T(8,128)S(1)}, f32[16,12544]{1,0:T(8,128)S(1)}, u32[]{:S(2)}, u32[]{:S(2)}) collective-permute-start(f32[16,12544]{1,0:T(8,128)S(1)} %bitcast_add_fusion.1), channel_id=1, source_target_pairs={{0,4},{5,1},{4,8},{9,5},{8,12},{13,9},{12,14},{15,13},{14,10},{11,... | collective-permute-start | bytes 2408456 | tf_op jit(solution)/shard_map/ppermute | solution.py:138
  137.7 5.4 %collective-permute-start.7 = (f32[16,1024]{1,0:T(8,128)S(1)}, f32[16,1024]{1,0:T(8,128)S(1)}, u32[]{:S(2)}, u32[]{:S(2)}) collective-permute-start(f32[16,1024]{1,0:T(8,128)S(1)} %reshape.34), channel_id=1, source_target_pairs={{0,8},{1,9},{2,10},{3,11},{4,12},{5,13},{6,14},{7,15},{8,0},{9,1},... | collective-permute-start | bytes 196616 | tf_op jit(solution)/shard_map/ppermute | solution.py:150
  143.2 5.0 %collective-permute-start.8 = (f32[32,1024]{1,0:T(8,128)S(1)}, f32[32,1024]{1,0:T(8,128)S(1)}, u32[]{:S(2)}, u32[]{:S(2)}) collective-permute-start(f32[32,1024]{1,0:T(8,128)S(1)} %pad_maximum_fusion.3), channel_id=1, source_target_pairs={{0,4},{1,5},{2,6},{3,7},{4,0},{5,1},{6,2},{7,3},{8,12},{9,13},{10,... | collective-permute-start | bytes 393224 | tf_op jit(solution)/shard_map/ppermute | solution.py:150
  148.2 6.4 %collective-permute-start.9 = (f32[64,1024]{1,0:T(8,128)S(1)}, f32[64,1024]{1,0:T(8,128)S(1)}, u32[]{:S(2)}, u32[]{:S(2)}) collective-permute-start(f32[64,1024]{1,0:T(8,128)S(1)} %pad_maximum_fusion.2), channel_id=1, source_target_pairs={{0,2},{1,3},{2,0},{3,1},{4,6},{5,7},{6,4},{7,5},{8,10},{9,11},{10,... | collective-permute-start | bytes 786440 | tf_op jit(solution)/shard_map/ppermute | solution.py:150
  154.7 2.0 collective-permute-start.10

commit v12 on v11

--- a/solution.py
+++ b/solution.py
@@ -116,13 +116,13 @@
     return list(range(0, n, 2)) + list(range(n - 1, 0, -2))
 
 
-def ring_reduce_scatter(x, axis, pair):
+def ring_reduce_scatter(xt, axis, pair):
     n = lax.axis_size(axis)
     order = _ring_order(n)
     me = lax.axis_index(pair)
     pos = jnp.asarray([order.index(c) for c in range(n)], jnp.int32)[lax.axis_index(axis)]
     owner = jnp.asarray(order, jnp.int32)
-    blocks = x.reshape(n, -1, x.shape[-1])
+    m = xt.shape[1] // n
     ring = []
     for q in range(n):
         ring.append((order[q] * 2, order[(q + 1) % n] * 2))
@@ -131,7 +131,7 @@
 
     def take(step):
         q = (pos - sign * (1 + step) + 2 * n) % n
-        return lax.dynamic_index_in_dim(blocks, owner[q], 0, keepdims=False)
+        return lax.dynamic_slice_in_dim(xt, owner[q] * m, m, axis=1).T
 
     acc = take(0)
     for step in range(1, n):
@@ -159,7 +159,7 @@
     width_in = in_part.shape[1]
     cells = in_part.shape[2]
     both = jnp.concatenate([jnp.transpose(in_part, (2, 1, 0)), jnp.transpose(out_part, (2, 1, 0))], axis=1)
-    both = both.reshape(-1, samples).T
+    both = both.reshape(-1, samples)
     both = ring_reduce_scatter(both, "chan", "samp")
     both = jnp.transpose(both.reshape(both.shape[0], cells, -1), (0, 2, 1))
     in_sum = both[:, :width_in]

time: 265 us -> 295 us (1.11)
  local copies, waits for them, and re-layouts: 23.7 us -> 90 us
  waiting for transfers between devices: 68.4 us -> 49.9 us
  between operations: 21.2 us -> 11.2 us
  other arithmetic: 12.9 us -> 5.76 us
    dynamic_slice x1 -> x2, local copies, waits for them, and re-layouts: 1.65 us -> 41.1 us  [take(): return lax.dynamic_slice_in_dim(xt, owner[q] * m, m, axis=1).T]
    unnamed x11 -> x19, local copies, waits for them, and re-layouts: 7.24 us -> 43.3 us
    ppermute x7, waiting for transfers between devices: 57.5 us -> 39 us  [ring_reduce_scatter(): acc = lax.ppermute(acc, (axis, pair), ring) + take(step)]
    reshape x1 -> x0, local copies, waits for them, and re-layouts: 8.05 us -> none  [local(): both = both.reshape(-1, samples).T]
    add x7, other arithmetic: 9.45 us -> 1.48 us  [ring_reduce_scatter(): acc = lax.ppermute(acc, (axis, pair), ring) + take(step)]
  transfers between devices with their start and end apart: 11 -> 11, of which waited for: 11 -> 11; matrix products, arithmetic and copies ran while one was open for 0% -> 11% of each run, Pallas kernels for 0% -> 0%
where the time goes in v12:
time: 295 us
  Pallas kernels  107 us (36%)
  local copies, waits for them, and re-layouts  90 us (31%)
  waiting for transfers between devices  49.9 us (17%)
  starting transfers between devices  23.1 us (8%)
  between operations  11.2 us (4%)
  matrix products  7.27 us (2%)
  other arithmetic  5.76 us (2%)
    pallas_call x1, Pallas kernels, damped_cholesky(): pl.pallas_call(functools.partial(_chol_kernel, nb=nb, b=b, scale=scale),...  107 us
    unnamed x19, local copies, waits for them, and re-layouts  43.3 us
    dynamic_slice x2, local copies, waits for them, and re-layouts, take(): return lax.dynamic_slice_in_dim(xt, owner[q] * m, m, axis=1).T  41.1 us
    ppermute x7, waiting for transfers between devices, ring_reduce_scatter(): acc = lax.ppermute(acc, (axis, pair), ring) + take(step)  39 us
    ppermute x7, starting transfers between devices, ring_reduce_scatter(): acc = lax.ppermute(acc, (axis, pair), ring) + take(step)  16 us
    ppermute x4, waiting for transfers between devices, doubling_gather(): other = lax.ppermute(x, axes, [(i, i ^ k) for i in range(size)])  10.9 us
    ppermute x4, starting transfers between devices, doubling_gather(): other = lax.ppermute(x, axes, [(i, i ^ k) for i in range(size)])  7.11 us
  transfers between devices with their start and end apart: 11, of which 11 were waited for; matrix products, arithmetic and copies ran while one was open for 11% of the time, Pallas kernels for 0%

profile of v12, /device:TPU:0, one launch (start us, length us, event | category | flops | bytes accessed | tf_op | source)
XLA Modules:
  0.0 294.7 jit_solution(13841090431928901406)
XLA Ops:
  0.7 1.4 dynamic_slice.51
  7.4 1.7 fusion.10
  14.1 0.8 add_convert_fusion
  14.9 0.1 copy.24
  15.0 7.2 %copy.11 = bf16[128,32,784]{0,1,2:T(8,128)(2,1)} copy(bf16[128,32,784]{0,2,1:T(8,128)(2,1)} %param.6) | data formatting | bytes 12845056 | tf_op args[0]
  22.2 0.6 convolution_bitcast_fusion
  22.8 4.8 %fusion.11 = f32[128,32,14,14]{0,1,3,2:T(8,128)S(1)} fusion(bf16[128,32,28,28]{0,1,3,2:T(8,128)(2,1)} %bitcast.41, bf16[32,3,3,32]{0,3,2,1:T(8,128)(2,1)S(1)} %bitcast.45), kind=kOutput, calls=%fused_computation.40 | convolution fusion | flops 440664064 | bytes 9652224 | tf_op jit(solution)/shard_map/conv_general_dilated | solution.py:89
  27.6 3.4 %pad_maximum_fusion = f32[196,64,128]{2,1,0:T(8,128)} fusion(f32[196,32,128]{2,1,0:T(8,128)S(1)} %convolution_bitcast_fusion, f32[196,32,128]{2,1,0:T(8,128)S(1)} %bitcast.43), kind=kLoop, calls=%fused_computation | loop fusion | flops 1605632 | bytes 12845056 | tf_op jit(solution)/shard_map/concatenate | solution.py:161
  31.0 39.5 %constant_dynamic-slice_fusion = (f32[12544,16]{1,0:T(8,128)}, f32[12544,16]{1,0:T(8,128)}, f32[12544,16]{1,0:T(8,128)}, f32[12544,16]{1,0:T(8,128)}, f32[12544,...) fusion(f32[12544,128]{1,0:T(8,128)} %bitcast.40, s32[]{:T(128)S(6)} %select_n.110, ...), kind=kLoop, calls=%fused_computation.27 | loop fusion | bytes 12845088 | tf_op jit(solution)/shard_map/dynamic_slice | solution.py:134
  70.5 4.5 %copy.26 = f32[12544,16]{0,1:T(8,128)S(1)} copy(f32[12544,16]{1,0:T(8,128)} %get-tuple-element.9) | data formatting | bytes 1605632
  75.0 3.1 %collective-permute-start = (f32[16,12544]{1,0:T(8,128)S(1)}, f32[16,12544]{1,0:T(8,128)S(1)}, u32[]{:S(2)}, u32[]{:S(2)}) collective-permute-start(f32[16,12544]{1,0:T(8,128)S(1)} %bitcast.44), channel_id=1, source_target_pairs={{0,4},{5,1},{4,8},{9,5},{8,12},{13,9},{12,14},{15,13},{14,10},{11,... | collective-permute-start | bytes 2408456 | tf_op jit(solution)/shard_map/ppermute | solution.py:138
  78.1 4.5 %copy.27 = f32[12544,16]{0,1:T(8,128)S(1)} copy(f32[12544,16]{1,0:T(8,128)} %get-tuple-element.8) | data formatting | bytes 1605632
  82.6 5.6 %collective-permute-done = f32[16,12544]{1,0:T(8,128)S(1)} collective-permute-done((f32[16,12544]{1,0:T(8,128)S(1)}, f32[16,12544]{1,0:T(8,128)S(1)}, u32[]{:S(2)}, u32[]{:S(2)}) %collective-permute-start) | collective-permute-done | bytes 802848 | tf_op jit(solution)/shard_map/ppermute | solution.py:138
  88.3 2.1 collective-permute-start.1
  90.4 4.5 %copy.28 = f32[12544,16]{0,1:T(8,128)S(1)} copy(f32[12544,16]{1,0:T(8,128)} %get-tuple-element.7) | data formatting | bytes 1605632
  94.9 5.6 %collective-permute-done.1 = f32[16,12544]{1,0:T(8,128)S(1)} collective-permute-done((f32[16,12544]{1,0:T(8,128)S(1)}, f32[16,12544]{1,0:T(8,128)S(1)}, u32[]{:S(2)}, u32[]{:S(2)}) %collective-permute-start.1) | collective-permute-done | bytes 802848 | tf_op jit(solution)/shard_map/ppermute | solution.py:138
  100.5 0.1 bitcast_add_fusion.5
  100.6 2.1 collective-permute-start.2
  102.7 4.5 %copy.29 = f32[12544,16]{0,1:T(8,128)S(1)} copy(f32[12544,16]{1,0:T(8,128)} %get-tuple-element.6) | data formatting | bytes 1605632
  107.2 5.6 %collective-permute-done.2 = f32[16,12544]{1,0:T(8,128)S(1)} collective-permute-done((f32[16,12544]{1,0:T(8,128)S(1)}, f32[16,12544]{1,0:T(8,128)S(1)}, u32[]{:S(2)}, u32[]{:S(2)}) %collective-permute-start.2) | collective-permute-done | bytes 802848 | tf_op jit(solution)/shard_map/ppermute | solution.py:138
  112.9 2.1 collective-permute-start.3
  115.0 4.5 %copy.30 = f32[12544,16]{0,1:T(8,128)S(1)} copy(f32[12544,16]{1,0:T(8,128)} %get-tuple-element.5) | data formatting | bytes 1605632
  119.5 5.6 %collective-permute-done.3 = f32[16,12544]{1,0:T(8,128)S(1)} collective-permute-done((f32[16,12544]{1,0:T(8,128)S(1)}, f32[16,12544]{1,0:T(8,128)S(1)}, u32[]{:S(2)}, u32[]{:S(2)}) %collective-permute-start.3) | collective-permute-done | bytes 802848 | tf_op jit(solution)/shard_map/ppermute | solution.py:138
  125.1 0.1 bitcast_add_fusion.3
  125.2 2.1 collective-permute-start.4
  127.3 4.5 %copy.31 = f32[12544,16]{0,1:T(8,128)S(1)} copy(f32[12544,16]{1,0:T(8,128)} %get-tuple-element.4) | data formatting | bytes 1605632
  131.8 5.6 %collective-permute-done.4 = f32[16,12544]{1,0:T(8,128)S(1)} collective-permute-done((f32[16,12544]{1,0:T(8,128)S(1)}, f32[16,12544]{1,0:T(8,128)S(1)}, u32[]{:S(2)}, u32[]{:S(2)}) %collective-permute-start.4) | collective-permute-done | bytes 802848 | tf_op jit(solution)/shard_map/ppermute | solution.py:138
  137.4 0.1 bitcast_add_fusion.2
  137.5 2.3 collective-permute-start.5
  139.8 4.5 %copy.32 = f32[12544,16]{0,1:T(8,128)S(1)} copy(f32[12544,16]{1,0:T(8,128)} %get-tuple-element.3) | data formatting | bytes 1605632
  144.3 5.6 %collective-permute-done.5 = f32[16,12544]{1,0:T(8,128)S(1)} collective-permute-done((f32[16,12544]{1,0:T(8,128)S(1)}, f32[16,12544]{1,0:T(8,128)S(1)}, u32[]{:S(2)}, u32[]{:S(2)}) %collective-permute-start.5) | collective-permute-done | bytes 802848 | tf_op jit(solution)/shard_map/ppermute | solution.py:138
  150.0 2.1 collective-permute-start.6
  152.1 4.5 %copy.33 = f32[12544,16]{0,1:T(8,128)S(1)} copy(f32[12544,16]{1,0:T(8,128)} %get-tuple-element.2) | data formatting | bytes 1605632
  156.6 5.6 %collective-permute-done.6 = f32[16,12544]{1,0:T(8,128)S(1)} collective-permute-done((f32[16,12544]{1,0:T(8,128)S(1)}, f32[16,12544]{1,0:T(8,128)S(1)}, u32[]{:S(2)}, u32[]{:S(2)}) %collective-permute-start.6) | collective-permute-done | bytes 802848 | tf_op jit(solution)/shard_map/ppermute | solution.py:138
  162.2 1.0 bitcast_add_fusion
  163.2 1.6 reshape.45
  164.8 1.6 copy.22
  166.3 1.9 convolution_multiply_fusion
  168.2 0.1 reshape.46
  168.3 3.1 %collective-permute-start.7 = (f32[16,1024]{1,0:T(8,128)S(1)}, f32[16,1024]{1,0:T(8,128)S(1)}, u32[]{:S(2)}, u32[]{:S(2)}) collective-permute-start(f32[16,1024]{1,0:T(8,128)S(1)} %reshape.46), channel_id=1, source_target_pairs={{0,8},{1,9},{2,10},{3,11},{4,12},{5,13},{6,14},{7,15},{8,0},{9,1},... | collective-permute-start | bytes 196616 | tf_op jit(solution)/shard_map/ppermute | solution.py:150
  171.5 2.2 collective-permute-done.7
  173.7 2.0 collective-permute-start.8
  175.7 3.1 %collective-permute-done.8 = f32[32,1024]{1,0:T(8,128)S(1)} collective-permute-done((f32[32,1024]{1,0:T(8,128)S(1)}, f32[32,1024]{1,0:T(8,128)S(1)}, u32[]{:S(2)}, u32[]{:S(2)}) %collective-permute-start.8) | collective-permute-done | bytes 131104 | tf_op jit(solution)/shard_map/ppermute | solution.py:150
  178.8 1.9 collective-permute-start.9
  180.7 4.5 %collective-permute-done.9 = f32[64,1024]{1,0:T(8,128)S(1)} collective-permute-done((f32[64,1024]{1,0:T(8,128)S(1)}, f32[64,1024]{1,0:T(8,128)S(1)}, u32[]{:S(2)}, u32[]{:S(2)}) %collective-permute-start.9) | collective-permute-done | bytes 262176 | tf_op jit(solution)/shard_map/ppermute | solution.py:150
  185.4 0.8 broadcast_in_dim_reshape.3
  186.2 1.1 collective-permute-done.10
  187.3 107.4 %shard_map.77 = f32[128,1024]{1,0:T(8,128)} custom-call(f32[256,1024]{1,0:T(8,128)S(1)} %constant_dynamic-update-slice_fusion.f_ref, s32[1]{0:T(128)} %bitcast.25.c_ref), custom_call_target="tpu_custom_call" | custom-call | tf_op jit(solution)/shard_map/pallas_call | solution.py:71
  (18 shorter events, 0.5 us)
Async XLA Ops:
  0.6 21.6 %copy-start = (bf16[128,32,196]{0,1,2:T(8,128)(2,1)S(1)}, bf16[128,32,196]{0,1,2:T(8,128)(2,1)}, u32[]{:S(2)}) copy-start(bf16[128,32,196]{0,1,2:T(8,128)(2,1)} %param.7) | copy-start | bytes 4816900
  15.0 7.2 %copy-start.2 = (s32[32,32]{1,0:T(8,128)S(1)}, s32[32,32]{1,0:T(8,128)}, u32[]{:S(2)}) copy-start(s32[32,32]{1,0:T(8,128)} %param.9) | copy-start | bytes 12292
  75.0 13.2 %collective-permute-start = (f32[16,12544]{1,0:T(8,128)S(1)}, f32[16,12544]{1,0:T(8,128)S(1)}, u32[]{:S(2)}, u32[]{:S(2)}) collective-permute-start(f32[16,12544]{1,0:T(8,128)S(1)} %bitcast.44), channel_id=1, source_target_pairs={{0,4},{5,1},{4,8},{9,5},{8,12},{13,9},{12,14},{15,13},{14,10},{11,... | collective-permute-start | bytes 2408456 | tf_op jit(solution)/shard_map/ppermute | solution.py:138
  88.3 12.2 %collective-permute-start.1 = (f32[16,12544]{1,0:T(8,128)S(1)}, f32[16,12544]{1,0:T(8,128)S(1)}, u32[]{:S(2)}, u32[]{:S(2)}) collective-permute-start(f32[16,12544]{1,0:T(8,128)S(1)} %bitcast_add_fusion.6), channel_id=1, source_target_pairs={{0,4},{5,1},{4,8},{9,5},{8,12},{13,9},{12,14},{15,13},{14,10},{11,... | collective-permute-start | bytes 2408456 | tf_op jit(solution)/shard_map/ppermute | solution.py:138
  100.6 12.2 %collective-permute-start.2 = (f32[16,12544]{1,0:T(8,128)S(1)}, f32[16,12544]{1,0:T(8,128)S(1)}, u32[]{:S(2)}, u32[]{:S(2)}) collective-permute-start(f32[16,12544]{1,0:T(8,128)S(1)} %bitcast_add_fusion.5), channel_id=1, source_target_pairs={{0,4},{5,1},{4,8},{9,5},{8,12},{13,9},{12,14},{15,13},{14,10},{11,... | collective-permute-start | bytes 2408456 | tf_op jit(solution)/shard_map/ppermute | solution.py:138
  112.9 12.2 %collective-permute-start.3 = (f32[16,12544]{1,0:T(8,128)S(1)}, f32[16,12544]{1,0:T(8,128)S(1)}, u32[]{:S(2)}, u32[]{:S(2)}) collective-permute-start(f32[16,12544]{1,0:T(8,128)S(1)} %bitcast_add_fusion.4), channel_id=1, source_target_pairs={{0,4},{5,1},{4,8},{9,5},{8,12},{13,9},{12,14},{15,13},{14,10},{11,... | collective-permute-start | bytes 2408456 | tf_op jit(solution)/shard_map/ppermute | solution.py:138
  125.2 12.2 %collective-permute-start.4 = (f32[16,12544]{1,0:T(8,128)S(1)}, f32[16,12544]{1,0:T(8,128)S(1)}, u32[]{:S(2)}, u32[]{:S(2)}) collective-permute-start(f32[16,12544]{1,0:T(8,128)S(1)} %bitcast_add_fusion.3), channel_id=1, source_target_pairs={{0,4},{5,1},{4,8},{9,5},{8,12},{13,9},{12,14},{15,13},{14,10},{11,... | collective-permute-start | bytes 2408456 | tf_op jit(solution)/shard_map/ppermute | solution.py:138
  137.5 12.4 %collective-permute-start.5 = (f32[16,12544]{1,0:T(8,128)S(1)}, f32[16,12544]{1,0:T(8,128)S(1)}, u32[]{:S(2)}, u32[]{:S(2)}) collective-permute-start(f32[16,12544]{1,0:T(8,128)S(1)} %bitcast_add_fusion.2), channel_id=1, source_target_pairs={{0,4},{5,1},{4,8},{9,5},{8,12},{13,9},{12,14},{15,13},{14,10},{11,... | collective-permute-start | bytes 2408456 | tf_op jit(solution)/shard_map/ppermute | solution.py:138
  150.0 12.2 %collective-permute-start.6 = (f32[16,12544]{1,0:T(8,128)S(1)}, f32[16,12544]{1,0:T(8,128)S(1)}, u32[]{:S(2)}, u32[]{:S(2)}) collective-permute-start(f32[16,12544]{1,0:T(8,128)S(1)} %bitcast_add_fusion.1), channel_id=1, source_target_pairs={{0,4},{5,1},{4,8},{9,5},{8,12},{13,9},{12,14},{15,13},{14,10},{11,... | collective-permute-start | bytes 2408456 | tf_op jit(solution)/shard_map/ppermute | solution.py:138
  162.2 132.5 %copy-start.1 = (bf16[128,32,196]{0,1,2:T(8,128)(2,1)S(1)}, bf16[128,32,196]{0,1,2:T(8,128)(2,1)}, u32[]{:S(2)}) copy-start(bf16[128,32,196]{0,1,2:T(8,128)(2,1)} %param.7) | copy-start | bytes 4816900
  168.3 5.4 %collective-permute-start.7 = (f32[16,1024]{1,0:T(8,128)S(1)}, f32[16,1024]{1,0:T(8,128)S(1)}, u32[]{:S(2)}, u32[]{:S(2)}) collective-permute-start(f32[16,1024]{1,0:T(8,128)S(1)} %reshape.46), channel_id=1, source_target_pairs={{0,8},{1,9},{2,10},{3,11},{4,12},{5,13},{6,14},{7,15},{8,0},{9,1},... | collective-permute-start | bytes 196616 | tf_op jit(solution)/shard_map/ppermute | solution.py:150
  173.7 5.0 %collective-permute-start.8 = (f32[32,1024]{1,0:T(8,128)S(1)}, f32[32,1024]{1,0:T(8,128)S(1)}, u32[]{:S(2)}, u32[]{:S(2)}) collective-permute-start(f32[32,1024]{1,0:T(8,128)S(1)} %pad_maximum_fusion.3), channel_id=1, source_target_pairs={{0,4},{1,5},{2,6},{3,7},{4,0},{5,1},{6,2},{7,3},{8,12},{9,13},{10,... | collective-permute-start | bytes 393224 | tf_op jit(solution)/shard_map/ppermute | solution.py:150
  178.8 6.4 %collective-permute-start.9 = (f32[64,1024]{1,0:T(8,128)S(1)}, f32[64,1024]{1,0:T(8,128)S(1)}, u32[]{:S(2)}, u32[]{:S(2)}) collective-permute-start(f32[64,1024]{1,0:T(8,128)S(1)} %pad_maximum_fusion.2), channel_id=1, source_target_pairs={{0,2},{1,3},{2,0},{3,1},{4,6},{5,7},{6,4},{7,5},{8,10},{9,11},{10,... | collective-permute-start | bytes 786440 | tf_op jit(solution)/shard_map/ppermute | solution.py:150
  185.3 2.0 collective-permute-start.10

commit v13 on v11

--- a/solution.py
+++ b/solution.py
@@ -35,13 +35,15 @@
         w_ref[i] = g
         w_ref[i, :, i * b:(i + 1) * b] = g[:, i * b:(i + 1) * b] + eye
 
-    def step(k, carry):
+    def diag(k):
         wk = w_ref[k]
         d = jnp.zeros((b, b), jnp.float32)
         for j in range(nb):
             d = jnp.where(k == j, wk[:, j * b:(j + 1) * b], d)
-        rkk, linv = _factor_block(d, b)
-        pfull = jnp.dot(linv, wk, precision=HI, preferred_element_type=jnp.float32)
+        return d
+
+    def panel(k, rkk, linv):
+        pfull = jnp.dot(linv, w_ref[k], precision=HI, preferred_element_type=jnp.float32)
         blocks = []
         pblocks = []
         for j in range(nb):
@@ -49,17 +51,28 @@
             blocks.append(jnp.where(j > k, pj, jnp.where(j == k, rkk, 0.0)))
             pblocks.append(jnp.where(j > k, pj, 0.0))
         r_ref[pl.ds(pl.multiple_of(k * b, b), b), :] = jnp.concatenate(blocks, axis=1)
+        return pblocks
+
+    def step(k, carry):
+        rkk, linv = carry
+        pblocks = panel(k, rkk, linv)
         p = jnp.concatenate(pblocks, axis=1)
-        for i in range(1, nb):
-            @pl.when(i > k)
-            def _():
-                ti = pblocks[i]
-                upd = lax.dot_general(ti, p[:, i * b:], (((0,), (0,)), ((), ())), precision=HI,
-                                      preferred_element_type=jnp.float32)
-                w_ref[i, :, i * b:] = w_ref[i, :, i * b:] - upd
-        return carry
+        t1 = jnp.zeros((b, b), jnp.float32)
+        for j in range(nb):
+            t1 = jnp.where(k + 1 == j, pblocks[j], t1)
+        k1 = k + 1
+        w_ref[k1] = w_ref[k1] - lax.dot_general(t1, p, (((0,), (0,)), ((), ())), precision=HI,
+                                                preferred_element_type=jnp.float32)
+        nxt = _factor_block(diag(k1), b)
+        for i in range(2, nb):
+            ti = jnp.where(i > k1, pblocks[i], 0.0)
+            upd = lax.dot_general(ti, p[:, i * b:], (((0,), (0,)), ((), ())), precision=HI,
+                                  preferred_element_type=jnp.float32)
+            w_ref[i, :, i * b:] = w_ref[i, :, i * b:] - upd
+        return nxt
 
-    lax.fori_loop(0, nb, step, 0)
+    last = lax.fori_loop(0, nb - 1, step, _factor_block(diag(0), b))
+    panel(nb - 1, *last)
     rows = o_ref.shape[0]
     o_ref[...] = r_ref[pl.ds(pl.multiple_of(c_ref[0] * rows, 8), rows), :]
 

time: 265 us -> 257 us (0.970)
  Pallas kernels: 107 us -> 98.8 us
    pallas_call x1, Pallas kernels: 107 us -> 98.8 us  [damped_cholesky(): pl.pallas_call(functools.partial(_chol_kernel, nb=nb, b=b, scale=scale),...]
where the time goes in v13:
time: 257 us; the launch traced here: 256 us
  Pallas kernels  98.8 us (38%)
  waiting for transfers between devices  68.4 us (27%)
  local copies, waits for them, and re-layouts  23.7 us (9%)
  starting transfers between devices  23.2 us (9%)
  between operations  21.2 us (8%)
  other arithmetic  12.9 us (5%)
  matrix products  7.26 us (3%)
    pallas_call x1, Pallas kernels, damped_cholesky(): pl.pallas_call(functools.partial(_chol_kernel, nb=nb, b=b, scale=scale),...  98.8 us
    ppermute x7, waiting for transfers between devices, ring_reduce_scatter(): acc = lax.ppermute(acc, (axis, pair), ring) + take(step)  57.5 us
    ppermute x7, starting transfers between devices, ring_reduce_scatter(): acc = lax.ppermute(acc, (axis, pair), ring) + take(step)  16.1 us
    ppermute x4, waiting for transfers between devices, doubling_gather(): other = lax.ppermute(x, axes, [(i, i ^ k) for i in range(size)])  10.9 us
    add x7, other arithmetic, ring_reduce_scatter(): acc = lax.ppermute(acc, (axis, pair), ring) + take(step)  9.45 us
    reshape x1, local copies, waits for them, and re-layouts, local(): both = both.reshape(-1, samples).T  8.05 us
    unnamed x11, local copies, waits for them, and re-layouts  7.24 us
    ppermute x4, starting transfers between devices, doubling_gather(): other = lax.ppermute(x, axes, [(i, i ^ k) for i in range(size)])  7.1 us
  transfers between devices with their start and end apart: 11, of which 11 were waited for; matrix products, arithmetic and copies ran while one was open for 0% of the time, Pallas kernels for 0%

profile of v13, /device:TPU:0, one launch (start us, length us, event | category | flops | bytes accessed | tf_op | source)
XLA Modules:
  0.0 255.6 jit_solution(15555683996609213933)
XLA Ops:
  0.6 0.0 copy-start
  0.6 1.4 dynamic_slice.52
  7.3 1.7 fusion.10
  10.4 0.0 copy-start.1
  10.4 7.2 %copy.11 = bf16[128,32,784]{0,1,2:T(8,128)(2,1)} copy(bf16[128,32,784]{0,2,1:T(8,128)(2,1)} %param.6) | data formatting | bytes 12845056 | tf_op args[0]
  17.6 0.1 copy.17
  17.7 4.8 %fusion.11 = f32[128,32,14,14]{0,1,3,2:T(8,128)S(1)} fusion(bf16[128,32,28,28]{0,1,3,2:T(8,128)(2,1)} %bitcast.53, bf16[32,3,3,32]{0,3,2,1:T(8,128)(2,1)S(1)} %bitcast.56), kind=kOutput, calls=%fused_computation.33 | convolution fusion | flops 440664064 | bytes 9652224 | tf_op jit(solution)/shard_map/conv_general_dilated | solution.py:102
  22.5 0.0 copy-done
  22.5 0.0 copy-done.2
  22.5 0.6 convolution_bitcast_fusion
  23.2 3.4 %pad_maximum_fusion = f32[196,64,128]{2,1,0:T(8,128)} fusion(f32[196,32,128]{2,1,0:T(8,128)S(1)} %convolution_bitcast_fusion, f32[196,32,128]{2,1,0:T(8,128)S(1)} %bitcast.55), kind=kLoop, calls=%fused_computation | loop fusion | flops 1605632 | bytes 12845056 | tf_op jit(solution)/shard_map/concatenate | solution.py:174
  26.5 8.1 %copy.14 = f32[12544,128]{0,1:T(8,128)} copy(f32[12544,128]{1,0:T(8,128)} %bitcast.52) | data formatting | bytes 12845056 | tf_op jit(solution)/shard_map/reshape | solution.py:175
  35.3 1.2 dynamic-slice_bitcast_fusion
  36.5 3.1 %collective-permute-start = (f32[16,12544]{1,0:T(8,128)S(1)}, f32[16,12544]{1,0:T(8,128)S(1)}, u32[]{:S(2)}, u32[]{:S(2)}) collective-permute-start(f32[16,12544]{1,0:T(8,128)S(1)} %dynamic-slice_bitcast_fusion), channel_id=1, source_target_pairs={{0,4},{5,1},{4,8},{9,5},{8,12},{13,9},{12,14},{15,13},{14,10},{11,... | collective-permute-start | bytes 2408456 | tf_op jit(solution)/shard_map/ppermute | solution.py:151
  41.4 8.2 %collective-permute-done = f32[16,12544]{1,0:T(8,128)S(1)} collective-permute-done((f32[16,12544]{1,0:T(8,128)S(1)}, f32[16,12544]{1,0:T(8,128)S(1)}, u32[]{:S(2)}, u32[]{:S(2)}) %collective-permute-start) | collective-permute-done | bytes 802848 | tf_op jit(solution)/shard_map/ppermute | solution.py:151
  49.6 1.2 bitcast_add_fusion.6
  50.9 2.1 collective-permute-start.1
  54.9 8.2 %collective-permute-done.1 = f32[16,12544]{1,0:T(8,128)S(1)} collective-permute-done((f32[16,12544]{1,0:T(8,128)S(1)}, f32[16,12544]{1,0:T(8,128)S(1)}, u32[]{:S(2)}, u32[]{:S(2)}) %collective-permute-start.1) | collective-permute-done | bytes 802848 | tf_op jit(solution)/shard_map/ppermute | solution.py:151
  63.1 1.2 bitcast_add_fusion.5
  64.3 2.1 collective-permute-start.2
  68.2 8.4 %collective-permute-done.2 = f32[16,12544]{1,0:T(8,128)S(1)} collective-permute-done((f32[16,12544]{1,0:T(8,128)S(1)}, f32[16,12544]{1,0:T(8,128)S(1)}, u32[]{:S(2)}, u32[]{:S(2)}) %collective-permute-start.2) | collective-permute-done | bytes 802848 | tf_op jit(solution)/shard_map/ppermute | solution.py:151
  76.5 1.2 bitcast_add_fusion.4
  77.7 2.1 collective-permute-start.3
  81.7 8.2 %collective-permute-done.3 = f32[16,12544]{1,0:T(8,128)S(1)} collective-permute-done((f32[16,12544]{1,0:T(8,128)S(1)}, f32[16,12544]{1,0:T(8,128)S(1)}, u32[]{:S(2)}, u32[]{:S(2)}) %collective-permute-start.3) | collective-permute-done | bytes 802848 | tf_op jit(solution)/shard_map/ppermute | solution.py:151
  90.0 1.2 bitcast_add_fusion.3
  91.2 2.1 collective-permute-start.4
  95.3 8.1 %collective-permute-done.4 = f32[16,12544]{1,0:T(8,128)S(1)} collective-permute-done((f32[16,12544]{1,0:T(8,128)S(1)}, f32[16,12544]{1,0:T(8,128)S(1)}, u32[]{:S(2)}, u32[]{:S(2)}) %collective-permute-start.4) | collective-permute-done | bytes 802848 | tf_op jit(solution)/shard_map/ppermute | solution.py:151
  103.4 1.2 bitcast_add_fusion.2
  104.6 2.1 collective-permute-start.5
  108.6 8.2 %collective-permute-done.5 = f32[16,12544]{1,0:T(8,128)S(1)} collective-permute-done((f32[16,12544]{1,0:T(8,128)S(1)}, f32[16,12544]{1,0:T(8,128)S(1)}, u32[]{:S(2)}, u32[]{:S(2)}) %collective-permute-start.5) | collective-permute-done | bytes 802848 | tf_op jit(solution)/shard_map/ppermute | solution.py:151
  116.8 1.2 bitcast_add_fusion.1
  118.1 2.3 collective-permute-start.6
  122.3 8.1 %collective-permute-done.6 = f32[16,12544]{1,0:T(8,128)S(1)} collective-permute-done((f32[16,12544]{1,0:T(8,128)S(1)}, f32[16,12544]{1,0:T(8,128)S(1)}, u32[]{:S(2)}, u32[]{:S(2)}) %collective-permute-start.6) | collective-permute-done | bytes 802848 | tf_op jit(solution)/shard_map/ppermute | solution.py:151
  130.5 2.1 bitcast_add_fusion
  132.6 1.6 reshape.33
  134.2 1.6 copy.15
  135.7 1.9 convolution_multiply_fusion
  137.6 0.1 reshape.34
  137.7 3.2 %collective-permute-start.7 = (f32[16,1024]{1,0:T(8,128)S(1)}, f32[16,1024]{1,0:T(8,128)S(1)}, u32[]{:S(2)}, u32[]{:S(2)}) collective-permute-start(f32[16,1024]{1,0:T(8,128)S(1)} %reshape.34), channel_id=1, source_target_pairs={{0,8},{1,9},{2,10},{3,11},{4,12},{5,13},{6,14},{7,15},{8,0},{9,1},... | collective-permute-start | bytes 196616 | tf_op jit(solution)/shard_map/ppermute | solution.py:163
  140.9 2.2 collective-permute-done.7
  143.2 2.0 collective-permute-start.8
  145.1 3.1 %collective-permute-done.8 = f32[32,1024]{1,0:T(8,128)S(1)} collective-permute-done((f32[32,1024]{1,0:T(8,128)S(1)}, f32[32,1024]{1,0:T(8,128)S(1)}, u32[]{:S(2)}, u32[]{:S(2)}) %collective-permute-start.8) | collective-permute-done | bytes 131104 | tf_op jit(solution)/shard_map/ppermute | solution.py:163
  148.2 1.9 collective-permute-start.9
  150.1 4.5 %collective-permute-done.9 = f32[64,1024]{1,0:T(8,128)S(1)} collective-permute-done((f32[64,1024]{1,0:T(8,128)S(1)}, f32[64,1024]{1,0:T(8,128)S(1)}, u32[]{:S(2)}, u32[]{:S(2)}) %collective-permute-start.9) | collective-permute-done | bytes 262176 | tf_op jit(solution)/shard_map/ppermute | solution.py:163
  154.7 0.1 collective-permute-start.10
  154.8 0.8 broadcast_in_dim_reshape.3
  155.6 1.1 collective-permute-done.10
  156.7 98.8 %shard_map.77 = f32[128,1024]{1,0:T(8,128)} custom-call(f32[256,1024]{1,0:T(8,128)S(1)} %constant_dynamic-update-slice_fusion.f_ref, s32[1]{0:T(128)} %bitcast.28.c_ref), custom_call_target="tpu_custom_call" | custom-call | tf_op jit(solution)/shard_map/pallas_call | solution.py:84
  (11 shorter events, 0.2 us)
Async XLA Ops:
  0.6 21.9 %copy-start = (bf16[128,32,196]{0,1,2:T(8,128)(2,1)S(1)}, bf16[128,32,196]{0,1,2:T(8,128)(2,1)}, u32[]{:S(2)}) copy-start(bf16[128,32,196]{0,1,2:T(8,128)(2,1)} %param.7) | copy-start | bytes 4816900
  10.4 7.2 %copy-start.1 = (s32[32,288]{1,0:T(8,128)S(1)}, s32[32,288]{1,0:T(8,128)}, u32[]{:S(2)}) copy-start(s32[32,288]{1,0:T(8,128)} %param.8) | copy-start | bytes 110596
  17.6 5.0 %copy-start.2 = (s32[32,32]{1,0:T(8,128)S(1)}, s32[32,32]{1,0:T(8,128)}, u32[]{:S(2)}) copy-start(s32[32,32]{1,0:T(8,128)} %param.9) | copy-start | bytes 12292
  36.5 13.2 %collective-permute-start = (f32[16,12544]{1,0:T(8,128)S(1)}, f32[16,12544]{1,0:T(8,128)S(1)}, u32[]{:S(2)}, u32[]{:S(2)}) collective-permute-start(f32[16,12544]{1,0:T(8,128)S(1)} %dynamic-slice_bitcast_fusion), channel_id=1, source_target_pairs={{0,4},{5,1},{4,8},{9,5},{8,12},{13,9},{12,14},{15,13},{14,10},{11,... | collective-permute-start | bytes 2408456 | tf_op jit(solution)/shard_map/ppermute | solution.py:151
  50.9 12.2 %collective-permute-start.1 = (f32[16,12544]{1,0:T(8,128)S(1)}, f32[16,12544]{1,0:T(8,128)S(1)}, u32[]{:S(2)}, u32[]{:S(2)}) collective-permute-start(f32[16,12544]{1,0:T(8,128)S(1)} %bitcast_add_fusion.6), channel_id=1, source_target_pairs={{0,4},{5,1},{4,8},{9,5},{8,12},{13,9},{12,14},{15,13},{14,10},{11,... | collective-permute-start | bytes 2408456 | tf_op jit(solution)/shard_map/ppermute | solution.py:151
  64.3 12.2 %collective-permute-start.2 = (f32[16,12544]{1,0:T(8,128)S(1)}, f32[16,12544]{1,0:T(8,128)S(1)}, u32[]{:S(2)}, u32[]{:S(2)}) collective-permute-start(f32[16,12544]{1,0:T(8,128)S(1)} %bitcast_add_fusion.5), channel_id=1, source_target_pairs={{0,4},{5,1},{4,8},{9,5},{8,12},{13,9},{12,14},{15,13},{14,10},{11,... | collective-permute-start | bytes 2408456 | tf_op jit(solution)/shard_map/ppermute | solution.py:151
  77.7 12.2 %collective-permute-start.3 = (f32[16,12544]{1,0:T(8,128)S(1)}, f32[16,12544]{1,0:T(8,128)S(1)}, u32[]{:S(2)}, u32[]{:S(2)}) collective-permute-start(f32[16,12544]{1,0:T(8,128)S(1)} %bitcast_add_fusion.4), channel_id=1, source_target_pairs={{0,4},{5,1},{4,8},{9,5},{8,12},{13,9},{12,14},{15,13},{14,10},{11,... | collective-permute-start | bytes 2408456 | tf_op jit(solution)/shard_map/ppermute | solution.py:151
  91.2 12.2 %collective-permute-start.4 = (f32[16,12544]{1,0:T(8,128)S(1)}, f32[16,12544]{1,0:T(8,128)S(1)}, u32[]{:S(2)}, u32[]{:S(2)}) collective-permute-start(f32[16,12544]{1,0:T(8,128)S(1)} %bitcast_add_fusion.3), channel_id=1, source_target_pairs={{0,4},{5,1},{4,8},{9,5},{8,12},{13,9},{12,14},{15,13},{14,10},{11,... | collective-permute-start | bytes 2408456 | tf_op jit(solution)/shard_map/ppermute | solution.py:151
  104.6 12.2 %collective-permute-start.5 = (f32[16,12544]{1,0:T(8,128)S(1)}, f32[16,12544]{1,0:T(8,128)S(1)}, u32[]{:S(2)}, u32[]{:S(2)}) collective-permute-start(f32[16,12544]{1,0:T(8,128)S(1)} %bitcast_add_fusion.2), channel_id=1, source_target_pairs={{0,4},{5,1},{4,8},{9,5},{8,12},{13,9},{12,14},{15,13},{14,10},{11,... | collective-permute-start | bytes 2408456 | tf_op jit(solution)/shard_map/ppermute | solution.py:151
  118.1 12.4 %collective-permute-start.6 = (f32[16,12544]{1,0:T(8,128)S(1)}, f32[16,12544]{1,0:T(8,128)S(1)}, u32[]{:S(2)}, u32[]{:S(2)}) collective-permute-start(f32[16,12544]{1,0:T(8,128)S(1)} %bitcast_add_fusion.1), channel_id=1, source_target_pairs={{0,4},{5,1},{4,8},{9,5},{8,12},{13,9},{12,14},{15,13},{14,10},{11,... | collective-permute-start | bytes 2408456 | tf_op jit(solution)/shard_map/ppermute | solution.py:151
  137.7 5.4 %collective-permute-start.7 = (f32[16,1024]{1,0:T(8,128)S(1)}, f32[16,1024]{1,0:T(8,128)S(1)}, u32[]{:S(2)}, u32[]{:S(2)}) collective-permute-start(f32[16,1024]{1,0:T(8,128)S(1)} %reshape.34), channel_id=1, source_target_pairs={{0,8},{1,9},{2,10},{3,11},{4,12},{5,13},{6,14},{7,15},{8,0},{9,1},... | collective-permute-start | bytes 196616 | tf_op jit(solution)/shard_map/ppermute | solution.py:163
  143.2 5.0 %collective-permute-start.8 = (f32[32,1024]{1,0:T(8,128)S(1)}, f32[32,1024]{1,0:T(8,128)S(1)}, u32[]{:S(2)}, u32[]{:S(2)}) collective-permute-start(f32[32,1024]{1,0:T(8,128)S(1)} %pad_maximum_fusion.3), channel_id=1, source_target_pairs={{0,4},{1,5},{2,6},{3,7},{4,0},{5,1},{6,2},{7,3},{8,12},{9,13},{10,... | collective-permute-start | bytes 393224 | tf_op jit(solution)/shard_map/ppermute | solution.py:163
  148.2 6.4 %collective-permute-start.9 = (f32[64,1024]{1,0:T(8,128)S(1)}, f32[64,1024]{1,0:T(8,128)S(1)}, u32[]{:S(2)}, u32[]{:S(2)}) collective-permute-start(f32[64,1024]{1,0:T(8,128)S(1)} %pad_maximum_fusion.2), channel_id=1, source_target_pairs={{0,2},{1,3},{2,0},{3,1},{4,6},{5,7},{6,4},{7,5},{8,10},{9,11},{10,... | collective-permute-start | bytes 786440 | tf_op jit(solution)/shard_map/ppermute | solution.py:163
  154.7 2.0 collective-permute-start.10

commit v14 on v13

--- a/solution.py
+++ b/solution.py
@@ -55,17 +55,19 @@
 
     def step(k, carry):
         rkk, linv = carry
+        k1 = k + 1
+        wk = w_ref[k]
+        a1 = jnp.zeros((b, b), jnp.float32)
+        for j in range(nb):
+            a1 = jnp.where(k1 == j, wk[:, j * b:(j + 1) * b], a1)
+        t1 = jnp.dot(linv, a1, precision=HI, preferred_element_type=jnp.float32)
+        d1 = diag(k1) - lax.dot_general(t1, t1, (((0,), (0,)), ((), ())), precision=HI,
+                                        preferred_element_type=jnp.float32)
+        nxt = _factor_block(d1, b)
         pblocks = panel(k, rkk, linv)
         p = jnp.concatenate(pblocks, axis=1)
-        t1 = jnp.zeros((b, b), jnp.float32)
-        for j in range(nb):
-            t1 = jnp.where(k + 1 == j, pblocks[j], t1)
-        k1 = k + 1
-        w_ref[k1] = w_ref[k1] - lax.dot_general(t1, p, (((0,), (0,)), ((), ())), precision=HI,
-                                                preferred_element_type=jnp.float32)
-        nxt = _factor_block(diag(k1), b)
-        for i in range(2, nb):
-            ti = jnp.where(i > k1, pblocks[i], 0.0)
+        for i in range(1, nb):
+            ti = jnp.where(i > k, pblocks[i], 0.0)
             upd = lax.dot_general(ti, p[:, i * b:], (((0,), (0,)), ((), ())), precision=HI,
                                   preferred_element_type=jnp.float32)
             w_ref[i, :, i * b:] = w_ref[i, :, i * b:] - upd

time: 257 us -> 252 us (0.981)
  Pallas kernels: 98.8 us -> 94.1 us
    pallas_call x1, Pallas kernels: 98.8 us -> 94.1 us  [damped_cholesky(): pl.pallas_call(functools.partial(_chol_kernel, nb=nb, b=b, scale=scale),...]
where the time goes in v14:
time: 252 us; the launch traced here: 251 us
  Pallas kernels  94.1 us (37%)
  waiting for transfers between devices  68.4 us (27%)
  local copies, waits for them, and re-layouts  23.7 us (9%)
  starting transfers between devices  23.2 us (9%)
  between operations  21.2 us (8%)
  other arithmetic  12.9 us (5%)
  matrix products  7.26 us (3%)
    pallas_call x1, Pallas kernels, damped_cholesky(): pl.pallas_call(functools.partial(_chol_kernel, nb=nb, b=b, scale=scale),...  94.1 us
    ppermute x7, waiting for transfers between devices, ring_reduce_scatter(): acc = lax.ppermute(acc, (axis, pair), ring) + take(step)  57.5 us
    ppermute x7, starting transfers between devices, ring_reduce_scatter(): acc = lax.ppermute(acc, (axis, pair), ring) + take(step)  16.1 us
    ppermute x4, waiting for transfers between devices, doubling_gather(): other = lax.ppermute(x, axes, [(i, i ^ k) for i in range(size)])  10.9 us
    add x7, other arithmetic, ring_reduce_scatter(): acc = lax.ppermute(acc, (axis, pair), ring) + take(step)  9.45 us
    reshape x1, local copies, waits for them, and re-layouts, local(): both = both.reshape(-1, samples).T  8.05 us
    unnamed x11, local copies, waits for them, and re-layouts  7.24 us
    ppermute x4, starting transfers between devices, doubling_gather(): other = lax.ppermute(x, axes, [(i, i ^ k) for i in range(size)])  7.1 us
  transfers between devices with their start and end apart: 11, of which 11 were waited for; matrix products, arithmetic and copies ran while one was open for 0% of the time, Pallas kernels for 0%

profile of v14, /device:TPU:0, one launch (start us, length us, event | category | flops | bytes accessed | tf_op | source)
XLA Modules:
  0.0 250.9 jit_solution(2984525802839534890)
XLA Ops:
  0.6 0.0 copy-start
  0.6 1.4 dynamic_slice.52
  7.3 1.7 fusion.10
  10.4 0.0 copy-start.1
  10.4 7.2 %copy.11 = bf16[128,32,784]{0,1,2:T(8,128)(2,1)} copy(bf16[128,32,784]{0,2,1:T(8,128)(2,1)} %param.6) | data formatting | bytes 12845056 | tf_op args[0]
  17.6 0.1 copy.17
  17.7 4.8 %fusion.11 = f32[128,32,14,14]{0,1,3,2:T(8,128)S(1)} fusion(bf16[128,32,28,28]{0,1,3,2:T(8,128)(2,1)} %bitcast.53, bf16[32,3,3,32]{0,3,2,1:T(8,128)(2,1)S(1)} %bitcast.56), kind=kOutput, calls=%fused_computation.33 | convolution fusion | flops 440664064 | bytes 9652224 | tf_op jit(solution)/shard_map/conv_general_dilated | solution.py:104
  22.5 0.0 copy-done
  22.5 0.0 copy-done.2
  22.5 0.6 convolution_bitcast_fusion
  23.2 3.4 %pad_maximum_fusion = f32[196,64,128]{2,1,0:T(8,128)} fusion(f32[196,32,128]{2,1,0:T(8,128)S(1)} %convolution_bitcast_fusion, f32[196,32,128]{2,1,0:T(8,128)S(1)} %bitcast.55), kind=kLoop, calls=%fused_computation | loop fusion | flops 1605632 | bytes 12845056 | tf_op jit(solution)/shard_map/concatenate | solution.py:176
  26.5 8.1 %copy.14 = f32[12544,128]{0,1:T(8,128)} copy(f32[12544,128]{1,0:T(8,128)} %bitcast.52) | data formatting | bytes 12845056 | tf_op jit(solution)/shard_map/reshape | solution.py:177
  35.3 1.2 dynamic-slice_bitcast_fusion
  36.5 3.1 %collective-permute-start = (f32[16,12544]{1,0:T(8,128)S(1)}, f32[16,12544]{1,0:T(8,128)S(1)}, u32[]{:S(2)}, u32[]{:S(2)}) collective-permute-start(f32[16,12544]{1,0:T(8,128)S(1)} %dynamic-slice_bitcast_fusion), channel_id=1, source_target_pairs={{0,4},{5,1},{4,8},{9,5},{8,12},{13,9},{12,14},{15,13},{14,10},{11,... | collective-permute-start | bytes 2408456 | tf_op jit(solution)/shard_map/ppermute | solution.py:153
  41.4 8.2 %collective-permute-done = f32[16,12544]{1,0:T(8,128)S(1)} collective-permute-done((f32[16,12544]{1,0:T(8,128)S(1)}, f32[16,12544]{1,0:T(8,128)S(1)}, u32[]{:S(2)}, u32[]{:S(2)}) %collective-permute-start) | collective-permute-done | bytes 802848 | tf_op jit(solution)/shard_map/ppermute | solution.py:153
  49.6 1.2 bitcast_add_fusion.6
  50.9 2.1 collective-permute-start.1
  54.9 8.2 %collective-permute-done.1 = f32[16,12544]{1,0:T(8,128)S(1)} collective-permute-done((f32[16,12544]{1,0:T(8,128)S(1)}, f32[16,12544]{1,0:T(8,128)S(1)}, u32[]{:S(2)}, u32[]{:S(2)}) %collective-permute-start.1) | collective-permute-done | bytes 802848 | tf_op jit(solution)/shard_map/ppermute | solution.py:153
  63.1 1.2 bitcast_add_fusion.5
  64.3 2.1 collective-permute-start.2
  68.2 8.4 %collective-permute-done.2 = f32[16,12544]{1,0:T(8,128)S(1)} collective-permute-done((f32[16,12544]{1,0:T(8,128)S(1)}, f32[16,12544]{1,0:T(8,128)S(1)}, u32[]{:S(2)}, u32[]{:S(2)}) %collective-permute-start.2) | collective-permute-done | bytes 802848 | tf_op jit(solution)/shard_map/ppermute | solution.py:153
  76.5 1.2 bitcast_add_fusion.4
  77.7 2.1 collective-permute-start.3
  81.7 8.2 %collective-permute-done.3 = f32[16,12544]{1,0:T(8,128)S(1)} collective-permute-done((f32[16,12544]{1,0:T(8,128)S(1)}, f32[16,12544]{1,0:T(8,128)S(1)}, u32[]{:S(2)}, u32[]{:S(2)}) %collective-permute-start.3) | collective-permute-done | bytes 802848 | tf_op jit(solution)/shard_map/ppermute | solution.py:153
  90.0 1.2 bitcast_add_fusion.3
  91.2 2.1 collective-permute-start.4
  95.3 8.1 %collective-permute-done.4 = f32[16,12544]{1,0:T(8,128)S(1)} collective-permute-done((f32[16,12544]{1,0:T(8,128)S(1)}, f32[16,12544]{1,0:T(8,128)S(1)}, u32[]{:S(2)}, u32[]{:S(2)}) %collective-permute-start.4) | collective-permute-done | bytes 802848 | tf_op jit(solution)/shard_map/ppermute | solution.py:153
  103.4 1.2 bitcast_add_fusion.2
  104.6 2.1 collective-permute-start.5
  108.6 8.2 %collective-permute-done.5 = f32[16,12544]{1,0:T(8,128)S(1)} collective-permute-done((f32[16,12544]{1,0:T(8,128)S(1)}, f32[16,12544]{1,0:T(8,128)S(1)}, u32[]{:S(2)}, u32[]{:S(2)}) %collective-permute-start.5) | collective-permute-done | bytes 802848 | tf_op jit(solution)/shard_map/ppermute | solution.py:153
  116.8 1.2 bitcast_add_fusion.1
  118.1 2.3 collective-permute-start.6
  122.3 8.1 %collective-permute-done.6 = f32[16,12544]{1,0:T(8,128)S(1)} collective-permute-done((f32[16,12544]{1,0:T(8,128)S(1)}, f32[16,12544]{1,0:T(8,128)S(1)}, u32[]{:S(2)}, u32[]{:S(2)}) %collective-permute-start.6) | collective-permute-done | bytes 802848 | tf_op jit(solution)/shard_map/ppermute | solution.py:153
  130.5 2.1 bitcast_add_fusion
  132.6 1.6 reshape.33
  134.2 1.6 copy.15
  135.7 1.9 convolution_multiply_fusion
  137.6 0.1 reshape.34
  137.7 3.2 %collective-permute-start.7 = (f32[16,1024]{1,0:T(8,128)S(1)}, f32[16,1024]{1,0:T(8,128)S(1)}, u32[]{:S(2)}, u32[]{:S(2)}) collective-permute-start(f32[16,1024]{1,0:T(8,128)S(1)} %reshape.34), channel_id=1, source_target_pairs={{0,8},{1,9},{2,10},{3,11},{4,12},{5,13},{6,14},{7,15},{8,0},{9,1},... | collective-permute-start | bytes 196616 | tf_op jit(solution)/shard_map/ppermute | solution.py:165
  140.9 2.2 collective-permute-done.7
  143.2 2.0 collective-permute-start.8
  145.1 3.1 %collective-permute-done.8 = f32[32,1024]{1,0:T(8,128)S(1)} collective-permute-done((f32[32,1024]{1,0:T(8,128)S(1)}, f32[32,1024]{1,0:T(8,128)S(1)}, u32[]{:S(2)}, u32[]{:S(2)}) %collective-permute-start.8) | collective-permute-done | bytes 131104 | tf_op jit(solution)/shard_map/ppermute | solution.py:165
  148.2 1.9 collective-permute-start.9
  150.1 4.5 %collective-permute-done.9 = f32[64,1024]{1,0:T(8,128)S(1)} collective-permute-done((f32[64,1024]{1,0:T(8,128)S(1)}, f32[64,1024]{1,0:T(8,128)S(1)}, u32[]{:S(2)}, u32[]{:S(2)}) %collective-permute-start.9) | collective-permute-done | bytes 262176 | tf_op jit(solution)/shard_map/ppermute | solution.py:165
  154.7 0.1 collective-permute-start.10
  154.8 0.8 broadcast_in_dim_reshape.3
  155.6 1.1 collective-permute-done.10
  156.7 94.1 %shard_map.77 = f32[128,1024]{1,0:T(8,128)} custom-call(f32[256,1024]{1,0:T(8,128)S(1)} %constant_dynamic-update-slice_fusion.f_ref, s32[1]{0:T(128)} %bitcast.28.c_ref), custom_call_target="tpu_custom_call" | custom-call | tf_op jit(solution)/shard_map/pallas_call | solution.py:86
  (11 shorter events, 0.2 us)
Async XLA Ops:
  0.6 21.9 %copy-start = (bf16[128,32,196]{0,1,2:T(8,128)(2,1)S(1)}, bf16[128,32,196]{0,1,2:T(8,128)(2,1)}, u32[]{:S(2)}) copy-start(bf16[128,32,196]{0,1,2:T(8,128)(2,1)} %param.7) | copy-start | bytes 4816900
  10.4 7.2 %copy-start.1 = (s32[32,288]{1,0:T(8,128)S(1)}, s32[32,288]{1,0:T(8,128)}, u32[]{:S(2)}) copy-start(s32[32,288]{1,0:T(8,128)} %param.8) | copy-start | bytes 110596
  17.6 5.0 %copy-start.2 = (s32[32,32]{1,0:T(8,128)S(1)}, s32[32,32]{1,0:T(8,128)}, u32[]{:S(2)}) copy-start(s32[32,32]{1,0:T(8,128)} %param.9) | copy-start | bytes 12292
  36.5 13.2 %collective-permute-start = (f32[16,12544]{1,0:T(8,128)S(1)}, f32[16,12544]{1,0:T(8,128)S(1)}, u32[]{:S(2)}, u32[]{:S(2)}) collective-permute-start(f32[16,12544]{1,0:T(8,128)S(1)} %dynamic-slice_bitcast_fusion), channel_id=1, source_target_pairs={{0,4},{5,1},{4,8},{9,5},{8,12},{13,9},{12,14},{15,13},{14,10},{11,... | collective-permute-start | bytes 2408456 | tf_op jit(solution)/shard_map/ppermute | solution.py:153
  50.9 12.2 %collective-permute-start.1 = (f32[16,12544]{1,0:T(8,128)S(1)}, f32[16,12544]{1,0:T(8,128)S(1)}, u32[]{:S(2)}, u32[]{:S(2)}) collective-permute-start(f32[16,12544]{1,0:T(8,128)S(1)} %bitcast_add_fusion.6), channel_id=1, source_target_pairs={{0,4},{5,1},{4,8},{9,5},{8,12},{13,9},{12,14},{15,13},{14,10},{11,... | collective-permute-start | bytes 2408456 | tf_op jit(solution)/shard_map/ppermute | solution.py:153
  64.3 12.2 %collective-permute-start.2 = (f32[16,12544]{1,0:T(8,128)S(1)}, f32[16,12544]{1,0:T(8,128)S(1)}, u32[]{:S(2)}, u32[]{:S(2)}) collective-permute-start(f32[16,12544]{1,0:T(8,128)S(1)} %bitcast_add_fusion.5), channel_id=1, source_target_pairs={{0,4},{5,1},{4,8},{9,5},{8,12},{13,9},{12,14},{15,13},{14,10},{11,... | collective-permute-start | bytes 2408456 | tf_op jit(solution)/shard_map/ppermute | solution.py:153
  77.7 12.2 %collective-permute-start.3 = (f32[16,12544]{1,0:T(8,128)S(1)}, f32[16,12544]{1,0:T(8,128)S(1)}, u32[]{:S(2)}, u32[]{:S(2)}) collective-permute-start(f32[16,12544]{1,0:T(8,128)S(1)} %bitcast_add_fusion.4), channel_id=1, source_target_pairs={{0,4},{5,1},{4,8},{9,5},{8,12},{13,9},{12,14},{15,13},{14,10},{11,... | collective-permute-start | bytes 2408456 | tf_op jit(solution)/shard_map/ppermute | solution.py:153
  91.2 12.2 %collective-permute-start.4 = (f32[16,12544]{1,0:T(8,128)S(1)}, f32[16,12544]{1,0:T(8,128)S(1)}, u32[]{:S(2)}, u32[]{:S(2)}) collective-permute-start(f32[16,12544]{1,0:T(8,128)S(1)} %bitcast_add_fusion.3), channel_id=1, source_target_pairs={{0,4},{5,1},{4,8},{9,5},{8,12},{13,9},{12,14},{15,13},{14,10},{11,... | collective-permute-start | bytes 2408456 | tf_op jit(solution)/shard_map/ppermute | solution.py:153
  104.6 12.2 %collective-permute-start.5 = (f32[16,12544]{1,0:T(8,128)S(1)}, f32[16,12544]{1,0:T(8,128)S(1)}, u32[]{:S(2)}, u32[]{:S(2)}) collective-permute-start(f32[16,12544]{1,0:T(8,128)S(1)} %bitcast_add_fusion.2), channel_id=1, source_target_pairs={{0,4},{5,1},{4,8},{9,5},{8,12},{13,9},{12,14},{15,13},{14,10},{11,... | collective-permute-start | bytes 2408456 | tf_op jit(solution)/shard_map/ppermute | solution.py:153
  118.1 12.4 %collective-permute-start.6 = (f32[16,12544]{1,0:T(8,128)S(1)}, f32[16,12544]{1,0:T(8,128)S(1)}, u32[]{:S(2)}, u32[]{:S(2)}) collective-permute-start(f32[16,12544]{1,0:T(8,128)S(1)} %bitcast_add_fusion.1), channel_id=1, source_target_pairs={{0,4},{5,1},{4,8},{9,5},{8,12},{13,9},{12,14},{15,13},{14,10},{11,... | collective-permute-start | bytes 2408456 | tf_op jit(solution)/shard_map/ppermute | solution.py:153
  137.7 5.4 %collective-permute-start.7 = (f32[16,1024]{1,0:T(8,128)S(1)}, f32[16,1024]{1,0:T(8,128)S(1)}, u32[]{:S(2)}, u32[]{:S(2)}) collective-permute-start(f32[16,1024]{1,0:T(8,128)S(1)} %reshape.34), channel_id=1, source_target_pairs={{0,8},{1,9},{2,10},{3,11},{4,12},{5,13},{6,14},{7,15},{8,0},{9,1},... | collective-permute-start | bytes 196616 | tf_op jit(solution)/shard_map/ppermute | solution.py:165
  143.2 5.0 %collective-permute-start.8 = (f32[32,1024]{1,0:T(8,128)S(1)}, f32[32,1024]{1,0:T(8,128)S(1)}, u32[]{:S(2)}, u32[]{:S(2)}) collective-permute-start(f32[32,1024]{1,0:T(8,128)S(1)} %pad_maximum_fusion.3), channel_id=1, source_target_pairs={{0,4},{1,5},{2,6},{3,7},{4,0},{5,1},{6,2},{7,3},{8,12},{9,13},{10,... | collective-permute-start | bytes 393224 | tf_op jit(solution)/shard_map/ppermute | solution.py:165
  148.2 6.4 %collective-permute-start.9 = (f32[64,1024]{1,0:T(8,128)S(1)}, f32[64,1024]{1,0:T(8,128)S(1)}, u32[]{:S(2)}, u32[]{:S(2)}) collective-permute-start(f32[64,1024]{1,0:T(8,128)S(1)} %pad_maximum_fusion.2), channel_id=1, source_target_pairs={{0,2},{1,3},{2,0},{3,1},{4,6},{5,7},{6,4},{7,5},{8,10},{9,11},{10,... | collective-permute-start | bytes 786440 | tf_op jit(solution)/shard_map/ppermute | solution.py:165
  154.7 2.0 collective-permute-start.10

commit v15 on v14

--- a/solution.py
+++ b/solution.py
@@ -36,11 +36,7 @@
         w_ref[i, :, i * b:(i + 1) * b] = g[:, i * b:(i + 1) * b] + eye
 
     def diag(k):
-        wk = w_ref[k]
-        d = jnp.zeros((b, b), jnp.float32)
-        for j in range(nb):
-            d = jnp.where(k == j, wk[:, j * b:(j + 1) * b], d)
-        return d
+        return w_ref[k, :, pl.ds(pl.multiple_of(k * b, b), b)]
 
     def panel(k, rkk, linv):
         pfull = jnp.dot(linv, w_ref[k], precision=HI, preferred_element_type=jnp.float32)
@@ -56,10 +52,7 @@
     def step(k, carry):
         rkk, linv = carry
         k1 = k + 1
-        wk = w_ref[k]
-        a1 = jnp.zeros((b, b), jnp.float32)
-        for j in range(nb):
-            a1 = jnp.where(k1 == j, wk[:, j * b:(j + 1) * b], a1)
+        a1 = w_ref[k, :, pl.ds(pl.multiple_of(k1 * b, b), b)]
         t1 = jnp.dot(linv, a1, precision=HI, preferred_element_type=jnp.float32)
         d1 = diag(k1) - lax.dot_general(t1, t1, (((0,), (0,)), ((), ())), precision=HI,
                                         preferred_element_type=jnp.float32)

time: 252 us -> 252 us (level)
  no operation moved by 1% of the time
where the time goes in v15:
time: 252 us; the launch traced here: 251 us
  Pallas kernels  94.1 us (37%)
  waiting for transfers between devices  68.4 us (27%)
  local copies, waits for them, and re-layouts  23.7 us (9%)
  starting transfers between devices  23.2 us (9%)
  between operations  21.2 us (8%)
  other arithmetic  12.9 us (5%)
  matrix products  7.26 us (3%)
    pallas_call x1, Pallas kernels, damped_cholesky(): pl.pallas_call(functools.partial(_chol_kernel, nb=nb, b=b, scale=scale),...  94.1 us
    ppermute x7, waiting for transfers between devices, ring_reduce_scatter(): acc = lax.ppermute(acc, (axis, pair), ring) + take(step)  57.5 us
    ppermute x7, starting transfers between devices, ring_reduce_scatter(): acc = lax.ppermute(acc, (axis, pair), ring) + take(step)  16.1 us
    ppermute x4, waiting for transfers between devices, doubling_gather(): other = lax.ppermute(x, axes, [(i, i ^ k) for i in range(size)])  10.9 us
    add x7, other arithmetic, ring_reduce_scatter(): acc = lax.ppermute(acc, (axis, pair), ring) + take(step)  9.45 us
    reshape x1, local copies, waits for them, and re-layouts, local(): both = both.reshape(-1, samples).T  8.05 us
    unnamed x11, local copies, waits for them, and re-layouts  7.24 us
    ppermute x4, starting transfers between devices, doubling_gather(): other = lax.ppermute(x, axes, [(i, i ^ k) for i in range(size)])  7.1 us
  transfers between devices with their start and end apart: 11, of which 11 were waited for; matrix products, arithmetic and copies ran while one was open for 0% of the time, Pallas kernels for 0%

profile of v15, /device:TPU:0, one launch (start us, length us, event | category | flops | bytes accessed | tf_op | source)
XLA Modules:
  0.0 250.8 jit_solution(8829727956186726279)
XLA Ops:
  0.6 0.0 copy-start
  0.6 1.4 dynamic_slice.52
  7.3 1.7 fusion.10
  10.4 0.0 copy-start.1
  10.4 7.2 %copy.11 = bf16[128,32,784]{0,1,2:T(8,128)(2,1)} copy(bf16[128,32,784]{0,2,1:T(8,128)(2,1)} %param.6) | data formatting | bytes 12845056 | tf_op args[0]
  17.6 0.1 copy.17
  17.7 4.8 %fusion.11 = f32[128,32,14,14]{0,1,3,2:T(8,128)S(1)} fusion(bf16[128,32,28,28]{0,1,3,2:T(8,128)(2,1)} %bitcast.53, bf16[32,3,3,32]{0,3,2,1:T(8,128)(2,1)S(1)} %bitcast.56), kind=kOutput, calls=%fused_computation.33 | convolution fusion | flops 440664064 | bytes 9652224 | tf_op jit(solution)/shard_map/conv_general_dilated | solution.py:97
  22.5 0.0 copy-done
  22.5 0.0 copy-done.2
  22.5 0.6 convolution_bitcast_fusion
  23.2 3.4 %pad_maximum_fusion = f32[196,64,128]{2,1,0:T(8,128)} fusion(f32[196,32,128]{2,1,0:T(8,128)S(1)} %convolution_bitcast_fusion, f32[196,32,128]{2,1,0:T(8,128)S(1)} %bitcast.55), kind=kLoop, calls=%fused_computation | loop fusion | flops 1605632 | bytes 12845056 | tf_op jit(solution)/shard_map/concatenate | solution.py:169
  26.5 8.1 %copy.14 = f32[12544,128]{0,1:T(8,128)} copy(f32[12544,128]{1,0:T(8,128)} %bitcast.52) | data formatting | bytes 12845056 | tf_op jit(solution)/shard_map/reshape | solution.py:170
  35.3 1.2 dynamic-slice_bitcast_fusion
  36.5 3.1 %collective-permute-start = (f32[16,12544]{1,0:T(8,128)S(1)}, f32[16,12544]{1,0:T(8,128)S(1)}, u32[]{:S(2)}, u32[]{:S(2)}) collective-permute-start(f32[16,12544]{1,0:T(8,128)S(1)} %dynamic-slice_bitcast_fusion), channel_id=1, source_target_pairs={{0,4},{5,1},{4,8},{9,5},{8,12},{13,9},{12,14},{15,13},{14,10},{11,... | collective-permute-start | bytes 2408456 | tf_op jit(solution)/shard_map/ppermute | solution.py:146
  41.4 8.2 %collective-permute-done = f32[16,12544]{1,0:T(8,128)S(1)} collective-permute-done((f32[16,12544]{1,0:T(8,128)S(1)}, f32[16,12544]{1,0:T(8,128)S(1)}, u32[]{:S(2)}, u32[]{:S(2)}) %collective-permute-start) | collective-permute-done | bytes 802848 | tf_op jit(solution)/shard_map/ppermute | solution.py:146
  49.6 1.2 bitcast_add_fusion.6
  50.9 2.1 collective-permute-start.1
  54.9 8.2 %collective-permute-done.1 = f32[16,12544]{1,0:T(8,128)S(1)} collective-permute-done((f32[16,12544]{1,0:T(8,128)S(1)}, f32[16,12544]{1,0:T(8,128)S(1)}, u32[]{:S(2)}, u32[]{:S(2)}) %collective-permute-start.1) | collective-permute-done | bytes 802848 | tf_op jit(solution)/shard_map/ppermute | solution.py:146
  63.1 1.2 bitcast_add_fusion.5
  64.3 2.1 collective-permute-start.2
  68.2 8.4 %collective-permute-done.2 = f32[16,12544]{1,0:T(8,128)S(1)} collective-permute-done((f32[16,12544]{1,0:T(8,128)S(1)}, f32[16,12544]{1,0:T(8,128)S(1)}, u32[]{:S(2)}, u32[]{:S(2)}) %collective-permute-start.2) | collective-permute-done | bytes 802848 | tf_op jit(solution)/shard_map/ppermute | solution.py:146
  76.5 1.2 bitcast_add_fusion.4
  77.7 2.1 collective-permute-start.3
  81.7 8.2 %collective-permute-done.3 = f32[16,12544]{1,0:T(8,128)S(1)} collective-permute-done((f32[16,12544]{1,0:T(8,128)S(1)}, f32[16,12544]{1,0:T(8,128)S(1)}, u32[]{:S(2)}, u32[]{:S(2)}) %collective-permute-start.3) | collective-permute-done | bytes 802848 | tf_op jit(solution)/shard_map/ppermute | solution.py:146
  90.0 1.2 bitcast_add_fusion.3
  91.2 2.1 collective-permute-start.4
  95.3 8.1 %collective-permute-done.4 = f32[16,12544]{1,0:T(8,128)S(1)} collective-permute-done((f32[16,12544]{1,0:T(8,128)S(1)}, f32[16,12544]{1,0:T(8,128)S(1)}, u32[]{:S(2)}, u32[]{:S(2)}) %collective-permute-start.4) | collective-permute-done | bytes 802848 | tf_op jit(solution)/shard_map/ppermute | solution.py:146
  103.4 1.2 bitcast_add_fusion.2
  104.6 2.1 collective-permute-start.5
  108.6 8.2 %collective-permute-done.5 = f32[16,12544]{1,0:T(8,128)S(1)} collective-permute-done((f32[16,12544]{1,0:T(8,128)S(1)}, f32[16,12544]{1,0:T(8,128)S(1)}, u32[]{:S(2)}, u32[]{:S(2)}) %collective-permute-start.5) | collective-permute-done | bytes 802848 | tf_op jit(solution)/shard_map/ppermute | solution.py:146
  116.8 1.2 bitcast_add_fusion.1
  118.1 2.3 collective-permute-start.6
  122.3 8.1 %collective-permute-done.6 = f32[16,12544]{1,0:T(8,128)S(1)} collective-permute-done((f32[16,12544]{1,0:T(8,128)S(1)}, f32[16,12544]{1,0:T(8,128)S(1)}, u32[]{:S(2)}, u32[]{:S(2)}) %collective-permute-start.6) | collective-permute-done | bytes 802848 | tf_op jit(solution)/shard_map/ppermute | solution.py:146
  130.5 2.1 bitcast_add_fusion
  132.6 1.6 reshape.33
  134.2 1.6 copy.15
  135.7 1.9 convolution_multiply_fusion
  137.6 0.1 reshape.34
  137.7 3.2 %collective-permute-start.7 = (f32[16,1024]{1,0:T(8,128)S(1)}, f32[16,1024]{1,0:T(8,128)S(1)}, u32[]{:S(2)}, u32[]{:S(2)}) collective-permute-start(f32[16,1024]{1,0:T(8,128)S(1)} %reshape.34), channel_id=1, source_target_pairs={{0,8},{1,9},{2,10},{3,11},{4,12},{5,13},{6,14},{7,15},{8,0},{9,1},... | collective-permute-start | bytes 196616 | tf_op jit(solution)/shard_map/ppermute | solution.py:158
  140.9 2.2 collective-permute-done.7
  143.2 2.0 collective-permute-start.8
  145.1 3.1 %collective-permute-done.8 = f32[32,1024]{1,0:T(8,128)S(1)} collective-permute-done((f32[32,1024]{1,0:T(8,128)S(1)}, f32[32,1024]{1,0:T(8,128)S(1)}, u32[]{:S(2)}, u32[]{:S(2)}) %collective-permute-start.8) | collective-permute-done | bytes 131104 | tf_op jit(solution)/shard_map/ppermute | solution.py:158
  148.2 1.9 collective-permute-start.9
  150.1 4.5 %collective-permute-done.9 = f32[64,1024]{1,0:T(8,128)S(1)} collective-permute-done((f32[64,1024]{1,0:T(8,128)S(1)}, f32[64,1024]{1,0:T(8,128)S(1)}, u32[]{:S(2)}, u32[]{:S(2)}) %collective-permute-start.9) | collective-permute-done | bytes 262176 | tf_op jit(solution)/shard_map/ppermute | solution.py:158
  154.7 0.1 collective-permute-start.10
  154.8 0.8 broadcast_in_dim_reshape.3
  155.6 1.1 collective-permute-done.10
  156.7 94.1 %shard_map.77 = f32[128,1024]{1,0:T(8,128)} custom-call(f32[256,1024]{1,0:T(8,128)S(1)} %constant_dynamic-update-slice_fusion.f_ref, s32[1]{0:T(128)} %bitcast.28.c_ref), custom_call_target="tpu_custom_call" | custom-call | tf_op jit(solution)/shard_map/pallas_call | solution.py:79
  (11 shorter events, 0.2 us)
Async XLA Ops:
  0.6 21.9 %copy-start = (bf16[128,32,196]{0,1,2:T(8,128)(2,1)S(1)}, bf16[128,32,196]{0,1,2:T(8,128)(2,1)}, u32[]{:S(2)}) copy-start(bf16[128,32,196]{0,1,2:T(8,128)(2,1)} %param.7) | copy-start | bytes 4816900
  10.4 7.2 %copy-start.1 = (s32[32,288]{1,0:T(8,128)S(1)}, s32[32,288]{1,0:T(8,128)}, u32[]{:S(2)}) copy-start(s32[32,288]{1,0:T(8,128)} %param.8) | copy-start | bytes 110596
  17.6 5.0 %copy-start.2 = (s32[32,32]{1,0:T(8,128)S(1)}, s32[32,32]{1,0:T(8,128)}, u32[]{:S(2)}) copy-start(s32[32,32]{1,0:T(8,128)} %param.9) | copy-start | bytes 12292
  36.5 13.2 %collective-permute-start = (f32[16,12544]{1,0:T(8,128)S(1)}, f32[16,12544]{1,0:T(8,128)S(1)}, u32[]{:S(2)}, u32[]{:S(2)}) collective-permute-start(f32[16,12544]{1,0:T(8,128)S(1)} %dynamic-slice_bitcast_fusion), channel_id=1, source_target_pairs={{0,4},{5,1},{4,8},{9,5},{8,12},{13,9},{12,14},{15,13},{14,10},{11,... | collective-permute-start | bytes 2408456 | tf_op jit(solution)/shard_map/ppermute | solution.py:146
  50.9 12.2 %collective-permute-start.1 = (f32[16,12544]{1,0:T(8,128)S(1)}, f32[16,12544]{1,0:T(8,128)S(1)}, u32[]{:S(2)}, u32[]{:S(2)}) collective-permute-start(f32[16,12544]{1,0:T(8,128)S(1)} %bitcast_add_fusion.6), channel_id=1, source_target_pairs={{0,4},{5,1},{4,8},{9,5},{8,12},{13,9},{12,14},{15,13},{14,10},{11,... | collective-permute-start | bytes 2408456 | tf_op jit(solution)/shard_map/ppermute | solution.py:146
  64.3 12.2 %collective-permute-start.2 = (f32[16,12544]{1,0:T(8,128)S(1)}, f32[16,12544]{1,0:T(8,128)S(1)}, u32[]{:S(2)}, u32[]{:S(2)}) collective-permute-start(f32[16,12544]{1,0:T(8,128)S(1)} %bitcast_add_fusion.5), channel_id=1, source_target_pairs={{0,4},{5,1},{4,8},{9,5},{8,12},{13,9},{12,14},{15,13},{14,10},{11,... | collective-permute-start | bytes 2408456 | tf_op jit(solution)/shard_map/ppermute | solution.py:146
  77.7 12.2 %collective-permute-start.3 = (f32[16,12544]{1,0:T(8,128)S(1)}, f32[16,12544]{1,0:T(8,128)S(1)}, u32[]{:S(2)}, u32[]{:S(2)}) collective-permute-start(f32[16,12544]{1,0:T(8,128)S(1)} %bitcast_add_fusion.4), channel_id=1, source_target_pairs={{0,4},{5,1},{4,8},{9,5},{8,12},{13,9},{12,14},{15,13},{14,10},{11,... | collective-permute-start | bytes 2408456 | tf_op jit(solution)/shard_map/ppermute | solution.py:146
  91.2 12.2 %collective-permute-start.4 = (f32[16,12544]{1,0:T(8,128)S(1)}, f32[16,12544]{1,0:T(8,128)S(1)}, u32[]{:S(2)}, u32[]{:S(2)}) collective-permute-start(f32[16,12544]{1,0:T(8,128)S(1)} %bitcast_add_fusion.3), channel_id=1, source_target_pairs={{0,4},{5,1},{4,8},{9,5},{8,12},{13,9},{12,14},{15,13},{14,10},{11,... | collective-permute-start | bytes 2408456 | tf_op jit(solution)/shard_map/ppermute | solution.py:146
  104.6 12.2 %collective-permute-start.5 = (f32[16,12544]{1,0:T(8,128)S(1)}, f32[16,12544]{1,0:T(8,128)S(1)}, u32[]{:S(2)}, u32[]{:S(2)}) collective-permute-start(f32[16,12544]{1,0:T(8,128)S(1)} %bitcast_add_fusion.2), channel_id=1, source_target_pairs={{0,4},{5,1},{4,8},{9,5},{8,12},{13,9},{12,14},{15,13},{14,10},{11,... | collective-permute-start | bytes 2408456 | tf_op jit(solution)/shard_map/ppermute | solution.py:146
  118.1 12.4 %collective-permute-start.6 = (f32[16,12544]{1,0:T(8,128)S(1)}, f32[16,12544]{1,0:T(8,128)S(1)}, u32[]{:S(2)}, u32[]{:S(2)}) collective-permute-start(f32[16,12544]{1,0:T(8,128)S(1)} %bitcast_add_fusion.1), channel_id=1, source_target_pairs={{0,4},{5,1},{4,8},{9,5},{8,12},{13,9},{12,14},{15,13},{14,10},{11,... | collective-permute-start | bytes 2408456 | tf_op jit(solution)/shard_map/ppermute | solution.py:146
  137.7 5.4 %collective-permute-start.7 = (f32[16,1024]{1,0:T(8,128)S(1)}, f32[16,1024]{1,0:T(8,128)S(1)}, u32[]{:S(2)}, u32[]{:S(2)}) collective-permute-start(f32[16,1024]{1,0:T(8,128)S(1)} %reshape.34), channel_id=1, source_target_pairs={{0,8},{1,9},{2,10},{3,11},{4,12},{5,13},{6,14},{7,15},{8,0},{9,1},... | collective-permute-start | bytes 196616 | tf_op jit(solution)/shard_map/ppermute | solution.py:158
  143.2 5.0 %collective-permute-start.8 = (f32[32,1024]{1,0:T(8,128)S(1)}, f32[32,1024]{1,0:T(8,128)S(1)}, u32[]{:S(2)}, u32[]{:S(2)}) collective-permute-start(f32[32,1024]{1,0:T(8,128)S(1)} %pad_maximum_fusion.3), channel_id=1, source_target_pairs={{0,4},{1,5},{2,6},{3,7},{4,0},{5,1},{6,2},{7,3},{8,12},{9,13},{10,... | collective-permute-start | bytes 393224 | tf_op jit(solution)/shard_map/ppermute | solution.py:158
  148.2 6.4 %collective-permute-start.9 = (f32[64,1024]{1,0:T(8,128)S(1)}, f32[64,1024]{1,0:T(8,128)S(1)}, u32[]{:S(2)}, u32[]{:S(2)}) collective-permute-start(f32[64,1024]{1,0:T(8,128)S(1)} %pad_maximum_fusion.2), channel_id=1, source_target_pairs={{0,2},{1,3},{2,0},{3,1},{4,6},{5,7},{6,4},{7,5},{8,10},{9,11},{10,... | collective-permute-start | bytes 786440 | tf_op jit(solution)/shard_map/ppermute | solution.py:158
  154.7 2.0 collective-permute-start.10

commit v16 on v14

--- a/solution.py
+++ b/solution.py
@@ -118,9 +118,9 @@
 def sketch(in_sum, out_sum, total_channels):
     in_feat = in_sum / math.sqrt(9 * total_channels)
     out_feat = out_sum / math.sqrt(total_channels)
-    cells = in_sum.shape[2]
+    cells = in_sum.shape[1]
     outer = jnp.einsum(
-        "nlp,njp->nlj", out_feat, in_feat, precision=lax.Precision.HIGHEST
+        "npl,npj->nlj", out_feat, in_feat, precision=lax.Precision.HIGHEST
     ) / math.sqrt(cells)
     return outer.reshape(outer.shape[0], -1)
 
@@ -176,9 +176,9 @@
     both = jnp.concatenate([jnp.transpose(in_part, (2, 1, 0)), jnp.transpose(out_part, (2, 1, 0))], axis=1)
     both = both.reshape(-1, samples).T
     both = ring_reduce_scatter(both, "chan", "samp")
-    both = jnp.transpose(both.reshape(both.shape[0], cells, -1), (0, 2, 1))
-    in_sum = both[:, :width_in]
-    out_sum = both[:, width_in:]
+    both = both.reshape(both.shape[0], cells, -1)
+    in_sum = both[:, :, :width_in]
+    out_sum = both[:, :, width_in:]
     own = sketch(in_sum, out_sum, C)
     every = doubling_gather(own, ("chan", "samp"))
     batch_total = samples * lax.axis_size("samp")

time: 252 us -> 255 us (1.012)
  local copies, waits for them, and re-layouts: 23.7 us -> 28.3 us
    unnamed x11 -> x13, local copies, waits for them, and re-layouts: 7.24 us -> 11.3 us
where the time goes in v16:
time: 255 us; the launch traced here: 254 us
  Pallas kernels  94.1 us (37%)
  waiting for transfers between devices  68.3 us (27%)
  local copies, waits for them, and re-layouts  28.3 us (11%)
  starting transfers between devices  23.1 us (9%)
  between operations  21.2 us (8%)
  other arithmetic  12.9 us (5%)
  matrix products  6.07 us (2%)
    pallas_call x1, Pallas kernels, damped_cholesky(): pl.pallas_call(functools.partial(_chol_kernel, nb=nb, b=b, scale=scale),...  94.1 us
    ppermute x7, waiting for transfers between devices, ring_reduce_scatter(): acc = lax.ppermute(acc, (axis, pair), ring) + take(step)  57.4 us
    ppermute x7, starting transfers between devices, ring_reduce_scatter(): acc = lax.ppermute(acc, (axis, pair), ring) + take(step)  16 us
    unnamed x13, local copies, waits for them, and re-layouts  11.3 us
    ppermute x4, waiting for transfers between devices, doubling_gather(): other = lax.ppermute(x, axes, [(i, i ^ k) for i in range(size)])  10.9 us
    add x7, other arithmetic, ring_reduce_scatter(): acc = lax.ppermute(acc, (axis, pair), ring) + take(step)  9.45 us
    reshape x1, local copies, waits for them, and re-layouts, local(): both = both.reshape(-1, samples).T  8 us
    ppermute x4, starting transfers between devices, doubling_gather(): other = lax.ppermute(x, axes, [(i, i ^ k) for i in range(size)])  7.1 us
  transfers between devices with their start and end apart: 11, of which 11 were waited for; matrix products, arithmetic and copies ran while one was open for 0% of the time, Pallas kernels for 0%

profile of v16, /device:TPU:0, one launch (start us, length us, event | category | flops | bytes accessed | tf_op | source)
XLA Modules:
  0.0 254.0 jit_solution(15017517869889861846)
XLA Ops:
  0.6 0.0 copy-start
  0.6 1.4 dynamic_slice.52
  7.3 1.6 fusion.13
  10.2 0.0 copy-start.1
  10.2 7.2 %copy.11 = bf16[128,32,784]{0,1,2:T(8,128)(2,1)} copy(bf16[128,32,784]{0,2,1:T(8,128)(2,1)} %param.6) | data formatting | bytes 12845056 | tf_op args[0]
  17.4 0.1 copy.18
  17.6 4.8 %fusion.14 = f32[128,32,14,14]{0,1,3,2:T(8,128)S(1)} fusion(bf16[128,32,28,28]{0,1,3,2:T(8,128)(2,1)} %bitcast.52, bf16[32,3,3,32]{0,3,2,1:T(8,128)(2,1)S(1)} %bitcast.54), kind=kOutput, calls=%fused_computation.34 | convolution fusion | flops 440664064 | bytes 9652224 | tf_op jit(solution)/shard_map/conv_general_dilated | solution.py:104
  22.4 0.6 convolution_bitcast_fusion
  23.0 3.4 %pad_maximum_fusion = f32[196,64,128]{2,1,0:T(8,128)} fusion(f32[196,32,128]{2,1,0:T(8,128)S(1)} %convolution_bitcast_fusion, f32[196,32,128]{2,1,0:T(8,128)S(1)} %bitcast.53), kind=kLoop, calls=%fused_computation | loop fusion | flops 1605632 | bytes 12845056 | tf_op jit(solution)/shard_map/concatenate | solution.py:176
  26.4 8.0 %copy.14 = f32[12544,128]{0,1:T(8,128)} copy(f32[12544,128]{1,0:T(8,128)} %bitcast.51) | data formatting | bytes 12845056 | tf_op jit(solution)/shard_map/reshape | solution.py:177
  35.0 1.2 dynamic-slice_bitcast_fusion
  36.2 3.1 %collective-permute-start = (f32[16,12544]{1,0:T(8,128)S(1)}, f32[16,12544]{1,0:T(8,128)S(1)}, u32[]{:S(2)}, u32[]{:S(2)}) collective-permute-start(f32[16,12544]{1,0:T(8,128)S(1)} %dynamic-slice_bitcast_fusion), channel_id=1, source_target_pairs={{0,4},{5,1},{4,8},{9,5},{8,12},{13,9},{12,14},{15,13},{14,10},{11,... | collective-permute-start | bytes 2408456 | tf_op jit(solution)/shard_map/ppermute | solution.py:153
  41.3 8.0 %collective-permute-done = f32[16,12544]{1,0:T(8,128)S(1)} collective-permute-done((f32[16,12544]{1,0:T(8,128)S(1)}, f32[16,12544]{1,0:T(8,128)S(1)}, u32[]{:S(2)}, u32[]{:S(2)}) %collective-permute-start) | collective-permute-done | bytes 802848 | tf_op jit(solution)/shard_map/ppermute | solution.py:153
  49.4 1.2 bitcast_add_fusion.6
  50.6 2.1 collective-permute-start.1
  54.6 8.2 %collective-permute-done.1 = f32[16,12544]{1,0:T(8,128)S(1)} collective-permute-done((f32[16,12544]{1,0:T(8,128)S(1)}, f32[16,12544]{1,0:T(8,128)S(1)}, u32[]{:S(2)}, u32[]{:S(2)}) %collective-permute-start.1) | collective-permute-done | bytes 802848 | tf_op jit(solution)/shard_map/ppermute | solution.py:153
  62.8 1.2 bitcast_add_fusion.5
  64.0 2.1 collective-permute-start.2
  68.0 8.2 %collective-permute-done.2 = f32[16,12544]{1,0:T(8,128)S(1)} collective-permute-done((f32[16,12544]{1,0:T(8,128)S(1)}, f32[16,12544]{1,0:T(8,128)S(1)}, u32[]{:S(2)}, u32[]{:S(2)}) %collective-permute-start.2) | collective-permute-done | bytes 802848 | tf_op jit(solution)/shard_map/ppermute | solution.py:153
  76.2 1.2 bitcast_add_fusion.4
  77.5 2.1 collective-permute-start.3
  81.3 8.4 %collective-permute-done.3 = f32[16,12544]{1,0:T(8,128)S(1)} collective-permute-done((f32[16,12544]{1,0:T(8,128)S(1)}, f32[16,12544]{1,0:T(8,128)S(1)}, u32[]{:S(2)}, u32[]{:S(2)}) %collective-permute-start.3) | collective-permute-done | bytes 802848 | tf_op jit(solution)/shard_map/ppermute | solution.py:153
  89.7 1.2 bitcast_add_fusion.3
  90.9 2.1 collective-permute-start.4
  95.0 8.1 %collective-permute-done.4 = f32[16,12544]{1,0:T(8,128)S(1)} collective-permute-done((f32[16,12544]{1,0:T(8,128)S(1)}, f32[16,12544]{1,0:T(8,128)S(1)}, u32[]{:S(2)}, u32[]{:S(2)}) %collective-permute-start.4) | collective-permute-done | bytes 802848 | tf_op jit(solution)/shard_map/ppermute | solution.py:153
  103.1 1.2 bitcast_add_fusion.2
  104.4 2.1 collective-permute-start.5
  108.3 8.2 %collective-permute-done.5 = f32[16,12544]{1,0:T(8,128)S(1)} collective-permute-done((f32[16,12544]{1,0:T(8,128)S(1)}, f32[16,12544]{1,0:T(8,128)S(1)}, u32[]{:S(2)}, u32[]{:S(2)}) %collective-permute-start.5) | collective-permute-done | bytes 802848 | tf_op jit(solution)/shard_map/ppermute | solution.py:153
  116.6 1.2 bitcast_add_fusion.1
  117.8 2.3 collective-permute-start.6
  122.0 8.1 %collective-permute-done.6 = f32[16,12544]{1,0:T(8,128)S(1)} collective-permute-done((f32[16,12544]{1,0:T(8,128)S(1)}, f32[16,12544]{1,0:T(8,128)S(1)}, u32[]{:S(2)}, u32[]{:S(2)}) %collective-permute-start.6) | collective-permute-done | bytes 802848 | tf_op jit(solution)/shard_map/ppermute | solution.py:153
  130.2 2.1 bitcast_add_fusion
  132.3 1.6 reshape.33
  133.9 2.2 fusion.12
  136.1 2.0 copy.20
  138.1 2.0 copy.21
  140.1 0.7 convolution_multiply_fusion
  140.8 0.1 reshape.34
  140.9 3.2 %collective-permute-start.7 = (f32[16,1024]{1,0:T(8,128)S(1)}, f32[16,1024]{1,0:T(8,128)S(1)}, u32[]{:S(2)}, u32[]{:S(2)}) collective-permute-start(f32[16,1024]{1,0:T(8,128)S(1)} %reshape.34), channel_id=1, source_target_pairs={{0,8},{1,9},{2,10},{3,11},{4,12},{5,13},{6,14},{7,15},{8,0},{9,1},... | collective-permute-start | bytes 196616 | tf_op jit(solution)/shard_map/ppermute | solution.py:165
  144.1 2.2 collective-permute-done.7
  146.3 2.0 collective-permute-start.8
  148.3 3.1 %collective-permute-done.8 = f32[32,1024]{1,0:T(8,128)S(1)} collective-permute-done((f32[32,1024]{1,0:T(8,128)S(1)}, f32[32,1024]{1,0:T(8,128)S(1)}, u32[]{:S(2)}, u32[]{:S(2)}) %collective-permute-start.8) | collective-permute-done | bytes 131104 | tf_op jit(solution)/shard_map/ppermute | solution.py:165
  151.4 1.9 collective-permute-start.9
  153.3 4.5 %collective-permute-done.9 = f32[64,1024]{1,0:T(8,128)S(1)} collective-permute-done((f32[64,1024]{1,0:T(8,128)S(1)}, f32[64,1024]{1,0:T(8,128)S(1)}, u32[]{:S(2)}, u32[]{:S(2)}) %collective-permute-start.9) | collective-permute-done | bytes 262176 | tf_op jit(solution)/shard_map/ppermute | solution.py:165
  157.9 0.1 collective-permute-start.10
  157.9 0.8 broadcast_in_dim_reshape.3
  158.8 1.1 collective-permute-done.10
  159.9 94.1 %shard_map.77 = f32[128,1024]{1,0:T(8,128)} custom-call(f32[256,1024]{1,0:T(8,128)S(1)} %constant_dynamic-update-slice_fusion.f_ref, s32[1]{0:T(128)} %bitcast.27.c_ref), custom_call_target="tpu_custom_call" | custom-call | tf_op jit(solution)/shard_map/pallas_call | solution.py:86
  (13 shorter events, 0.2 us)
Async XLA Ops:
  0.6 21.8 %copy-start = (bf16[128,32,196]{0,1,2:T(8,128)(2,1)S(1)}, bf16[128,32,196]{0,1,2:T(8,128)(2,1)}, u32[]{:S(2)}) copy-start(bf16[128,32,196]{0,1,2:T(8,128)(2,1)} %param.7) | copy-start | bytes 4816900
  10.2 7.2 %copy-start.1 = (s32[32,288]{1,0:T(8,128)S(1)}, s32[32,288]{1,0:T(8,128)}, u32[]{:S(2)}) copy-start(s32[32,288]{1,0:T(8,128)} %param.8) | copy-start | bytes 110596
  17.4 5.0 %copy-start.2 = (s32[32,32]{1,0:T(8,128)S(1)}, s32[32,32]{1,0:T(8,128)}, u32[]{:S(2)}) copy-start(s32[32,32]{1,0:T(8,128)} %param.9) | copy-start | bytes 12292
  36.2 13.2 %collective-permute-start = (f32[16,12544]{1,0:T(8,128)S(1)}, f32[16,12544]{1,0:T(8,128)S(1)}, u32[]{:S(2)}, u32[]{:S(2)}) collective-permute-start(f32[16,12544]{1,0:T(8,128)S(1)} %dynamic-slice_bitcast_fusion), channel_id=1, source_target_pairs={{0,4},{5,1},{4,8},{9,5},{8,12},{13,9},{12,14},{15,13},{14,10},{11,... | collective-permute-start | bytes 2408456 | tf_op jit(solution)/shard_map/ppermute | solution.py:153
  50.6 12.2 %collective-permute-start.1 = (f32[16,12544]{1,0:T(8,128)S(1)}, f32[16,12544]{1,0:T(8,128)S(1)}, u32[]{:S(2)}, u32[]{:S(2)}) collective-permute-start(f32[16,12544]{1,0:T(8,128)S(1)} %bitcast_add_fusion.6), channel_id=1, source_target_pairs={{0,4},{5,1},{4,8},{9,5},{8,12},{13,9},{12,14},{15,13},{14,10},{11,... | collective-permute-start | bytes 2408456 | tf_op jit(solution)/shard_map/ppermute | solution.py:153
  64.0 12.2 %collective-permute-start.2 = (f32[16,12544]{1,0:T(8,128)S(1)}, f32[16,12544]{1,0:T(8,128)S(1)}, u32[]{:S(2)}, u32[]{:S(2)}) collective-permute-start(f32[16,12544]{1,0:T(8,128)S(1)} %bitcast_add_fusion.5), channel_id=1, source_target_pairs={{0,4},{5,1},{4,8},{9,5},{8,12},{13,9},{12,14},{15,13},{14,10},{11,... | collective-permute-start | bytes 2408456 | tf_op jit(solution)/shard_map/ppermute | solution.py:153
  77.5 12.2 %collective-permute-start.3 = (f32[16,12544]{1,0:T(8,128)S(1)}, f32[16,12544]{1,0:T(8,128)S(1)}, u32[]{:S(2)}, u32[]{:S(2)}) collective-permute-start(f32[16,12544]{1,0:T(8,128)S(1)} %bitcast_add_fusion.4), channel_id=1, source_target_pairs={{0,4},{5,1},{4,8},{9,5},{8,12},{13,9},{12,14},{15,13},{14,10},{11,... | collective-permute-start | bytes 2408456 | tf_op jit(solution)/shard_map/ppermute | solution.py:153
  90.9 12.2 %collective-permute-start.4 = (f32[16,12544]{1,0:T(8,128)S(1)}, f32[16,12544]{1,0:T(8,128)S(1)}, u32[]{:S(2)}, u32[]{:S(2)}) collective-permute-start(f32[16,12544]{1,0:T(8,128)S(1)} %bitcast_add_fusion.3), channel_id=1, source_target_pairs={{0,4},{5,1},{4,8},{9,5},{8,12},{13,9},{12,14},{15,13},{14,10},{11,... | collective-permute-start | bytes 2408456 | tf_op jit(solution)/shard_map/ppermute | solution.py:153
  104.4 12.2 %collective-permute-start.5 = (f32[16,12544]{1,0:T(8,128)S(1)}, f32[16,12544]{1,0:T(8,128)S(1)}, u32[]{:S(2)}, u32[]{:S(2)}) collective-permute-start(f32[16,12544]{1,0:T(8,128)S(1)} %bitcast_add_fusion.2), channel_id=1, source_target_pairs={{0,4},{5,1},{4,8},{9,5},{8,12},{13,9},{12,14},{15,13},{14,10},{11,... | collective-permute-start | bytes 2408456 | tf_op jit(solution)/shard_map/ppermute | solution.py:153
  117.8 12.4 %collective-permute-start.6 = (f32[16,12544]{1,0:T(8,128)S(1)}, f32[16,12544]{1,0:T(8,128)S(1)}, u32[]{:S(2)}, u32[]{:S(2)}) collective-permute-start(f32[16,12544]{1,0:T(8,128)S(1)} %bitcast_add_fusion.1), channel_id=1, source_target_pairs={{0,4},{5,1},{4,8},{9,5},{8,12},{13,9},{12,14},{15,13},{14,10},{11,... | collective-permute-start | bytes 2408456 | tf_op jit(solution)/shard_map/ppermute | solution.py:153
  140.9 5.4 %collective-permute-start.7 = (f32[16,1024]{1,0:T(8,128)S(1)}, f32[16,1024]{1,0:T(8,128)S(1)}, u32[]{:S(2)}, u32[]{:S(2)}) collective-permute-start(f32[16,1024]{1,0:T(8,128)S(1)} %reshape.34), channel_id=1, source_target_pairs={{0,8},{1,9},{2,10},{3,11},{4,12},{5,13},{6,14},{7,15},{8,0},{9,1},... | collective-permute-start | bytes 196616 | tf_op jit(solution)/shard_map/ppermute | solution.py:165
  146.3 5.0 %collective-permute-start.8 = (f32[32,1024]{1,0:T(8,128)S(1)}, f32[32,1024]{1,0:T(8,128)S(1)}, u32[]{:S(2)}, u32[]{:S(2)}) collective-permute-start(f32[32,1024]{1,0:T(8,128)S(1)} %pad_maximum_fusion.3), channel_id=1, source_target_pairs={{0,4},{1,5},{2,6},{3,7},{4,0},{5,1},{6,2},{7,3},{8,12},{9,13},{10,... | collective-permute-start | bytes 393224 | tf_op jit(solution)/shard_map/ppermute | solution.py:165
  151.4 6.4 %collective-permute-start.9 = (f32[64,1024]{1,0:T(8,128)S(1)}, f32[64,1024]{1,0:T(8,128)S(1)}, u32[]{:S(2)}, u32[]{:S(2)}) collective-permute-start(f32[64,1024]{1,0:T(8,128)S(1)} %pad_maximum_fusion.2), channel_id=1, source_target_pairs={{0,2},{1,3},{2,0},{3,1},{4,6},{5,7},{6,4},{7,5},{8,10},{9,11},{10,... | collective-permute-start | bytes 786440 | tf_op jit(solution)/shard_map/ppermute | solution.py:165
  157.9 2.0 collective-permute-start.10
